TPU v7x, 32 devices: a whole 2x2x4 slice. The times are simulated.
32 devices in a mesh: groups: 2 (over y), tile: 4 (over z), chan: 2 (over x), low: 2 (over core).
Axes of the slice: x: 2, y: 2, z: 4, core: 2. Of those that a mesh axis runs over, the one named last changes fastest.
Arguments:
- latent_map: bfloat16 [16, 16, 16, 512], P('groups', 'tile', 'chan'), parts along dimension 0, may hold values from -6 to 6
- inner_map: bfloat16 [16, 16, 16, 512], P(('groups', 'tile'), None, 'chan'), parts along dimension 0, may hold values from -6 to 6
- timestep: int32 [16], P('groups'), parts along dimension 0, may hold values from 0 to 999
- conv_weight: bfloat16 [3, 3, 512, 512], P(None, None, None, 'low'), may hold values from -0.09375 to 0.09375
- time_weight: bfloat16 [256, 512], P(None, 'low'), may hold values from -0.375 to 0.375
- attend_weight: bfloat16 [3, 512, 512], P(None, None, 'low'), may hold values from -8 to 8
Outputs:
- attended: bfloat16 [16, 16, 16, 512], P(('groups', 'tile'), None, 'chan', 'low'), parts along dimension 0
There are 2 independent parts, one for each index of `groups`. A program takes and returns all parts, laid end to end along the dimension named above; an argument that names none is the same for every part. Nothing has to cross between parts.
All inputs are finite; a program needn't handle non-finite values.
Results may differ from a plain program's by a relative error of at most 0.017.
The roundings to bfloat16 on the way count: a program that leaves them out, or rounds other values in their place, can miss the bound.
Values may be sent and summed in bfloat16 or wider, within the bound.
No kernel may reach another device: no remote copies, remote signals or barrier semaphores. Data moves between devices by JAX's collectives and lax.ppermute only.
A program may use at most 64 MiB of HBM per device.

v0:
```python
import math

import jax
import jax.numpy as jnp
from jax import lax
from jax.sharding import PartitionSpec as P

HEAD = 64
TE = 256


def extended(cells, sides, width):
    for axis, dim in sides:
        count = lax.axis_size(axis)
        ends = count - 1
        head = lax.slice_in_dim(cells, 0, width, axis=dim)
        tail = lax.slice_in_dim(cells, cells.shape[dim] - width, cells.shape[dim], axis=dim)
        cells = jnp.concatenate(
            [
                lax.ppermute(tail, axis, [(i, (i + 1) % count) for i in range(ends)]),
                cells,
                lax.ppermute(head, axis, [((i + 1) % count, i) for i in range(ends)]),
            ],
            axis=dim,
        )
    return cells


def time_embedding(timestep):
    halfway = TE // 2
    ladder = jnp.arange(halfway, dtype=jnp.float32)
    frequency = jnp.exp(ladder * (-math.log(10000.0) / halfway))
    angles = timestep.astype(jnp.float32)[:, None] * frequency[None, :]
    return jnp.concatenate([jnp.sin(angles), jnp.cos(angles)], axis=1)


def convolve(padded, conv_weight, row_count, col_count):
    samples = padded.shape[0]
    positions = samples * row_count * col_count
    summed = jnp.zeros((positions, conv_weight.shape[3]), jnp.float32)
    for row_shift in range(3):
        for col_shift in range(3):
            window = padded[
                :, row_shift : row_shift + row_count, col_shift : col_shift + col_count, :
            ]
            summed = summed + jnp.dot(
                window.reshape(positions, padded.shape[3]),
                conv_weight[row_shift, col_shift],
                preferred_element_type=jnp.float32,
            )
    return summed.reshape(samples, row_count, col_count, conv_weight.shape[3])


def empty_state(heads_local, token_count):
    return (
        jnp.full((heads_local, token_count), -1e30, jnp.float32),
        jnp.zeros((heads_local, token_count), jnp.float32),
        jnp.zeros((heads_local, token_count, HEAD), jnp.float32),
    )


def attend_block(state_in, queries, key_block, value_block):
    heads_local = queries.shape[0]
    key_split = key_block.reshape(key_block.shape[0], heads_local, HEAD)
    value_split = value_block.reshape(value_block.shape[0], heads_local, HEAD)
    scores = jnp.einsum(
        "hqd,khd->hqk", queries, key_split, preferred_element_type=jnp.float32
    ) * HEAD ** (-0.5)
    running, totals, accumulated = state_in
    newest = jnp.maximum(running, jnp.max(scores, axis=2))
    shrink = jnp.exp(running - newest)
    weights = jnp.exp(scores - newest[:, :, None])
    totals = totals * shrink + jnp.sum(weights, axis=2)
    update = jnp.einsum(
        "hqk,khd->hqd",
        weights.astype(jnp.bfloat16),
        value_split,
        preferred_element_type=jnp.float32,
    )
    accumulated = accumulated * shrink[:, :, None] + update
    return (newest, totals, accumulated)


def sweep_keys(state_in, queries, key_rows, value_rows, block_rows):
    blocks = key_rows.shape[0] // block_rows
    key_blocks = key_rows.reshape(blocks, block_rows, key_rows.shape[1])
    value_blocks = value_rows.reshape(blocks, block_rows, value_rows.shape[1])

    def advance(state_step, block_pair):
        return (attend_block(state_step, queries, block_pair[0], block_pair[1]), None)

    final_state, unused = lax.scan(advance, state_in, (key_blocks, value_blocks))
    return final_state


def project_pair(features_own, attend_weight, token_count):
    half_width = features_own.shape[1]
    all_weight = jnp.concatenate([attend_weight[0], attend_weight[1], attend_weight[2]], axis=1)
    starting = jnp.zeros((token_count, 3 * half_width), jnp.float32)
    portion = lax.all_gather(features_own, "low", axis=0, tiled=True)
    blocks = portion.shape[0] // token_count

    def one_block(summed, block_pair):
        block_data, block_number = block_pair
        rows_weight = lax.dynamic_slice_in_dim(all_weight, block_number * half_width, half_width, 0)
        return (summed + jnp.dot(block_data, rows_weight, preferred_element_type=jnp.float32), None)

    numbers = jnp.arange(blocks, dtype=jnp.int32)
    result, unused = lax.scan(
        one_block, starting, (portion.reshape(blocks, token_count, half_width), numbers)
    )
    return result


def attend_sample(sample_map, attend_weight):
    row_total = sample_map.shape[0]
    col_local = sample_map.shape[1]
    half_width = sample_map.shape[2]
    token_count = row_total * col_local
    heads_local = half_width // HEAD
    features_own = sample_map.reshape(token_count, half_width)
    projected = project_pair(features_own, attend_weight, token_count).astype(jnp.bfloat16)
    head_queries = (
        projected[:, :half_width].reshape(token_count, heads_local, HEAD).transpose(1, 0, 2)
    )
    kv_pair = projected[:, half_width:]
    portion = lax.all_gather(kv_pair, "chan", axis=0, tiled=True)
    final_state = sweep_keys(
        empty_state(heads_local, token_count),
        head_queries,
        portion[:, :half_width],
        portion[:, half_width:],
        token_count,
    )
    running, totals, accumulated = final_state
    attended = (
        (accumulated / totals[:, :, None])
        .transpose(1, 0, 2)
        .reshape(1, row_total, col_local, half_width)
    )
    return attended.astype(jnp.bfloat16)


def per_device(latent_map, inner_map, timestep, conv_weight, time_weight, attend_weight):
    modulation = jnp.dot(
        time_embedding(timestep), time_weight.astype(jnp.float32), precision=lax.Precision.HIGHEST
    )
    arrived = lax.all_to_all(inner_map, "tile", split_axis=1, concat_axis=0, tiled=True)
    joined = (latent_map.astype(jnp.float32) + arrived.astype(jnp.float32)).astype(jnp.bfloat16)
    padded = extended(joined, (("tile", 1), ("chan", 2)), 1)
    convolved = convolve(padded, conv_weight, joined.shape[1], joined.shape[2])
    features = jax.nn.silu(convolved * (1.0 + modulation[:, None, None, :])).astype(jnp.bfloat16)
    by_sample = lax.all_to_all(features, "tile", split_axis=0, concat_axis=1, tiled=True)
    outputs = [
        attend_sample(by_sample[which], attend_weight) for which in range(by_sample.shape[0])
    ]
    return jnp.concatenate(outputs, axis=0)


def solution(mesh):
    in_specs = (
        P("groups", "tile", "chan", None),
        P(("groups", "tile"), None, "chan", None),
        P("groups"),
        P(None, None, None, "low"),
        P(None, "low"),
        P(None, None, "low"),
    )
    out_specs = P(("groups", "tile"), None, "chan", "low")
    return jax.shard_map(
        per_device, mesh=mesh, in_specs=in_specs, out_specs=out_specs, check_vma=False
    )
```

profile of v0, /device:TPU:0, one launch (start us, length us, event | category | flops | bytes accessed | tf_op | source)
XLA Modules:
  0.0 75.0 jit_solution(11728907591840259298)
XLA Ops:
  0.0 1.7 %copy.38 = bf16[2,16,8,512]{3,2,0,1:T(8,128)(2,1)} copy(bf16[2,16,8,512]{3,2,1,0:T(8,128)(2,1)} %param.15) | data formatting | bytes 524288 | tf_op args[1]
  1.7 6.3 %all-to-all-start = ((bf16[2,16,8,512]{3,2,0,1:T(8,128)(2,1)}), bf16[2,16,8,512]{3,2,0,1:T(8,128)(2,1)S(1)}, u32[]{:S(2)}, u32[]{:S(2)}) async-start(bf16[2,16,8,512]{3,2,0,1:T(8,128)(2,1)} %copy.38), calls=%async_computation | async-start | bytes 524288 | tf_op jit(solution)/shard_map/all_to_all | solution.py:148
  8.1 0.7 convert_element_type.77
  8.8 8.1 %all-to-all-done = bf16[2,16,8,512]{3,2,0,1:T(8,128)(2,1)S(1)} async-done(((bf16[2,16,8,512]{3,2,0,1:T(8,128)(2,1)}), bf16[2,16,8,512]{3,2,0,1:T(8,128)(2,1)S(1)}, u32[]{:S(2)}, u32[]{:S(2)}) %all-to-all-start) | async-done | bytes 262176 | tf_op jit(solution)/shard_map/all_to_all | solution.py:148
  17.2 2.2 %collective-permute-start = (bf16[8,1,8,512]{3,2,1,0:T(8,128)(2,1)S(1)}, bf16[8,1,8,512]{3,2,1,0:T(8,128)(2,1)S(1)}, u32[]{:S(2)}, u32[]{:S(2)}) collective-permute-start(bf16[8,1,8,512]{3,2,1,0:T(8,128)(2,1)S(1)} %get-tuple-element.346), channel_id=1, source_target_pairs={{0,4},{4,8},{8,12},{1,5},{5,9},{9,13},{2,6},{6,10},{10,14},{3,7},{... | collective-permute-start | bytes 196616 | tf_op jit(solution)/shard_map/ppermute | solution.py:20
  19.4 1.3 %collective-permute-start.1 = (bf16[8,1,8,512]{3,2,1,0:T(8,128)(2,1)S(1)}, bf16[8,1,8,512]{3,2,1,0:T(8,128)(2,1)S(1)}, u32[]{:S(2)}, u32[]{:S(2)}) collective-permute-start(bf16[8,1,8,512]{3,2,1,0:T(8,128)(2,1)S(1)} %get-tuple-element.347), channel_id=1, source_target_pairs={{4,0},{8,4},{12,8},{5,1},{9,5},{13,9},{6,2},{10,6},{14,10},{7,3},{... | collective-permute-start | bytes 196616 | tf_op jit(solution)/shard_map/ppermute | solution.py:22
  20.8 0.4 collective-permute-done
  21.3 4.3 %collective-permute-done.1 = bf16[8,1,8,512]{3,2,1,0:T(8,128)(2,1)S(1)} collective-permute-done((bf16[8,1,8,512]{3,2,1,0:T(8,128)(2,1)S(1)}, bf16[8,1,8,512]{3,2,1,0:T(8,128)(2,1)S(1)}, u32[]{:S(2)}, u32[]{:S(2)}) %collective-permute-start.1) | collective-permute-done | bytes 65568 | tf_op jit(solution)/shard_map/ppermute | solution.py:22
  25.7 3.4 %collective-permute-start.2 = (bf16[8,6,1,512]{3,2,1,0:T(2,128)(2,1)S(1)}, bf16[8,6,1,512]{3,2,1,0:T(2,128)(2,1)S(1)}, u32[]{:S(2)}, u32[]{:S(2)}) collective-permute-start(bf16[8,6,1,512]{3,2,1,0:T(2,128)(2,1)S(1)} %get-tuple-element.338), channel_id=1, source_target_pairs={{0,2},{1,3},{4,6},{5,7},{8,10},{9,11},{12,14},{13,15},{16,18},{17,... | collective-permute-start | bytes 147464 | tf_op jit(solution)/shard_map/ppermute | solution.py:20
  29.1 1.3 %collective-permute-start.3 = (bf16[8,6,1,512]{3,2,1,0:T(2,128)(2,1)S(1)}, bf16[8,6,1,512]{3,2,1,0:T(2,128)(2,1)S(1)}, u32[]{:S(2)}, u32[]{:S(2)}) collective-permute-start(bf16[8,6,1,512]{3,2,1,0:T(2,128)(2,1)S(1)} %get-tuple-element.339), channel_id=1, source_target_pairs={{2,0},{3,1},{6,4},{7,5},{10,8},{11,9},{14,12},{15,13},{18,16},{19,... | collective-permute-start | bytes 147464 | tf_op jit(solution)/shard_map/ppermute | solution.py:22
  30.7 0.6 collective-permute-done.2
  31.3 4.3 %collective-permute-done.3 = bf16[8,6,1,512]{3,2,1,0:T(2,128)(2,1)S(1)} collective-permute-done((bf16[8,6,1,512]{3,2,1,0:T(2,128)(2,1)S(1)}, bf16[8,6,1,512]{3,2,1,0:T(2,128)(2,1)S(1)}, u32[]{:S(2)}, u32[]{:S(2)}) %collective-permute-start.3) | collective-permute-done | bytes 49184 | tf_op jit(solution)/shard_map/ppermute | solution.py:22
  35.6 0.5 maximum_maximum_fusion
  38.2 0.7 multiply_convert_fusion
  38.9 3.3 %all-to-all-start.1 = ((bf16[8,4,8,256]{3,2,1,0:T(8,128)(2,1)}), bf16[8,4,8,256]{3,2,1,0:T(8,128)(2,1)S(1)}, u32[]{:S(2)}, u32[]{:S(2)}) async-start(bf16[8,4,8,256]{3,2,1,0:T(8,128)(2,1)} %multiply_convert_fusion), calls=%async_computation.1 | async-start | bytes 262144 | tf_op jit(solution)/shard_map/all_to_all | solution.py:153
  42.5 5.7 %all-to-all-done.1 = bf16[8,4,8,256]{3,2,1,0:T(8,128)(2,1)S(1)} async-done(((bf16[8,4,8,256]{3,2,1,0:T(8,128)(2,1)}), bf16[8,4,8,256]{3,2,1,0:T(8,128)(2,1)S(1)}, u32[]{:S(2)}, u32[]{:S(2)}) %all-to-all-start.1) | async-done | bytes 131104 | tf_op jit(solution)/shard_map/all_to_all | solution.py:153
  48.2 1.9 %all_gather.12 = bf16[256,256]{1,0:T(8,128)(2,1)S(1)} all-gather(bf16[128,256]{1,0:T(8,128)(2,1)S(1)} %bitcast.157), channel_id=1, replica_groups=mesh['groups'=2,'tile'=4,'chan'=2,'low'=2] {'low'}, dimensions={0}, use_global_device_ids=true | all-gather | bytes 196608 | tf_op jit(solution)/shard_map/all_gather | solution.py:100
  50.1 3.0 %while.52 = (s32[]{:T(128)}, f32[128,768]{1,0:T(8,128)S(1)}, bf16[2,128,256]{2,1,0:T(8,128)(2,1)S(1)}, s32[2]{0:T(128)S(1)}, bf16[512,768]{1,0:T(8,128)(2,1)S(1)...) while((s32[]{:T(128)}, f32[128,768]{1,0:T(8,128)S(1)}, bf16[2,128,256]{2,1,0:T(8,128)(2,1)S(1)}, ...), condition=%wide.region_1.2_spmd.clone, body=%wide.region_0.1_spmd.clone.sunk | while | flops 50528264 | bytes 1245353 | solution.py:109
  50.1 0.6 dynamic_slice.68
  51.3 0.3 convolution_add_fusion.16
  51.6 0.6 dynamic_slice.68
  52.8 0.3 convolution_add_fusion.16
  53.2 1.9 %all_gather.14 = bf16[256,256]{1,0:T(8,128)(2,1)S(1)} all-gather(bf16[128,256]{1,0:T(8,128)(2,1)S(1)} %bitcast.156), channel_id=1, replica_groups=mesh['groups'=2,'tile'=4,'chan'=2,'low'=2] {'low'}, dimensions={0}, use_global_device_ids=true | all-gather | bytes 196608 | tf_op jit(solution)/shard_map/all_gather | solution.py:100
  55.1 3.0 %while.54 = (s32[]{:T(128)}, f32[128,768]{1,0:T(8,128)S(1)}, bf16[2,128,256]{2,1,0:T(8,128)(2,1)S(1)}, s32[2]{0:T(128)S(1)}, bf16[512,768]{1,0:T(8,128)(2,1)S(1)...) while((s32[]{:T(128)}, f32[128,768]{1,0:T(8,128)S(1)}, bf16[2,128,256]{2,1,0:T(8,128)(2,1)S(1)}, ...), condition=%wide.region_7.8_spmd.clone, body=%wide.region_6.7_spmd.clone.sunk | while | flops 50528264 | bytes 1245353 | solution.py:109
  55.1 0.6 dynamic_slice.72
  56.6 0.6 dynamic_slice.72
  57.9 0.3 convolution_add_fusion.18
  58.2 6.2 %all_gather.13 = bf16[256,512]{1,0:T(8,128)(2,1)S(1)} all-gather(bf16[128,512]{1,0:T(8,128)(2,1)S(1)} %slice.158), channel_id=1, replica_groups=mesh['groups'=2,'tile'=4,'chan'=2,'low'=2] {'chan'}, dimensions={0}, use_global_device_ids=true | all-gather | bytes 393216 | tf_op jit(solution)/shard_map/all_gather | solution.py:127
  64.6 1.7 %while.53 = (s32[]{:T(128)}, f32[4,128]{1,0:T(4,128)S(1)}, f32[4,128]{1,0:T(4,128)S(1)}, f32[4,128,64]{1,2,0:T(8,128)S(1)}, bf16[2,128,256]{2,1,0:T(8,128)(2,1)S...) while((s32[]{:T(128)}, f32[4,128]{1,0:T(4,128)S(1)}, ...), condition=%wide.region_5.6_spmd.clone, body=%wide.region_2.5_spmd.clone.sunk | while | flops 17271300 | bytes 1802349 | solution.py:92
  66.6 5.6 %all_gather.15 = bf16[256,512]{1,0:T(8,128)(2,1)S(1)} all-gather(bf16[128,512]{1,0:T(8,128)(2,1)S(1)} %slice.163), channel_id=1, replica_groups=mesh['groups'=2,'tile'=4,'chan'=2,'low'=2] {'chan'}, dimensions={0}, use_global_device_ids=true | all-gather | bytes 393216 | tf_op jit(solution)/shard_map/all_gather | solution.py:127
  72.4 1.7 %while.55 = (s32[]{:T(128)}, f32[4,128]{1,0:T(4,128)S(1)}, f32[4,128]{1,0:T(4,128)S(1)}, f32[4,128,64]{1,2,0:T(8,128)S(1)}, bf16[2,128,256]{2,1,0:T(8,128)(2,1)S...) while((s32[]{:T(128)}, f32[4,128]{1,0:T(4,128)S(1)}, ...), condition=%wide.region_11.12_spmd.clone, body=%wide.region_8.11_spmd.clone.sunk | while | flops 17271300 | bytes 1802349 | solution.py:92
  74.4 0.7 pad_maximum_fusion.4
  (93 shorter events, 7.3 us)
Async XLA Ops:
  0.0 20.7 %copy-start = (bf16[256,256]{1,0:T(8,128)(2,1)S(1)}, bf16[256,256]{1,0:T(8,128)(2,1)}, u32[]{:S(2)}) copy-start(bf16[256,256]{1,0:T(8,128)(2,1)} %param.18) | copy-start | bytes 393220
  0.0 17.1 %copy-start.3 = (bf16[8,4,8,512]{3,2,1,0:T(8,128)(2,1)S(1)}, bf16[8,4,8,512]{3,2,1,0:T(8,128)(2,1)}, u32[]{:S(2)}) copy-start(bf16[8,4,8,512]{3,2,1,0:T(8,128)(2,1)} %param.14) | copy-start | bytes 786436
  1.7 15.2 %all-to-all-start = ((bf16[2,16,8,512]{3,2,0,1:T(8,128)(2,1)}), bf16[2,16,8,512]{3,2,0,1:T(8,128)(2,1)S(1)}, u32[]{:S(2)}, u32[]{:S(2)}) async-start(bf16[2,16,8,512]{3,2,0,1:T(8,128)(2,1)} %copy.38), calls=%async_computation | async-start | bytes 524288 | tf_op jit(solution)/shard_map/all_to_all | solution.py:148
  17.0 13.5 %copy-start.1 = (bf16[3,3,512,256]{3,2,1,0:T(8,128)(2,1)S(1)}, bf16[3,3,512,256]{3,2,1,0:T(8,128)(2,1)}, u32[]{:S(2)}) copy-start(bf16[3,3,512,256]{3,2,1,0:T(8,128)(2,1)} %param.17) | copy-start | bytes 7077892
  17.2 4.1 %collective-permute-start = (bf16[8,1,8,512]{3,2,1,0:T(8,128)(2,1)S(1)}, bf16[8,1,8,512]{3,2,1,0:T(8,128)(2,1)S(1)}, u32[]{:S(2)}, u32[]{:S(2)}) collective-permute-start(bf16[8,1,8,512]{3,2,1,0:T(8,128)(2,1)S(1)} %get-tuple-element.346), channel_id=1, source_target_pairs={{0,4},{4,8},{8,12},{1,5},{5,9},{9,13},{2,6},{6,10},{10,14},{3,7},{... | collective-permute-start | bytes 196616 | tf_op jit(solution)/shard_map/ppermute | solution.py:20
  19.4 6.2 %collective-permute-start.1 = (bf16[8,1,8,512]{3,2,1,0:T(8,128)(2,1)S(1)}, bf16[8,1,8,512]{3,2,1,0:T(8,128)(2,1)S(1)}, u32[]{:S(2)}, u32[]{:S(2)}) collective-permute-start(bf16[8,1,8,512]{3,2,1,0:T(8,128)(2,1)S(1)} %get-tuple-element.347), channel_id=1, source_target_pairs={{4,0},{8,4},{12,8},{5,1},{9,5},{13,9},{6,2},{10,6},{14,10},{7,3},{... | collective-permute-start | bytes 196616 | tf_op jit(solution)/shard_map/ppermute | solution.py:22
  25.7 5.6 %collective-permute-start.2 = (bf16[8,6,1,512]{3,2,1,0:T(2,128)(2,1)S(1)}, bf16[8,6,1,512]{3,2,1,0:T(2,128)(2,1)S(1)}, u32[]{:S(2)}, u32[]{:S(2)}) collective-permute-start(bf16[8,6,1,512]{3,2,1,0:T(2,128)(2,1)S(1)} %get-tuple-element.338), channel_id=1, source_target_pairs={{0,2},{1,3},{4,6},{5,7},{8,10},{9,11},{12,14},{13,15},{16,18},{17,... | collective-permute-start | bytes 147464 | tf_op jit(solution)/shard_map/ppermute | solution.py:20
  29.1 6.5 %collective-permute-start.3 = (bf16[8,6,1,512]{3,2,1,0:T(2,128)(2,1)S(1)}, bf16[8,6,1,512]{3,2,1,0:T(2,128)(2,1)S(1)}, u32[]{:S(2)}, u32[]{:S(2)}) collective-permute-start(bf16[8,6,1,512]{3,2,1,0:T(2,128)(2,1)S(1)} %get-tuple-element.339), channel_id=1, source_target_pairs={{2,0},{3,1},{6,4},{7,5},{10,8},{11,9},{14,12},{15,13},{18,16},{19,... | collective-permute-start | bytes 147464 | tf_op jit(solution)/shard_map/ppermute | solution.py:22
  37.2 5.0 %copy-start.2 = (bf16[3,512,256]{2,1,0:T(8,128)(2,1)S(1)}, bf16[3,512,256]{2,1,0:T(8,128)(2,1)}, u32[]{:S(2)}) copy-start(bf16[3,512,256]{2,1,0:T(8,128)(2,1)} %param.19) | copy-start | bytes 2359300
  38.9 9.2 %all-to-all-start.1 = ((bf16[8,4,8,256]{3,2,1,0:T(8,128)(2,1)}), bf16[8,4,8,256]{3,2,1,0:T(8,128)(2,1)S(1)}, u32[]{:S(2)}, u32[]{:S(2)}) async-start(bf16[8,4,8,256]{3,2,1,0:T(8,128)(2,1)} %multiply_convert_fusion), calls=%async_computation.1 | async-start | bytes 262144 | tf_op jit(solution)/shard_map/all_to_all | solution.py:153
where the time goes:
time: 75.5 us; the launch traced here: 75 us
  waiting for transfers between devices  23.4 us (31%)
  starting transfers between devices  17.8 us (24%)
  blocking collectives  15.7 us (21%)
  local copies, waits for them, and re-layouts  6.24 us (8%)
  matrix products  4.99 us (7%)
  other arithmetic  3.44 us (5%)
  loops' own time  2.99 us (4%)
    all_gather x2, blocking collectives, attend_sample(): portion = lax.all_gather(kv_pair, 'chan', axis=0, tiled=True)  11.9 us
    ppermute x2, waiting for transfers between devices, extended(): lax.ppermute(head, axis, [((i + 1) % count, i) for i in range(ends)])  8.59 us
    all_to_all x1, waiting for transfers between devices, per_device(): lax.all_to_all(inner_map, 'tile', split_axis=1, concat_axis=0, tiled=True)  8.13 us
    all_to_all x1, starting transfers between devices, per_device(): lax.all_to_all(inner_map, 'tile', split_axis=1, concat_axis=0, tiled=True)  6.32 us
    all_to_all x1, waiting for transfers between devices, per_device(): lax.all_to_all(features, 'tile', split_axis=0, concat_axis=1, tiled=True)  5.68 us
    ppermute x2, starting transfers between devices, extended(): lax.ppermute(tail, axis, [(i, (i + 1) % count) for i in range(ends)])  5.6 us
    all_gather x2, blocking collectives, project_pair(): portion = lax.all_gather(features_own, 'low', axis=0, tiled=True)  3.8 us
    all_to_all x1, starting transfers between devices, per_device(): lax.all_to_all(features, 'tile', split_axis=0, concat_axis=1, tiled=True)  3.33 us
  transfers between devices with their start and end apart: 6, of which 6 were waited for; matrix products, arithmetic and copies ran while one was open for 2% of the time, Pallas kernels for 0%

commit v1 on v0

v1 whole, which is shorter than its diff:
```python
import math

import jax
import jax.numpy as jnp
from jax import lax
from jax.sharding import PartitionSpec as P

HEAD = 64
TE = 256


def time_embedding(timestep):
    halfway = TE // 2
    ladder = jnp.arange(halfway, dtype=jnp.float32)
    frequency = jnp.exp(ladder * (-math.log(10000.0) / halfway))
    angles = timestep.astype(jnp.float32)[:, None] * frequency[None, :]
    return jnp.concatenate([jnp.sin(angles), jnp.cos(angles)], axis=1)


def swap(tree, axis):
    return lax.ppermute(tree, axis, [(0, 1), (1, 0)])


def convolve(joined, weight):
    return lax.conv_general_dilated(
        joined,
        weight,
        window_strides=(1, 1),
        padding=((1, 1), (1, 1)),
        dimension_numbers=("NHWC", "HWIO", "NHWC"),
        preferred_element_type=jnp.float32,
    )


def attend(queries, keys, values):
    scores = jnp.einsum("nqd,nkd->nqk", queries, keys, preferred_element_type=jnp.float32)
    scores = scores * HEAD ** (-0.5)
    row_peak = jnp.max(scores, axis=2, keepdims=True)
    weights = jnp.exp(scores - row_peak)
    totals = jnp.sum(weights, axis=2, keepdims=True)
    summed = jnp.einsum(
        "nqk,nkd->nqd", weights.astype(jnp.bfloat16), values, preferred_element_type=jnp.float32
    )
    return (summed / totals).astype(jnp.bfloat16)


def per_device(latent_map, inner_map, timestep, conv_weight, time_weight, attend_weight):
    tiles = lax.axis_size("tile")
    lows = lax.axis_size("low")
    t_idx = lax.axis_index("tile")
    c_idx = lax.axis_index("chan")
    l_idx = lax.axis_index("low")
    samples, row_local, col_local, width = latent_map.shape
    per_tile = samples // tiles
    per_core = per_tile // lows
    half = conv_weight.shape[3]
    heads_local = attend_weight.shape[2] // HEAD

    conv_other, time_other = swap((conv_weight, time_weight), "low")

    start = l_idx * per_core
    outgoing = lax.dynamic_slice_in_dim(
        latent_map.reshape(tiles, per_tile, row_local, col_local, width), start, per_core, 1
    ).reshape(tiles * per_core, row_local, col_local, width)
    arrived = lax.all_to_all(outgoing, "tile", split_axis=0, concat_axis=1, tiled=True)
    inner_own = lax.dynamic_slice_in_dim(inner_map, start, per_core, 0)
    joined = (arrived.astype(jnp.float32) + inner_own.astype(jnp.float32)).astype(jnp.bfloat16)
    whole = lax.all_gather(joined, "chan", axis=2, tiled=True)

    stamps = lax.dynamic_slice_in_dim(timestep, t_idx * per_tile + start, per_core, 0)
    embedded = time_embedding(stamps)
    mod_own = jnp.dot(embedded, time_weight.astype(jnp.float32), precision=lax.Precision.HIGHEST)
    mod_other = jnp.dot(embedded, time_other.astype(jnp.float32), precision=lax.Precision.HIGHEST)

    def features_of(weight, modulation):
        convolved = convolve(whole, weight)
        return jax.nn.silu(convolved * (1.0 + modulation[:, None, None, :])).astype(jnp.bfloat16)

    feat_own = features_of(conv_weight, mod_own)
    feat_other = features_of(conv_other, mod_other)
    part_own, part_other = swap((feat_own, feat_other), "low")
    first = l_idx == 0
    half_a = jnp.where(first, jnp.concatenate([feat_own, part_other], 0), jnp.concatenate([part_other, feat_own], 0))
    half_b = jnp.where(first, jnp.concatenate([feat_other, part_own], 0), jnp.concatenate([part_own, feat_other], 0))

    rows_total, cols_total = half_a.shape[1], half_a.shape[2]
    tokens = rows_total * cols_total
    weight_a = lax.dynamic_slice_in_dim(attend_weight, l_idx * half, half, 1)
    weight_b = lax.dynamic_slice_in_dim(attend_weight, (1 - l_idx) * half, half, 1)

    def project(part_a, part_b, which):
        return (
            jnp.dot(part_a, weight_a[which], preferred_element_type=jnp.float32)
            + jnp.dot(part_b, weight_b[which], preferred_element_type=jnp.float32)
        ).astype(jnp.bfloat16)

    col_start = c_idx * col_local
    own_a = lax.dynamic_slice_in_dim(half_a, col_start, col_local, 2)
    own_b = lax.dynamic_slice_in_dim(half_b, col_start, col_local, 2)
    queries = project(own_a.reshape(per_tile, -1, half), own_b.reshape(per_tile, -1, half), 0)
    keys = project(half_a.reshape(per_tile, tokens, half), half_b.reshape(per_tile, tokens, half), 1)
    values = project(half_a.reshape(per_tile, tokens, half), half_b.reshape(per_tile, tokens, half), 2)

    def by_head(x):
        n, k, _ = x.shape
        return x.reshape(n, k, heads_local, HEAD).transpose(0, 2, 1, 3).reshape(n * heads_local, k, HEAD)

    q_heads, k_heads, v_heads = by_head(queries), by_head(keys), by_head(values)
    if tokens * tokens * 4 * q_heads.shape[0] <= (8 << 20):
        out = attend(q_heads, k_heads, v_heads)
    else:
        out = lax.map(lambda trio: attend(*(x[None] for x in trio))[0], (q_heads, k_heads, v_heads))
    out = out.reshape(per_tile, heads_local, row_local * tiles, col_local, HEAD)
    return out.transpose(0, 2, 3, 1, 4).reshape(per_tile, row_local * tiles, col_local, heads_local * HEAD)


def solution(mesh):
    in_specs = (
        P("groups", "tile", "chan", None),
        P(("groups", "tile"), None, "chan", None),
        P("groups"),
        P(None, None, None, "low"),
        P(None, "low"),
        P(None, None, "low"),
    )
    out_specs = P(("groups", "tile"), None, "chan", "low")
    return jax.shard_map(
        per_device, mesh=mesh, in_specs=in_specs, out_specs=out_specs, check_vma=False
    )
```

time: 75.5 us -> 32 us (0.42)
  waiting for transfers between devices: 23.4 us -> 3.81 us
  starting transfers between devices: 17.8 us -> 7.46 us
  blocking collectives: 15.7 us -> 5.78 us
  loops' own time: 2.99 us -> 0 us
  other arithmetic: 3.44 us -> 0.63 us
  matrix products: 4.99 us -> 7.33 us
    all_to_all x2 -> x1, waiting for transfers between devices: 13.8 us -> 2.96 us  [per_device(): lax.all_to_all(outgoing, 'tile', split_axis=0, concat_axis=1, tiled=True)]
    all_gather x4 -> x1, blocking collectives: 15.7 us -> 5.78 us  [per_device(): whole = lax.all_gather(joined, 'chan', axis=2, tiled=True)]
    ppermute x4, waiting for transfers between devices: 9.63 us -> 0.85 us  [swap(): return lax.ppermute(tree, axis, [(0, 1), (1, 0)])]
    ppermute x4, starting transfers between devices: 8.18 us -> 1.16 us  [swap(): return lax.ppermute(tree, axis, [(0, 1), (1, 0)])]
    conv_general_dilated x0 -> x2, matrix products: none -> 3.88 us  [convolve(): lax.conv_general_dilated(joined, weight, window_strides=(1, 1), padding=(...]
    all_to_all x2 -> x1, starting transfers between devices: 9.64 us -> 6.3 us  [per_device(): lax.all_to_all(outgoing, 'tile', split_axis=0, concat_axis=1, tiled=True)]
    another operation x4 -> x0, loops' own time: 2.99 us -> none  [the longest x2 2.71 us: project_pair(): lax.scan(one_block, starting, (portion.reshape(blocks, token_count, half_...]
    convert_element_type x8 -> x1, other arithmetic: 1.61 us -> 0.04 us  [per_device(): (arrived.astype(jnp.float32) + inner_own.astype(jnp.float32)).astype(jnp....]
  transfers between devices with their start and end apart: 6 -> 5, of which waited for: 6 -> 2; matrix products, arithmetic and copies ran while one was open for 2% -> 27% of each run, Pallas kernels for 0% -> 0%
where the time goes in v1:
time: 32 us; the launch traced here: 31.7 us
  starting transfers between devices  7.46 us (23%)
  matrix products  7.33 us (23%)
  blocking collectives  5.78 us (18%)
  local copies, waits for them, and re-layouts  5.76 us (18%)
  waiting for transfers between devices  3.81 us (12%)
  between operations  0.94 us (3%)
  other arithmetic  0.63 us (2%)
    all_to_all x1, starting transfers between devices, per_device(): lax.all_to_all(outgoing, 'tile', split_axis=0, concat_axis=1, tiled=True)  6.3 us
    all_gather x1, blocking collectives, per_device(): whole = lax.all_gather(joined, 'chan', axis=2, tiled=True)  5.78 us
    conv_general_dilated x2, matrix products, convolve(): lax.conv_general_dilated(joined, weight, window_strides=(1, 1), padding=(...  3.88 us
    all_to_all x1, waiting for transfers between devices, per_device(): lax.all_to_all(outgoing, 'tile', split_axis=0, concat_axis=1, tiled=True)  2.96 us
    dynamic_slice x1, local copies, waits for them, and re-layouts, per_device(): lax.dynamic_slice_in_dim(timestep, t_idx * per_tile + start, per_core, 0)  1.27 us
    ppermute x4, starting transfers between devices, swap(): return lax.ppermute(tree, axis, [(0, 1), (1, 0)])  1.16 us
    dot_general x1, matrix products, per_device(): jnp.dot(embedded, time_weight.astype(jnp.float32), precision=lax.Precisio...  1.04 us
    dynamic_slice x1, local copies, waits for them, and re-layouts, per_device(): lax.dynamic_slice_in_dim(latent_map.reshape(tiles, per_tile, row_local, c...  0.91 us
  transfers between devices with their start and end apart: 5, of which 2 were waited for; matrix products, arithmetic and copies ran while one was open for 27% of the time, Pallas kernels for 0%

profile of v1, /device:TPU:0, one launch (start us, length us, event | category | flops | bytes accessed | tf_op | source)
XLA Modules:
  0.0 31.7 jit_solution(18254122364025589512)
XLA Ops:
  0.0 0.5 %collective-permute-start = (bf16[3,3,512,256]{3,2,1,0:T(8,128)(2,1)}, bf16[3,3,512,256]{3,2,1,0:T(8,128)(2,1)}, u32[]{:S(2)}, u32[]{:S(2)}) collective-permute-start(bf16[3,3,512,256]{3,2,1,0:T(8,128)(2,1)} %param.9), channel_id=1, source_target_pairs={{0,1},{1,0},{2,3},{3,2},{4,5},{5,4},{6,7},{7,6},{8,9},{9,8},{10,11... | collective-permute-start | bytes 7077896 | tf_op jit(solution)/shard_map/ppermute | solution.py:21
  0.5 0.1 collective-permute-start.1
  0.5 0.9 %constant_dynamic-slice_fusion = bf16[4,1,4,8,512]{4,3,2,1,0:T(8,128)(2,1)S(1)} fusion(bf16[4,2,4,8,512]{4,3,2,1,0:T(8,128)(2,1)} %bitcast.95, s32[]{:T(128)S(6)} %select_n.38), kind=kLoop, calls=%fused_computation.66 | loop fusion | bytes 262148 | tf_op jit(solution)/shard_map/dynamic_slice | solution.py:62
  1.5 0.7 %copy.126 = bf16[4,1,4,8,512]{4,2,3,0,1:T(4,128)(2,1)} copy(bf16[4,1,4,8,512]{4,3,2,1,0:T(8,128)(2,1)S(1)} %constant_dynamic-slice_fusion) | data formatting | bytes 262144
  2.2 6.3 %all-to-all-start = ((bf16[4,4,8,512]{3,1,2,0:T(4,128)(2,1)}), bf16[4,4,8,512]{3,1,2,0:T(4,128)(2,1)S(1)}, u32[]{:S(2)}, u32[]{:S(2)}) async-start(bf16[4,4,8,512]{3,1,2,0:T(4,128)(2,1)} %bitcast.78), calls=%async_computation | async-start | bytes 262144 | tf_op jit(solution)/shard_map/all_to_all | solution.py:65
  8.5 1.3 %dynamic_slice.23 = s32[1]{0:T(128)} dynamic-slice(s32[8]{0:T(128)} %param.8, s32[]{:T(128)S(6)} %select_n.39), dynamic_slice_sizes={1} | dynamic-slice | bytes 12 | tf_op jit(solution)/shard_map/dynamic_slice | solution.py:70
  10.4 1.0 %fusion.50 = f32[1,256]{1,0:T(1,128)S(1)} fusion(bf16[256,256]{1,0:T(8,128)(2,1)} %param.10, f32[1,128]{1,0:T(1,128)S(1)} %get-tuple-element.23, f32[1,128]{1,0:T(1,128)S(1)} %get-tuple-element.24), kind=kOutput, calls=%fused_computation.84 | convolution fusion | flops 786688 | bytes 133120 | tf_op jit(solution)/shard_map/dot_general | solution.py:72
  11.5 0.1 fusion.49
  11.7 3.0 %all-to-all-done = bf16[4,4,8,512]{3,1,2,0:T(4,128)(2,1)S(1)} async-done(((bf16[4,4,8,512]{3,1,2,0:T(4,128)(2,1)}), bf16[4,4,8,512]{3,1,2,0:T(4,128)(2,1)S(1)}, u32[]{:S(2)}, u32[]{:S(2)}) %all-to-all-start) | async-done | bytes 131104 | tf_op jit(solution)/shard_map/all_to_all | solution.py:65
  14.8 5.8 %all_gather.3 = bf16[1,16,16,512]{3,1,0,2:T(8,128)(2,1)S(1)} all-gather(bf16[1,16,8,512]{3,1,0,2:T(8,128)(2,1)S(1)} %copy.79), channel_id=1, replica_groups=mesh['groups'=2,'tile'=4,'chan'=2,'low'=2] {'chan'}, dimensions={2}, use_global_device_ids=true | all-gather | bytes 393216 | tf_op jit(solution)/shard_map/all_gather | solution.py:68
  20.6 0.2 copy.81
  20.9 1.1 %multiply_convert_fusion.1 = bf16[16,8,3,256]{3,1,2,0:T(8,128)(2,1)S(1)} fusion(bf16[3,3,512,256]{3,2,1,0:T(8,128)(2,1)S(1)} %copy-done.2, bf16[16,1,7,2,512]{4,2,3,0,1:T(8,128)(2,1)S(1)} %slice.76, bf16[16,1,8,3,512]{4,2,3,0,1:T(8,128)(2,1)S(1)} %copy.81, f32[256]{0:T(256)S(1)} %broadcast_add_fusion.1, pred[8,3]{0,1:T(4,128)(4,1)S(1)} %copy-done.3), kind=kOutput, calls=%fused_computation.22 | convolution fusion | flops 870875136 | bytes 3179544 | tf_op jit(solution)/shard_map/conv_general_dilated | solution.py:25
  22.2 2.8 %multiply_convert_fusion = bf16[16,8,3,256]{3,1,2,0:T(8,128)(2,1)S(1)} fusion(bf16[3,3,512,256]{3,2,1,0:T(8,128)(2,1)} %collective-permute-done, bf16[16,1,7,2,512]{4,2,3,0,1:T(8,128)(2,1)S(1)} %slice.76, bf16[16,1,8,3,512]{4,2,3,0,1:T(8,128)(2,1)S(1)} %copy.81, f32[256]{0:T(256)S(1)} %broadcast_add_fusion, pred[8,3]{0,1:T(4,128)(4,1)S(1)} %copy-done.3), kind=kOutput, calls=%fused_computation.21 | convolution fusion | flops 870875136 | bytes 3179544 | tf_op jit(solution)/shard_map/conv_general_dilated | solution.py:25
  25.0 0.6 %collective-permute-start.2 = (bf16[1,16,16,256]{3,1,2,0:T(8,128)(2,1)S(1)}, bf16[1,16,16,256]{3,1,2,0:T(8,128)(2,1)S(1)}, u32[]{:S(2)}, u32[]{:S(2)}) collective-permute-start(bf16[1,16,16,256]{3,1,2,0:T(8,128)(2,1)S(1)} %get-tuple-element.14), channel_id=1, source_target_pairs={{0,1},{1,0},{2,3},{3,2},{4,5},{5,4},{6,7},{7,6},{8,9},{9,8},{10,11... | collective-permute-start | bytes 393224 | tf_op jit(solution)/shard_map/ppermute | solution.py:21
  25.8 0.8 %collective-permute-done.2 = bf16[1,16,16,256]{3,1,2,0:T(8,128)(2,1)S(1)} collective-permute-done((bf16[1,16,16,256]{3,1,2,0:T(8,128)(2,1)S(1)}, bf16[1,16,16,256]{3,1,2,0:T(8,128)(2,1)S(1)}, u32[]{:S(2)}, u32[]{:S(2)}) %collective-permute-start.2) | collective-permute-done | bytes 131104 | tf_op jit(solution)/shard_map/ppermute | solution.py:21
  26.6 0.3 fusion.25
  26.9 0.3 fusion.1
  27.3 0.3 copy.92
  27.6 0.1 reshape.109
  27.7 0.2 fusion.26
  27.9 0.2 fusion.5
  28.1 0.1 fusion.55
  28.2 0.3 fusion.24
  28.5 0.3 fusion.2
  28.8 0.3 copy.97
  29.1 0.1 reshape.110
  29.3 0.4 %fusion.56 = (f32[8,128]{1,0:T(8,128)S(1)}, f32[8,128,256]{2,1,0:T(8,128)S(1)}) fusion(bf16[8,128,64]{2,1,0:T(8,128)(2,1)S(1)} %bitcast.83, bf16[8,256,64]{1,0,2:T(8,128)(2,1)S(1)} %reshape.109), kind=kOutput, calls=%fused_computation.92 | convolution fusion | flops 34077696 | bytes 1445888 | tf_op jit(solution)/shard_map/nqd,nkd->nqk/dot_general | solution.py:36
  29.7 0.4 %fusion.7 = f32[8,128]{1,0:T(8,128)S(1)} fusion(f32[8,128,256]{2,1,0:T(8,128)S(1)} %get-tuple-element.22, f32[8,128]{1,0:T(8,128)S(1)} %get-tuple-element.21), kind=kLoop, calls=%fused_computation.16 | loop fusion | flops 523264 | bytes 1056768 | tf_op jit(solution)/shard_map/reduce_sum | solution.py:40
  30.0 0.4 %fusion.6 = bf16[8,128,64]{1,2,0:T(8,128)(2,1)S(1)} fusion(f32[8,128,256]{2,1,0:T(8,128)S(1)} %get-tuple-element.22, f32[8,128]{1,0:T(8,128)S(1)} %get-tuple-element.21, bf16[8,256,64]{1,0,2:T(8,128)(2,1)S(1)} %reshape.110, f32[8,128]{1,0:T(8,128)S(1)} %fusion.7), kind=kOutput, calls=%fused_computation.14 | convolution fusion | flops 34209792 | bytes 1449984 | tf_op jit(solution)/shard_map/nqk,nkd->nqd/dot_general | solution.py:41
  30.4 0.2 copy.99
  30.6 0.2 copy.100
  30.8 0.9 %reshape.112 = bf16[2,16,8,256]{3,2,1,0:T(8,128)(2,1)} reshape(bf16[2,16,8,4,64]{4,3,2,1,0:T(4,128)(2,1)S(1)} %copy.100) | data formatting | bytes 262144 | tf_op jit(solution)/shard_map/reshape | solution.py:114
  (35 shorter events, 0.9 us)
Async XLA Ops:
  0.0 26.6 %copy-start = (bf16[3,512,256]{2,1,0:T(8,128)(2,1)S(1)}, bf16[3,512,256]{2,1,0:T(8,128)(2,1)}, u32[]{:S(2)}) copy-start(bf16[3,512,256]{2,1,0:T(8,128)(2,1)} %param.11) | copy-start | bytes 2359300
  0.0 14.7 %copy-start.1 = (bf16[2,16,8,512]{3,2,1,0:T(8,128)(2,1)S(1)}, bf16[2,16,8,512]{3,2,1,0:T(8,128)(2,1)}, u32[]{:S(2)}) copy-start(bf16[2,16,8,512]{3,2,1,0:T(8,128)(2,1)} %param.7) | copy-start | bytes 786436
  0.0 22.2 %collective-permute-start = (bf16[3,3,512,256]{3,2,1,0:T(8,128)(2,1)}, bf16[3,3,512,256]{3,2,1,0:T(8,128)(2,1)}, u32[]{:S(2)}, u32[]{:S(2)}) collective-permute-start(bf16[3,3,512,256]{3,2,1,0:T(8,128)(2,1)} %param.9), channel_id=1, source_target_pairs={{0,1},{1,0},{2,3},{3,2},{4,5},{5,4},{6,7},{7,6},{8,9},{9,8},{10,11... | collective-permute-start | bytes 7077896 | tf_op jit(solution)/shard_map/ppermute | solution.py:21
  0.5 11.1 %collective-permute-start.1 = (bf16[256,256]{1,0:T(8,128)(2,1)}, bf16[256,256]{1,0:T(8,128)(2,1)S(1)}, u32[]{:S(2)}, u32[]{:S(2)}) collective-permute-start(bf16[256,256]{1,0:T(8,128)(2,1)} %param.10), channel_id=1, source_target_pairs={{0,1},{1,0},{2,3},{3,2},{4,5},{5,4},{6,7},{7,6},{8,9},{9,8},{10,11... | collective-permute-start | bytes 393224 | tf_op jit(solution)/shard_map/ppermute | solution.py:21
  2.2 12.4 %all-to-all-start = ((bf16[4,4,8,512]{3,1,2,0:T(4,128)(2,1)}), bf16[4,4,8,512]{3,1,2,0:T(4,128)(2,1)S(1)}, u32[]{:S(2)}, u32[]{:S(2)}) async-start(bf16[4,4,8,512]{3,1,2,0:T(4,128)(2,1)} %bitcast.78), calls=%async_computation | async-start | bytes 262144 | tf_op jit(solution)/shard_map/all_to_all | solution.py:65
  14.7 6.2 %copy-start.2 = (bf16[3,3,512,256]{3,2,1,0:T(8,128)(2,1)S(1)}, bf16[3,3,512,256]{3,2,1,0:T(8,128)(2,1)}, u32[]{:S(2)}) copy-start(bf16[3,3,512,256]{3,2,1,0:T(8,128)(2,1)} %param.9) | copy-start | bytes 7077892
  14.7 6.2 %copy-start.3 = (pred[8,3]{0,1:T(4,128)(4,1)S(1)}, pred[8,3]{0,1:T(4,128)(4,1)}, u32[]{:S(2)}) copy-start(pred[8,3]{0,1:T(4,128)(4,1)} %constant.47) | copy-start | bytes 76
  22.1 3.5 %collective-permute-start.3 = (bf16[1,16,16,256]{3,1,2,0:T(8,128)(2,1)S(1)}, bf16[1,16,16,256]{3,1,2,0:T(8,128)(2,1)S(1)}, u32[]{:S(2)}, u32[]{:S(2)}) collective-permute-start(bf16[1,16,16,256]{3,1,2,0:T(8,128)(2,1)S(1)} %get-tuple-element.16), channel_id=1, source_target_pairs={{0,1},{1,0},{2,3},{3,2},{4,5},{5,4},{6,7},{7,6},{8,9},{9,8},{10,11... | collective-permute-start | bytes 393224 | tf_op jit(solution)/shard_map/ppermute | solution.py:21
  25.0 1.6 %collective-permute-start.2 = (bf16[1,16,16,256]{3,1,2,0:T(8,128)(2,1)S(1)}, bf16[1,16,16,256]{3,1,2,0:T(8,128)(2,1)S(1)}, u32[]{:S(2)}, u32[]{:S(2)}) collective-permute-start(bf16[1,16,16,256]{3,1,2,0:T(8,128)(2,1)S(1)} %get-tuple-element.14), channel_id=1, source_target_pairs={{0,1},{1,0},{2,3},{3,2},{4,5},{5,4},{6,7},{7,6},{8,9},{9,8},{10,11... | collective-permute-start | bytes 393224 | tf_op jit(solution)/shard_map/ppermute | solution.py:21

commit v2 on v1

--- a/solution.py
+++ b/solution.py
@@ -19,6 +19,38 @@
 
 def swap(tree, axis):
     return lax.ppermute(tree, axis, [(0, 1), (1, 0)])
+
+
+def gather_map(latent_map, inner_map, start, per_core):
+    tiles = lax.axis_size("tile")
+    chans = lax.axis_size("chan")
+    t_idx = lax.axis_index("tile")
+    c_idx = lax.axis_index("chan")
+    samples, row_local, col_local, width = latent_map.shape
+    per_tile = samples // tiles
+    blocks = latent_map.reshape(tiles, per_tile, row_local, col_local, width)
+    inner_own = lax.dynamic_slice_in_dim(inner_map, start, per_core, 0)
+    if tiles > 4 or chans != 2:
+        outgoing = lax.dynamic_slice_in_dim(blocks, start, per_core, 1)
+        outgoing = outgoing.reshape(tiles * per_core, row_local, col_local, width)
+        arrived = lax.all_to_all(outgoing, "tile", split_axis=0, concat_axis=1, tiled=True)
+        joined = (arrived.astype(jnp.float32) + inner_own.astype(jnp.float32)).astype(jnp.bfloat16)
+        return lax.all_gather(joined, "chan", axis=2, tiled=True)
+    canvas = jnp.zeros((per_core, row_local * tiles, col_local * 2, width), jnp.bfloat16)
+    for shift in range(tiles):
+        target = (t_idx + shift) % tiles
+        chunk = lax.dynamic_slice(
+            blocks, (target, start, 0, 0, 0), (1, per_core, row_local, col_local, width)
+        )[0]
+        if shift:
+            chunk = lax.ppermute(chunk, "tile", [(i, (i + shift) % tiles) for i in range(tiles)])
+        rows = ((t_idx - shift) % tiles) * row_local
+        inner_rows = lax.dynamic_slice_in_dim(inner_own, rows, row_local, 1)
+        joined = (chunk.astype(jnp.float32) + inner_rows.astype(jnp.float32)).astype(jnp.bfloat16)
+        partner = swap(joined, "chan")
+        canvas = lax.dynamic_update_slice(canvas, joined, (0, rows, c_idx * col_local, 0))
+        canvas = lax.dynamic_update_slice(canvas, partner, (0, rows, (1 - c_idx) * col_local, 0))
+    return canvas
 
 
 def convolve(joined, weight):
@@ -57,49 +89,38 @@
     heads_local = attend_weight.shape[2] // HEAD
 
     conv_other, time_other = swap((conv_weight, time_weight), "low")
+    conv_full = lax.dynamic_slice_in_dim(
+        jnp.concatenate([conv_weight, conv_other, conv_weight], axis=3), l_idx * half, 2 * half, 3
+    )
+    time_full = lax.dynamic_slice_in_dim(
+        jnp.concatenate([time_weight, time_other, time_weight], axis=1), l_idx * half, 2 * half, 1
+    )
 
     start = l_idx * per_core
-    outgoing = lax.dynamic_slice_in_dim(
-        latent_map.reshape(tiles, per_tile, row_local, col_local, width), start, per_core, 1
-    ).reshape(tiles * per_core, row_local, col_local, width)
-    arrived = lax.all_to_all(outgoing, "tile", split_axis=0, concat_axis=1, tiled=True)
-    inner_own = lax.dynamic_slice_in_dim(inner_map, start, per_core, 0)
-    joined = (arrived.astype(jnp.float32) + inner_own.astype(jnp.float32)).astype(jnp.bfloat16)
-    whole = lax.all_gather(joined, "chan", axis=2, tiled=True)
+    whole = gather_map(latent_map, inner_map, start, per_core)
 
     stamps = lax.dynamic_slice_in_dim(timestep, t_idx * per_tile + start, per_core, 0)
-    embedded = time_embedding(stamps)
-    mod_own = jnp.dot(embedded, time_weight.astype(jnp.float32), precision=lax.Precision.HIGHEST)
-    mod_other = jnp.dot(embedded, time_other.astype(jnp.float32), precision=lax.Precision.HIGHEST)
+    modulation = jnp.dot(
+        time_embedding(stamps), time_full.astype(jnp.float32), precision=lax.Precision.HIGHEST
+    )
+    convolved = convolve(whole, conv_full)
+    feat_own = jax.nn.silu(convolved * (1.0 + modulation[:, None, None, :])).astype(jnp.bfloat16)
+    feat_part = swap(feat_own, "low")
+    features = lax.dynamic_slice_in_dim(
+        jnp.concatenate([feat_own, feat_part, feat_own], axis=0), l_idx * per_core, per_tile, 0
+    )
 
-    def features_of(weight, modulation):
-        convolved = convolve(whole, weight)
-        return jax.nn.silu(convolved * (1.0 + modulation[:, None, None, :])).astype(jnp.bfloat16)
+    rows_total, cols_total = features.shape[1], features.shape[2]
+    tokens = rows_total * cols_total
 
-    feat_own = features_of(conv_weight, mod_own)
-    feat_other = features_of(conv_other, mod_other)
-    part_own, part_other = swap((feat_own, feat_other), "low")
-    first = l_idx == 0
-    half_a = jnp.where(first, jnp.concatenate([feat_own, part_other], 0), jnp.concatenate([part_other, feat_own], 0))
-    half_b = jnp.where(first, jnp.concatenate([feat_other, part_own], 0), jnp.concatenate([part_own, feat_other], 0))
+    def project(part, which):
+        return jnp.dot(part, attend_weight[which], preferred_element_type=jnp.float32).astype(jnp.bfloat16)
 
-    rows_total, cols_total = half_a.shape[1], half_a.shape[2]
-    tokens = rows_total * cols_total
-    weight_a = lax.dynamic_slice_in_dim(attend_weight, l_idx * half, half, 1)
-    weight_b = lax.dynamic_slice_in_dim(attend_weight, (1 - l_idx) * half, half, 1)
-
-    def project(part_a, part_b, which):
-        return (
-            jnp.dot(part_a, weight_a[which], preferred_element_type=jnp.float32)
-            + jnp.dot(part_b, weight_b[which], preferred_element_type=jnp.float32)
-        ).astype(jnp.bfloat16)
-
-    col_start = c_idx * col_local
-    own_a = lax.dynamic_slice_in_dim(half_a, col_start, col_local, 2)
-    own_b = lax.dynamic_slice_in_dim(half_b, col_start, col_local, 2)
-    queries = project(own_a.reshape(per_tile, -1, half), own_b.reshape(per_tile, -1, half), 0)
-    keys = project(half_a.reshape(per_tile, tokens, half), half_b.reshape(per_tile, tokens, half), 1)
-    values = project(half_a.reshape(per_tile, tokens, half), half_b.reshape(per_tile, tokens, half), 2)
+    own_cols = lax.dynamic_slice_in_dim(features, c_idx * col_local, col_local, 2)
+    flat = features.reshape(per_tile, tokens, width)
+    queries = project(own_cols.reshape(per_tile, -1, width), 0)
+    keys = project(flat, 1)
+    values = project(flat, 2)
 
     def by_head(x):
         n, k, _ = x.shape

time: 32 us -> 38.2 us (1.19)
  waiting for transfers between devices: 3.81 us -> 12.7 us
  blocking collectives: 5.78 us -> 0 us
  starting transfers between devices: 7.46 us -> 10.6 us
  matrix products: 7.33 us -> 6.43 us
  local copies, waits for them, and re-layouts: 5.76 us -> 6.47 us
    ppermute x4 -> x7, waiting for transfers between devices: 0.85 us -> 7.79 us  [swap(): return lax.ppermute(tree, axis, [(0, 1), (1, 0)])]
    all_to_all x1 -> x0, starting transfers between devices: 6.3 us -> none  [per_device(): lax.all_to_all(outgoing, 'tile', split_axis=0, concat_axis=1, tiled=True)]
    all_gather x1 -> x0, blocking collectives: 5.78 us -> none  [per_device(): whole = lax.all_gather(joined, 'chan', axis=2, tiled=True)]
    ppermute x0 -> x3, waiting for transfers between devices: none -> 4.94 us  [gather_map(): lax.ppermute(chunk, 'tile', [(i, (i + shift) % tiles) for i in range(tile...]
    ppermute x4 -> x7, starting transfers between devices: 1.16 us -> 5.87 us  [swap(): return lax.ppermute(tree, axis, [(0, 1), (1, 0)])]
    ppermute x0 -> x3, starting transfers between devices: none -> 4.68 us  [gather_map(): lax.ppermute(chunk, 'tile', [(i, (i + shift) % tiles) for i in range(tile...]
    all_to_all x1 -> x0, waiting for transfers between devices: 2.96 us -> none  [per_device(): lax.all_to_all(outgoing, 'tile', split_axis=0, concat_axis=1, tiled=True)]
    dot_general x8 -> x4, matrix products: 2.71 us -> 1.29 us  [the longest x3 0.98 us: project(): jnp.dot(part, attend_weight[which], preferred_element_type=jnp.float32)]
  transfers between devices with their start and end apart: 5 -> 10, of which waited for: 2 -> 6; matrix products, arithmetic and copies ran while one was open for 27% -> 11% of each run, Pallas kernels for 0% -> 0%
where the time goes in v2:
time: 38.2 us; the launch traced here: 38 us
  waiting for transfers between devices  12.7 us (33%)
  starting transfers between devices  10.6 us (28%)
  local copies, waits for them, and re-layouts  6.47 us (17%)
  matrix products  6.43 us (17%)
  between operations  1.02 us (3%)
  other arithmetic  0.79 us (2%)
    ppermute x7, waiting for transfers between devices, swap(): return lax.ppermute(tree, axis, [(0, 1), (1, 0)])  7.79 us
    ppermute x7, starting transfers between devices, swap(): return lax.ppermute(tree, axis, [(0, 1), (1, 0)])  5.87 us
    ppermute x3, waiting for transfers between devices, gather_map(): lax.ppermute(chunk, 'tile', [(i, (i + shift) % tiles) for i in range(tile...  4.94 us
    ppermute x3, starting transfers between devices, gather_map(): lax.ppermute(chunk, 'tile', [(i, (i + shift) % tiles) for i in range(tile...  4.68 us
    conv_general_dilated x1, matrix products, convolve(): lax.conv_general_dilated(joined, weight, window_strides=(1, 1), padding=(...  4.4 us
    dynamic_slice x1, local copies, waits for them, and re-layouts, per_device(): lax.dynamic_slice_in_dim(timestep, t_idx * per_tile + start, per_core, 0)  1.24 us
    unnamed x9, local copies, waits for them, and re-layouts  1.11 us
    dynamic_slice x1, local copies, waits for them, and re-layouts, gather_map(): inner_rows = lax.dynamic_slice_in_dim(inner_own, rows, row_local, 1)  0.98 us
  transfers between devices with their start and end apart: 10, of which 6 were waited for; matrix products, arithmetic and copies ran while one was open for 11% of the time, Pallas kernels for 0%

profile of v2, /device:TPU:0, one launch (start us, length us, event | category | flops | bytes accessed | tf_op | source)
XLA Modules:
  0.0 38.0 jit_solution(16045900420150105618)
XLA Ops:
  0.0 0.5 %collective-permute-start.7 = (bf16[3,3,512,256]{3,2,1,0:T(8,128)(2,1)}, bf16[3,3,512,256]{3,2,1,0:T(8,128)(2,1)}, u32[]{:S(2)}, u32[]{:S(2)}) collective-permute-start(bf16[3,3,512,256]{3,2,1,0:T(8,128)(2,1)} %param.9), channel_id=1, source_target_pairs={{0,1},{1,0},{2,3},{3,2},{4,5},{5,4},{6,7},{7,6},{8,9},{9,8},{10,11... | collective-permute-start | bytes 7077896 | tf_op jit(solution)/shard_map/ppermute | solution.py:21
  0.5 1.1 %copy.29 = bf16[8,4,8,512]{3,1,2,0:T(4,128)(2,1)S(1)} copy(bf16[8,4,8,512]{3,2,1,0:T(8,128)(2,1)} %param.6) | data formatting | bytes 524288 | tf_op args[0]
  1.6 1.0 %constant_dynamic-slice_fusion.2 = (bf16[1,4,8,512]{3,2,1,0:T(8,128)(2,1)S(1)}, bf16[1,4,8,512]{3,2,1,0:T(8,128)(2,1)S(1)}, bf16[1,4,8,512]{3,2,1,0:T(8,128)(2,1)S(1)}, bf16[1,4,8,512]{3,2,1,0:T(8,128)(2,1)S(1)}) fusion(bf16[2,16,8,512]{3,2,1,0:T(8,128)(2,1)} %param.7, s32[]{:T(128)S(6)} %select_n.112, s32[]{:T(128)S(6)} %select_n.131, s32[]{:T(128)S(6)} %select_n.126, ...), kind=kLoop, calls=%fused_computation.68 | loop fusion | bytes 262164 | tf_op jit(solution)/shard_map/dynamic_slice | solution.py:48
  2.6 2.6 %collective-permute-start = (bf16[1,4,8,512]{3,1,2,0:T(4,128)(2,1)S(1)}, bf16[1,4,8,512]{3,1,2,0:T(4,128)(2,1)S(1)}, u32[]{:S(2)}, u32[]{:S(2)}) collective-permute-start(bf16[1,4,8,512]{3,1,2,0:T(4,128)(2,1)S(1)} %get-tuple-element.12), channel_id=1, source_target_pairs={{0,2},{2,0},{1,3},{3,1},{4,6},{6,4},{5,7},{7,5},{8,10},{10,8},{9,1... | collective-permute-start | bytes 98312 | tf_op jit(solution)/shard_map/ppermute | solution.py:21
  5.3 1.6 %collective-permute-start.1 = (bf16[1,4,8,512]{3,1,2,0:T(4,128)(2,1)S(1)}, bf16[1,4,8,512]{3,1,2,0:T(4,128)(2,1)S(1)}, u32[]{:S(2)}, u32[]{:S(2)}) collective-permute-start(bf16[1,4,8,512]{3,1,2,0:T(4,128)(2,1)S(1)} %get-tuple-element.23), channel_id=1, source_target_pairs={{0,4},{4,8},{8,12},{12,0},{1,5},{5,9},{9,13},{13,1},{2,6},{6,10},{... | collective-permute-start | bytes 98312 | tf_op jit(solution)/shard_map/ppermute | solution.py:46
  6.9 0.4 collective-permute-done
  7.3 3.8 %collective-permute-done.1 = bf16[1,4,8,512]{3,1,2,0:T(4,128)(2,1)S(1)} collective-permute-done((bf16[1,4,8,512]{3,1,2,0:T(4,128)(2,1)S(1)}, bf16[1,4,8,512]{3,1,2,0:T(4,128)(2,1)S(1)}, u32[]{:S(2)}, u32[]{:S(2)}) %collective-permute-start.1) | collective-permute-done | bytes 32800 | tf_op jit(solution)/shard_map/ppermute | solution.py:46
  11.1 0.4 %collective-permute-start.2 = (bf16[1,4,8,512]{3,1,2,0:T(4,128)(2,1)S(1)}, bf16[1,4,8,512]{3,1,2,0:T(4,128)(2,1)S(1)}, u32[]{:S(2)}, u32[]{:S(2)}) collective-permute-start(bf16[1,4,8,512]{3,1,2,0:T(4,128)(2,1)S(1)} %get-tuple-element.10), channel_id=1, source_target_pairs={{0,2},{2,0},{1,3},{3,1},{4,6},{6,4},{5,7},{7,5},{8,10},{10,8},{9,1... | collective-permute-start | bytes 98312 | tf_op jit(solution)/shard_map/ppermute | solution.py:21
  11.5 1.0 %collective-permute-start.3 = (bf16[1,4,8,512]{3,1,2,0:T(4,128)(2,1)S(1)}, bf16[1,4,8,512]{3,1,2,0:T(4,128)(2,1)S(1)}, u32[]{:S(2)}, u32[]{:S(2)}) collective-permute-start(bf16[1,4,8,512]{3,1,2,0:T(4,128)(2,1)S(1)} %get-tuple-element.22), channel_id=1, source_target_pairs={{0,8},{4,12},{8,0},{12,4},{1,9},{5,13},{9,1},{13,5},{2,10},{6,14},... | collective-permute-start | bytes 98312 | tf_op jit(solution)/shard_map/ppermute | solution.py:46
  12.5 2.6 %collective-permute-done.2 = bf16[1,4,8,512]{3,1,2,0:T(4,128)(2,1)S(1)} collective-permute-done((bf16[1,4,8,512]{3,1,2,0:T(4,128)(2,1)S(1)}, bf16[1,4,8,512]{3,1,2,0:T(4,128)(2,1)S(1)}, u32[]{:S(2)}, u32[]{:S(2)}) %collective-permute-start.2) | collective-permute-done | bytes 32800 | tf_op jit(solution)/shard_map/ppermute | solution.py:21
  15.1 1.2 %collective-permute-done.3 = bf16[1,4,8,512]{3,1,2,0:T(4,128)(2,1)S(1)} collective-permute-done((bf16[1,4,8,512]{3,1,2,0:T(4,128)(2,1)S(1)}, bf16[1,4,8,512]{3,1,2,0:T(4,128)(2,1)S(1)}, u32[]{:S(2)}, u32[]{:S(2)}) %collective-permute-start.3) | collective-permute-done | bytes 32800 | tf_op jit(solution)/shard_map/ppermute | solution.py:46
  16.3 1.8 %collective-permute-start.4 = (bf16[1,4,8,512]{3,1,2,0:T(4,128)(2,1)S(1)}, bf16[1,4,8,512]{3,1,2,0:T(4,128)(2,1)S(1)}, u32[]{:S(2)}, u32[]{:S(2)}) collective-permute-start(bf16[1,4,8,512]{3,1,2,0:T(4,128)(2,1)S(1)} %get-tuple-element.8), channel_id=1, source_target_pairs={{0,2},{2,0},{1,3},{3,1},{4,6},{6,4},{5,7},{7,5},{8,10},{10,8},{9,1... | collective-permute-start | bytes 98312 | tf_op jit(solution)/shard_map/ppermute | solution.py:21
  18.1 2.0 %collective-permute-start.5 = (bf16[1,4,8,512]{3,1,2,0:T(4,128)(2,1)S(1)}, bf16[1,4,8,512]{3,1,2,0:T(4,128)(2,1)S(1)}, u32[]{:S(2)}, u32[]{:S(2)}) collective-permute-start(bf16[1,4,8,512]{3,1,2,0:T(4,128)(2,1)S(1)} %get-tuple-element.21), channel_id=1, source_target_pairs={{0,12},{4,0},{8,4},{12,8},{1,13},{5,1},{9,5},{13,9},{2,14},{6,2},{... | collective-permute-start | bytes 98312 | tf_op jit(solution)/shard_map/ppermute | solution.py:46
  20.1 1.2 %dynamic_slice.54 = s32[1]{0:T(128)} dynamic-slice(s32[8]{0:T(128)} %param.8, s32[]{:T(128)S(6)} %select_n.133), dynamic_slice_sizes={1} | dynamic-slice | bytes 12 | tf_op jit(solution)/shard_map/dynamic_slice | solution.py:102
  22.1 0.6 %collective-permute-start.6 = (bf16[1,4,8,512]{3,1,2,0:T(4,128)(2,1)S(1)}, bf16[1,4,8,512]{3,1,2,0:T(4,128)(2,1)S(1)}, u32[]{:S(2)}, u32[]{:S(2)}) collective-permute-start(bf16[1,4,8,512]{3,1,2,0:T(4,128)(2,1)S(1)} %get-tuple-element.6), channel_id=1, source_target_pairs={{0,2},{2,0},{1,3},{3,1},{4,6},{6,4},{5,7},{7,5},{8,10},{10,8},{9,1... | collective-permute-start | bytes 98312 | tf_op jit(solution)/shard_map/ppermute | solution.py:21
  22.8 3.3 %collective-permute-done.6 = bf16[1,4,8,512]{3,1,2,0:T(4,128)(2,1)S(1)} collective-permute-done((bf16[1,4,8,512]{3,1,2,0:T(4,128)(2,1)S(1)}, bf16[1,4,8,512]{3,1,2,0:T(4,128)(2,1)S(1)}, u32[]{:S(2)}, u32[]{:S(2)}) %collective-permute-start.6) | collective-permute-done | bytes 32800 | tf_op jit(solution)/shard_map/ppermute | solution.py:21
  26.2 0.2 copy.35
  26.5 0.3 fusion.37
  26.9 4.4 %multiply_convert_fusion = bf16[16,8,3,512]{3,1,2,0:T(8,128)(2,1)S(1)} fusion(s32[]{:T(128)S(6)} %select_n.132, bf16[3,3,512,256]{3,2,1,0:T(8,128)(2,1)S(1)} %copy-done.1, bf16[3,3,512,256]{3,2,1,0:T(8,128)(2,1)} %collective-permute-done.7, bf16[16,1,7,2,512]{4,2,3,0,1:T(8,128)(2,1)S(1)} %slice.62, bf16[16,1,8,3,512]{4,2,3,0,1:T(8,128)(2,1)S(1)} %copy.35, ...), kind=kOutput, calls=%fused_computation.20 | convolution fusion | flops 1753939968 | bytes 5736476 | tf_op jit(solution)/shard_map/conv_general_dilated | solution.py:57
  31.5 1.5 %collective-permute-done.9 = bf16[1,16,16,512]{3,1,2,0:T(8,128)(2,1)S(1)} collective-permute-done((bf16[1,16,16,512]{3,1,2,0:T(8,128)(2,1)S(1)}, bf16[1,16,16,512]{3,1,2,0:T(8,128)(2,1)S(1)}, u32[]{:S(2)}, u32[]{:S(2)}) %collective-permute-start.9) | collective-permute-done | bytes 262176 | tf_op jit(solution)/shard_map/ppermute | solution.py:21
  33.2 0.3 copy.38
  33.5 0.3 convolution_convert_fusion
  33.8 0.3 convolution_convert_fusion.1
  34.2 0.3 convolution_convert_fusion.2
  34.7 0.3 copy.40
  35.1 0.3 copy.44
  35.6 0.4 fusion.55
  36.0 0.4 fusion.12
  36.3 0.4 %fusion.11 = bf16[8,128,64]{1,2,0:T(8,128)(2,1)S(1)} fusion(f32[8,128,256]{2,1,0:T(8,128)S(1)} %get-tuple-element.33, f32[8,128]{1,0:T(8,128)S(1)} %get-tuple-element.32, bf16[8,256,64]{1,0,2:T(8,128)(2,1)S(1)} %reshape.84, f32[8,128]{1,0:T(8,128)S(1)} %fusion.12), kind=kOutput, calls=%fused_computation.14 | convolution fusion | flops 34209792 | bytes 1449984 | tf_op jit(solution)/shard_map/nqk,nkd->nqd/dot_general | solution.py:73
  36.7 0.2 copy.46
  36.9 0.2 copy.47
  37.1 0.9 %reshape.86 = bf16[2,16,8,256]{3,2,1,0:T(8,128)(2,1)} reshape(bf16[2,16,8,4,64]{4,3,2,1,0:T(4,128)(2,1)S(1)} %copy.47) | data formatting | bytes 262144 | tf_op jit(solution)/shard_map/reshape | solution.py:135
  (41 shorter events, 1.3 us)
Async XLA Ops:
  0.0 26.5 %copy-start.2 = (bf16[256,256]{1,0:T(8,128)(2,1)S(1)}, bf16[256,256]{1,0:T(8,128)(2,1)}, u32[]{:S(2)}) copy-start(bf16[256,256]{1,0:T(8,128)(2,1)} %param.10) | copy-start | bytes 393220
  0.0 26.8 %collective-permute-start.7 = (bf16[3,3,512,256]{3,2,1,0:T(8,128)(2,1)}, bf16[3,3,512,256]{3,2,1,0:T(8,128)(2,1)}, u32[]{:S(2)}, u32[]{:S(2)}) collective-permute-start(bf16[3,3,512,256]{3,2,1,0:T(8,128)(2,1)} %param.9), channel_id=1, source_target_pairs={{0,1},{1,0},{2,3},{3,2},{4,5},{5,4},{6,7},{7,6},{8,9},{9,8},{10,11... | collective-permute-start | bytes 7077896 | tf_op jit(solution)/shard_map/ppermute | solution.py:21
  1.5 25.3 %copy-start.1 = (bf16[3,3,512,256]{3,2,1,0:T(8,128)(2,1)S(1)}, bf16[3,3,512,256]{3,2,1,0:T(8,128)(2,1)}, u32[]{:S(2)}) copy-start(bf16[3,3,512,256]{3,2,1,0:T(8,128)(2,1)} %param.9) | copy-start | bytes 7077892
  1.6 25.3 %copy-start.3 = (pred[8,3]{0,1:T(4,128)(4,1)S(1)}, pred[8,3]{0,1:T(4,128)(4,1)}, u32[]{:S(2)}) copy-start(pred[8,3]{0,1:T(4,128)(4,1)} %constant.185) | copy-start | bytes 76
  2.6 4.6 %collective-permute-start = (bf16[1,4,8,512]{3,1,2,0:T(4,128)(2,1)S(1)}, bf16[1,4,8,512]{3,1,2,0:T(4,128)(2,1)S(1)}, u32[]{:S(2)}, u32[]{:S(2)}) collective-permute-start(bf16[1,4,8,512]{3,1,2,0:T(4,128)(2,1)S(1)} %get-tuple-element.12), channel_id=1, source_target_pairs={{0,2},{2,0},{1,3},{3,1},{4,6},{6,4},{5,7},{7,5},{8,10},{10,8},{9,1... | collective-permute-start | bytes 98312 | tf_op jit(solution)/shard_map/ppermute | solution.py:21
  5.3 5.8 %collective-permute-start.1 = (bf16[1,4,8,512]{3,1,2,0:T(4,128)(2,1)S(1)}, bf16[1,4,8,512]{3,1,2,0:T(4,128)(2,1)S(1)}, u32[]{:S(2)}, u32[]{:S(2)}) collective-permute-start(bf16[1,4,8,512]{3,1,2,0:T(4,128)(2,1)S(1)} %get-tuple-element.23), channel_id=1, source_target_pairs={{0,4},{4,8},{8,12},{12,0},{1,5},{5,9},{9,13},{13,1},{2,6},{6,10},{... | collective-permute-start | bytes 98312 | tf_op jit(solution)/shard_map/ppermute | solution.py:46
  11.1 4.0 %collective-permute-start.2 = (bf16[1,4,8,512]{3,1,2,0:T(4,128)(2,1)S(1)}, bf16[1,4,8,512]{3,1,2,0:T(4,128)(2,1)S(1)}, u32[]{:S(2)}, u32[]{:S(2)}) collective-permute-start(bf16[1,4,8,512]{3,1,2,0:T(4,128)(2,1)S(1)} %get-tuple-element.10), channel_id=1, source_target_pairs={{0,2},{2,0},{1,3},{3,1},{4,6},{6,4},{5,7},{7,5},{8,10},{10,8},{9,1... | collective-permute-start | bytes 98312 | tf_op jit(solution)/shard_map/ppermute | solution.py:21
  11.5 4.8 %collective-permute-start.3 = (bf16[1,4,8,512]{3,1,2,0:T(4,128)(2,1)S(1)}, bf16[1,4,8,512]{3,1,2,0:T(4,128)(2,1)S(1)}, u32[]{:S(2)}, u32[]{:S(2)}) collective-permute-start(bf16[1,4,8,512]{3,1,2,0:T(4,128)(2,1)S(1)} %get-tuple-element.22), channel_id=1, source_target_pairs={{0,8},{4,12},{8,0},{12,4},{1,9},{5,13},{9,1},{13,5},{2,10},{6,14},... | collective-permute-start | bytes 98312 | tf_op jit(solution)/shard_map/ppermute | solution.py:46
  16.3 5.7 %collective-permute-start.4 = (bf16[1,4,8,512]{3,1,2,0:T(4,128)(2,1)S(1)}, bf16[1,4,8,512]{3,1,2,0:T(4,128)(2,1)S(1)}, u32[]{:S(2)}, u32[]{:S(2)}) collective-permute-start(bf16[1,4,8,512]{3,1,2,0:T(4,128)(2,1)S(1)} %get-tuple-element.8), channel_id=1, source_target_pairs={{0,2},{2,0},{1,3},{3,1},{4,6},{6,4},{5,7},{7,5},{8,10},{10,8},{9,1... | collective-permute-start | bytes 98312 | tf_op jit(solution)/shard_map/ppermute | solution.py:21
  18.1 8.4 %collective-permute-start.8 = (bf16[256,256]{1,0:T(8,128)(2,1)}, bf16[256,256]{1,0:T(8,128)(2,1)S(1)}, u32[]{:S(2)}, u32[]{:S(2)}) collective-permute-start(bf16[256,256]{1,0:T(8,128)(2,1)} %param.10), channel_id=1, source_target_pairs={{0,1},{1,0},{2,3},{3,2},{4,5},{5,4},{6,7},{7,6},{8,9},{9,8},{10,11... | collective-permute-start | bytes 393224 | tf_op jit(solution)/shard_map/ppermute | solution.py:21
  18.1 4.0 %collective-permute-start.5 = (bf16[1,4,8,512]{3,1,2,0:T(4,128)(2,1)S(1)}, bf16[1,4,8,512]{3,1,2,0:T(4,128)(2,1)S(1)}, u32[]{:S(2)}, u32[]{:S(2)}) collective-permute-start(bf16[1,4,8,512]{3,1,2,0:T(4,128)(2,1)S(1)} %get-tuple-element.21), channel_id=1, source_target_pairs={{0,12},{4,0},{8,4},{12,8},{1,13},{5,1},{9,5},{13,9},{2,14},{6,2},{... | collective-permute-start | bytes 98312 | tf_op jit(solution)/shard_map/ppermute | solution.py:46
  22.1 4.0 %collective-permute-start.6 = (bf16[1,4,8,512]{3,1,2,0:T(4,128)(2,1)S(1)}, bf16[1,4,8,512]{3,1,2,0:T(4,128)(2,1)S(1)}, u32[]{:S(2)}, u32[]{:S(2)}) collective-permute-start(bf16[1,4,8,512]{3,1,2,0:T(4,128)(2,1)S(1)} %get-tuple-element.6), channel_id=1, source_target_pairs={{0,2},{2,0},{1,3},{3,1},{4,6},{6,4},{5,7},{7,5},{8,10},{10,8},{9,1... | collective-permute-start | bytes 98312 | tf_op jit(solution)/shard_map/ppermute | solution.py:21
  31.3 2.2 %copy-start = (bf16[3,512,256]{2,1,0:T(8,128)(2,1)S(1)}, bf16[3,512,256]{2,1,0:T(8,128)(2,1)}, u32[]{:S(2)}) copy-start(bf16[3,512,256]{2,1,0:T(8,128)(2,1)} %param.11) | copy-start | bytes 2359300
  31.4 1.6 %collective-permute-start.9 = (bf16[1,16,16,512]{3,1,2,0:T(8,128)(2,1)S(1)}, bf16[1,16,16,512]{3,1,2,0:T(8,128)(2,1)S(1)}, u32[]{:S(2)}, u32[]{:S(2)}) collective-permute-start(bf16[1,16,16,512]{3,1,2,0:T(8,128)(2,1)S(1)} %slice_bitcast_fusion), channel_id=1, source_target_pairs={{0,1},{1,0},{2,3},{3,2},{4,5},{5,4},{6,7},{7,6},{8,9},{9,8},{10,11... | collective-permute-start | bytes 786440 | tf_op jit(solution)/shard_map/ppermute | solution.py:21

commit v3 on v1

--- a/solution.py
+++ b/solution.py
@@ -61,13 +61,22 @@
     start = l_idx * per_core
     outgoing = lax.dynamic_slice_in_dim(
         latent_map.reshape(tiles, per_tile, row_local, col_local, width), start, per_core, 1
-    ).reshape(tiles * per_core, row_local, col_local, width)
-    arrived = lax.all_to_all(outgoing, "tile", split_axis=0, concat_axis=1, tiled=True)
+    )
+    arrived = lax.all_to_all(outgoing, "tile", split_axis=0, concat_axis=0, tiled=True)
+    arrived = arrived.transpose(1, 0, 2, 3, 4).reshape(per_core, tiles * row_local, col_local, width)
     inner_own = lax.dynamic_slice_in_dim(inner_map, start, per_core, 0)
     joined = (arrived.astype(jnp.float32) + inner_own.astype(jnp.float32)).astype(jnp.bfloat16)
-    whole = lax.all_gather(joined, "chan", axis=2, tiled=True)
+    if lax.axis_size("chan") == 2:
+        partner = swap(joined, "chan")
+        whole = lax.dynamic_slice_in_dim(
+            jnp.concatenate([joined, partner, joined], axis=2), c_idx * col_local, 2 * col_local, 2
+        )
+    else:
+        whole = lax.all_gather(joined, "chan", axis=2, tiled=True)
 
-    stamps = lax.dynamic_slice_in_dim(timestep, t_idx * per_tile + start, per_core, 0)
+    picks = t_idx * per_tile + start + jnp.arange(per_core)
+    chosen = jnp.arange(samples)[None, :] == picks[:, None]
+    stamps = jnp.sum(jnp.where(chosen, timestep[None, :], 0), axis=1)
     embedded = time_embedding(stamps)
     mod_own = jnp.dot(embedded, time_weight.astype(jnp.float32), precision=lax.Precision.HIGHEST)
     mod_other = jnp.dot(embedded, time_other.astype(jnp.float32), precision=lax.Precision.HIGHEST)

time: 32 us -> 33.3 us (1.041)
  blocking collectives: 5.78 us -> 0 us
  waiting for transfers between devices: 3.81 us -> 7.23 us
  other arithmetic: 0.63 us -> 3.02 us
  starting transfers between devices: 7.46 us -> 8.75 us
    all_gather x1 -> x0, blocking collectives: 5.78 us -> none  [per_device(): whole = lax.all_gather(joined, 'chan', axis=2, tiled=True)]
    ppermute x4 -> x5, waiting for transfers between devices: 0.85 us -> 4.32 us  [swap(): return lax.ppermute(tree, axis, [(0, 1), (1, 0)])]
    ppermute x4 -> x5, starting transfers between devices: 1.16 us -> 2.8 us  [swap(): return lax.ppermute(tree, axis, [(0, 1), (1, 0)])]
    reduce_sum x0 -> x1, other arithmetic: none -> 1.37 us  [per_device(): stamps = jnp.sum(jnp.where(chosen, timestep[None, :], 0), axis=1)]
    dynamic_slice x1 -> x2, local copies, waits for them, and re-layouts: 1.27 us -> 0.18 us  [per_device(): lax.dynamic_slice_in_dim(jnp.concatenate([joined, partner, joined], axis=...]
    convert_element_type x1, other arithmetic: 0.04 us -> 0.94 us  [per_device(): (arrived.astype(jnp.float32) + inner_own.astype(jnp.float32)).astype(jnp....]
    dynamic_slice x1, local copies, waits for them, and re-layouts: 0.91 us -> 1.57 us  [per_device(): lax.dynamic_slice_in_dim(latent_map.reshape(tiles, per_tile, row_local, c...]
    unnamed x9 -> x6, local copies, waits for them, and re-layouts: 0.74 us -> 1.17 us
  transfers between devices with their start and end apart: 5 -> 6, of which waited for: 2 -> 3; matrix products, arithmetic and copies ran while one was open for 27% -> 30% of each run, Pallas kernels for 0% -> 0%
where the time goes in v3:
time: 33.3 us; the launch traced here: 33 us
  starting transfers between devices  8.75 us (26%)
  matrix products  7.3 us (22%)
  waiting for transfers between devices  7.23 us (22%)
  local copies, waits for them, and re-layouts  5.65 us (17%)
  other arithmetic  3.02 us (9%)
  between operations  1 us (3%)
    all_to_all x1, starting transfers between devices, per_device(): lax.all_to_all(outgoing, 'tile', split_axis=0, concat_axis=0, tiled=True)  5.95 us
    ppermute x5, waiting for transfers between devices, swap(): return lax.ppermute(tree, axis, [(0, 1), (1, 0)])  4.32 us
    conv_general_dilated x2, matrix products, convolve(): lax.conv_general_dilated(joined, weight, window_strides=(1, 1), padding=(...  3.88 us
    all_to_all x1, waiting for transfers between devices, per_device(): lax.all_to_all(outgoing, 'tile', split_axis=0, concat_axis=0, tiled=True)  2.91 us
    ppermute x5, starting transfers between devices, swap(): return lax.ppermute(tree, axis, [(0, 1), (1, 0)])  2.8 us
    dynamic_slice x1, local copies, waits for them, and re-layouts, per_device(): lax.dynamic_slice_in_dim(latent_map.reshape(tiles, per_tile, row_local, c...  1.57 us
    reduce_sum x1, other arithmetic, per_device(): stamps = jnp.sum(jnp.where(chosen, timestep[None, :], 0), axis=1)  1.37 us
    unnamed x6, local copies, waits for them, and re-layouts  1.17 us
  transfers between devices with their start and end apart: 6, of which 3 were waited for; matrix products, arithmetic and copies ran while one was open for 30% of the time, Pallas kernels for 0%

profile of v3, /device:TPU:0, one launch (start us, length us, event | category | flops | bytes accessed | tf_op | source)
XLA Modules:
  0.0 33.0 jit_solution(4446382657662572718)
XLA Ops:
  0.0 0.5 %collective-permute-start.1 = (bf16[3,3,512,256]{3,2,1,0:T(8,128)(2,1)}, bf16[3,3,512,256]{3,2,1,0:T(8,128)(2,1)}, u32[]{:S(2)}, u32[]{:S(2)}) collective-permute-start(bf16[3,3,512,256]{3,2,1,0:T(8,128)(2,1)} %param.9), channel_id=1, source_target_pairs={{0,1},{1,0},{2,3},{3,2},{4,5},{5,4},{6,7},{7,6},{8,9},{9,8},{10,11... | collective-permute-start | bytes 7077896 | tf_op jit(solution)/shard_map/ppermute | solution.py:21
  0.5 1.6 %constant_dynamic-slice_fusion = bf16[4,1,4,8,512]{4,3,2,1,0:T(8,128)(2,1)} fusion(bf16[4,2,4,8,512]{4,3,2,1,0:T(8,128)(2,1)} %bitcast.91, s32[]{:T(128)S(6)} %select_n.43), kind=kLoop, calls=%fused_computation.71 | loop fusion | bytes 262148 | tf_op jit(solution)/shard_map/dynamic_slice | solution.py:62
  2.0 6.0 %all-to-all-start = ((bf16[4,1,4,8,512]{4,3,2,1,0:T(8,128)(2,1)}), bf16[4,1,4,8,512]{4,3,2,1,0:T(8,128)(2,1)S(1)}, u32[]{:S(2)}, u32[]{:S(2)}) async-start(bf16[4,1,4,8,512]{4,3,2,1,0:T(8,128)(2,1)} %constant_dynamic-slice_fusion), calls=%async_computation | async-start | bytes 262144 | tf_op jit(solution)/shard_map/all_to_all | solution.py:65
  8.0 0.2 collective-permute-start.2
  8.1 1.4 %fusion.39 = s32[]{:T(128)} fusion(s32[8]{0:T(128)} %param.8, s32[]{:T(128)S(6)} %add.50), kind=kLoop, calls=%fused_computation.74 | loop fusion | flops 23 | bytes 40 | tf_op jit(solution)/shard_map/reduce_sum | solution.py:79
  10.3 1.0 %fusion.53 = f32[1,256]{1,0:T(1,128)S(1)} fusion(bf16[256,256]{1,0:T(8,128)(2,1)} %param.10, f32[1,128]{1,0:T(1,128)S(1)} %get-tuple-element.23, f32[1,128]{1,0:T(1,128)S(1)} %get-tuple-element.24), kind=kOutput, calls=%fused_computation.91 | convolution fusion | flops 786688 | bytes 133120 | tf_op jit(solution)/shard_map/dot_general | solution.py:81
  11.4 0.1 fusion.52
  11.5 2.9 %all-to-all-done = bf16[4,1,4,8,512]{4,3,2,1,0:T(8,128)(2,1)S(1)} async-done(((bf16[4,1,4,8,512]{4,3,2,1,0:T(8,128)(2,1)}), bf16[4,1,4,8,512]{4,3,2,1,0:T(8,128)(2,1)S(1)}, u32[]{:S(2)}, u32[]{:S(2)}) %all-to-all-start) | async-done | bytes 131104 | tf_op jit(solution)/shard_map/all_to_all | solution.py:65
  14.4 0.9 %fusion.17 = bf16[1,16,8,512]{3,2,1,0:T(8,128)(2,1)S(1)} fusion(bf16[1,16,8,512]{3,2,1,0:T(8,128)(2,1)S(1)} %bitcast.82, bf16[2,16,8,512]{3,2,1,0:T(8,128)(2,1)} %param.7, s32[]{:T(128)S(6)} %select_n.43), kind=kLoop, calls=%fused_computation.42 | loop fusion | flops 262144 | bytes 393220 | tf_op jit(solution)/shard_map/convert_element_type | solution.py:68
  15.3 1.6 %collective-permute-start = (bf16[1,16,8,512]{3,2,1,0:T(8,128)(2,1)S(1)}, bf16[1,16,8,512]{3,2,1,0:T(8,128)(2,1)S(1)}, u32[]{:S(2)}, u32[]{:S(2)}) collective-permute-start(bf16[1,16,8,512]{3,2,1,0:T(8,128)(2,1)S(1)} %fusion.17), channel_id=1, source_target_pairs={{0,2},{2,0},{1,3},{3,1},{4,6},{6,4},{5,7},{7,5},{8,10},{10,8},{9,1... | collective-permute-start | bytes 393224 | tf_op jit(solution)/shard_map/ppermute | solution.py:21
  16.9 3.5 %collective-permute-done = bf16[1,16,8,512]{3,2,1,0:T(8,128)(2,1)S(1)} collective-permute-done((bf16[1,16,8,512]{3,2,1,0:T(8,128)(2,1)S(1)}, bf16[1,16,8,512]{3,2,1,0:T(8,128)(2,1)S(1)}, u32[]{:S(2)}, u32[]{:S(2)}) %collective-permute-start) | collective-permute-done | bytes 131104 | tf_op jit(solution)/shard_map/ppermute | solution.py:21
  20.5 0.2 copy.101
  20.7 0.2 copy.57
  21.0 1.2 %copy-done.1 = bf16[3,3,512,256]{3,2,1,0:T(8,128)(2,1)S(1)} copy-done((bf16[3,3,512,256]{3,2,1,0:T(8,128)(2,1)S(1)}, bf16[3,3,512,256]{3,2,1,0:T(8,128)(2,1)}, u32[]{:S(2)}) %copy-start.1) | copy-done | bytes 2359320
  22.2 1.1 %multiply_convert_fusion.1 = bf16[16,8,3,256]{3,1,2,0:T(8,128)(2,1)S(1)} fusion(bf16[3,3,512,256]{3,2,1,0:T(8,128)(2,1)S(1)} %copy-done.1, bf16[16,1,7,2,512]{4,2,3,0,1:T(8,128)(2,1)S(1)} %slice.76, bf16[16,1,8,3,512]{4,2,3,0,1:T(8,128)(2,1)S(1)} %copy.57, f32[256]{0:T(256)S(1)} %broadcast_add_fusion.1, pred[8,3]{0,1:T(4,128)(4,1)S(1)} %copy-done.2), kind=kOutput, calls=%fused_computation.25 | convolution fusion | flops 870875136 | bytes 3179544 | tf_op jit(solution)/shard_map/conv_general_dilated | solution.py:25
  23.5 2.8 %multiply_convert_fusion = bf16[16,8,3,256]{3,1,2,0:T(8,128)(2,1)S(1)} fusion(bf16[3,3,512,256]{3,2,1,0:T(8,128)(2,1)} %collective-permute-done.1, bf16[16,1,7,2,512]{4,2,3,0,1:T(8,128)(2,1)S(1)} %slice.76, bf16[16,1,8,3,512]{4,2,3,0,1:T(8,128)(2,1)S(1)} %copy.57, f32[256]{0:T(256)S(1)} %broadcast_add_fusion, pred[8,3]{0,1:T(4,128)(4,1)S(1)} %copy-done.2), kind=kOutput, calls=%fused_computation.24 | convolution fusion | flops 870875136 | bytes 3179544 | tf_op jit(solution)/shard_map/conv_general_dilated | solution.py:25
  26.3 0.6 %collective-permute-start.3 = (bf16[1,16,16,256]{3,1,2,0:T(8,128)(2,1)S(1)}, bf16[1,16,16,256]{3,1,2,0:T(8,128)(2,1)S(1)}, u32[]{:S(2)}, u32[]{:S(2)}) collective-permute-start(bf16[1,16,16,256]{3,1,2,0:T(8,128)(2,1)S(1)} %get-tuple-element.14), channel_id=1, source_target_pairs={{0,1},{1,0},{2,3},{3,2},{4,5},{5,4},{6,7},{7,6},{8,9},{9,8},{10,11... | collective-permute-start | bytes 393224 | tf_op jit(solution)/shard_map/ppermute | solution.py:21
  27.1 0.8 %collective-permute-done.3 = bf16[1,16,16,256]{3,1,2,0:T(8,128)(2,1)S(1)} collective-permute-done((bf16[1,16,16,256]{3,1,2,0:T(8,128)(2,1)S(1)}, bf16[1,16,16,256]{3,1,2,0:T(8,128)(2,1)S(1)}, u32[]{:S(2)}, u32[]{:S(2)}) %collective-permute-start.3) | collective-permute-done | bytes 131104 | tf_op jit(solution)/shard_map/ppermute | solution.py:21
  27.9 0.3 fusion.27
  28.2 0.3 fusion.1
  28.5 0.3 copy.68
  29.0 0.2 fusion.28
  29.2 0.2 fusion.5
  29.5 0.3 fusion.26
  29.8 0.3 fusion.2
  30.1 0.3 copy.73
  30.5 0.4 %fusion.59 = (f32[8,128]{1,0:T(8,128)S(1)}, f32[8,128,256]{2,1,0:T(8,128)S(1)}) fusion(bf16[8,128,64]{2,1,0:T(8,128)(2,1)S(1)} %bitcast.79, bf16[8,256,64]{1,0,2:T(8,128)(2,1)S(1)} %reshape.111), kind=kOutput, calls=%fused_computation.99 | convolution fusion | flops 34077696 | bytes 1445888 | tf_op jit(solution)/shard_map/nqd,nkd->nqk/dot_general | solution.py:36
  30.9 0.4 %fusion.7 = f32[8,128]{1,0:T(8,128)S(1)} fusion(f32[8,128,256]{2,1,0:T(8,128)S(1)} %get-tuple-element.22, f32[8,128]{1,0:T(8,128)S(1)} %get-tuple-element.21), kind=kLoop, calls=%fused_computation.16 | loop fusion | flops 523264 | bytes 1056768 | tf_op jit(solution)/shard_map/reduce_sum | solution.py:40
  31.3 0.4 %fusion.6 = bf16[8,128,64]{1,2,0:T(8,128)(2,1)S(1)} fusion(f32[8,128,256]{2,1,0:T(8,128)S(1)} %get-tuple-element.22, f32[8,128]{1,0:T(8,128)S(1)} %get-tuple-element.21, bf16[8,256,64]{1,0,2:T(8,128)(2,1)S(1)} %reshape.112, f32[8,128]{1,0:T(8,128)S(1)} %fusion.7), kind=kOutput, calls=%fused_computation.14 | convolution fusion | flops 34209792 | bytes 1449984 | tf_op jit(solution)/shard_map/nqk,nkd->nqd/dot_general | solution.py:41
  31.7 0.2 copy.75
  31.9 0.2 copy.76
  32.1 0.9 %reshape.114 = bf16[2,16,8,256]{3,2,1,0:T(8,128)(2,1)} reshape(bf16[2,16,8,4,64]{4,3,2,1,0:T(4,128)(2,1)S(1)} %copy.76) | data formatting | bytes 262144 | tf_op jit(solution)/shard_map/reshape | solution.py:123
  (33 shorter events, 1.2 us)
Async XLA Ops:
  0.0 27.9 %copy-start = (bf16[3,512,256]{2,1,0:T(8,128)(2,1)S(1)}, bf16[3,512,256]{2,1,0:T(8,128)(2,1)}, u32[]{:S(2)}) copy-start(bf16[3,512,256]{2,1,0:T(8,128)(2,1)} %param.11) | copy-start | bytes 2359300
  0.0 23.5 %collective-permute-start.1 = (bf16[3,3,512,256]{3,2,1,0:T(8,128)(2,1)}, bf16[3,3,512,256]{3,2,1,0:T(8,128)(2,1)}, u32[]{:S(2)}, u32[]{:S(2)}) collective-permute-start(bf16[3,3,512,256]{3,2,1,0:T(8,128)(2,1)} %param.9), channel_id=1, source_target_pairs={{0,1},{1,0},{2,3},{3,2},{4,5},{5,4},{6,7},{7,6},{8,9},{9,8},{10,11... | collective-permute-start | bytes 7077896 | tf_op jit(solution)/shard_map/ppermute | solution.py:21
  2.0 12.4 %all-to-all-start = ((bf16[4,1,4,8,512]{4,3,2,1,0:T(8,128)(2,1)}), bf16[4,1,4,8,512]{4,3,2,1,0:T(8,128)(2,1)S(1)}, u32[]{:S(2)}, u32[]{:S(2)}) async-start(bf16[4,1,4,8,512]{4,3,2,1,0:T(8,128)(2,1)} %constant_dynamic-slice_fusion), calls=%async_computation | async-start | bytes 262144 | tf_op jit(solution)/shard_map/all_to_all | solution.py:65
  8.0 3.4 %collective-permute-start.2 = (bf16[256,256]{1,0:T(8,128)(2,1)}, bf16[256,256]{1,0:T(8,128)(2,1)S(1)}, u32[]{:S(2)}, u32[]{:S(2)}) collective-permute-start(bf16[256,256]{1,0:T(8,128)(2,1)} %param.10), channel_id=1, source_target_pairs={{0,1},{1,0},{2,3},{3,2},{4,5},{5,4},{6,7},{7,6},{8,9},{9,8},{10,11... | collective-permute-start | bytes 393224 | tf_op jit(solution)/shard_map/ppermute | solution.py:21
  15.3 5.0 %collective-permute-start = (bf16[1,16,8,512]{3,2,1,0:T(8,128)(2,1)S(1)}, bf16[1,16,8,512]{3,2,1,0:T(8,128)(2,1)S(1)}, u32[]{:S(2)}, u32[]{:S(2)}) collective-permute-start(bf16[1,16,8,512]{3,2,1,0:T(8,128)(2,1)S(1)} %fusion.17), channel_id=1, source_target_pairs={{0,2},{2,0},{1,3},{3,1},{4,6},{6,4},{5,7},{7,5},{8,10},{10,8},{9,1... | collective-permute-start | bytes 393224 | tf_op jit(solution)/shard_map/ppermute | solution.py:21
  20.5 1.7 %copy-start.1 = (bf16[3,3,512,256]{3,2,1,0:T(8,128)(2,1)S(1)}, bf16[3,3,512,256]{3,2,1,0:T(8,128)(2,1)}, u32[]{:S(2)}) copy-start(bf16[3,3,512,256]{3,2,1,0:T(8,128)(2,1)} %param.9) | copy-start | bytes 7077892
  20.5 1.7 %copy-start.2 = (pred[8,3]{0,1:T(4,128)(4,1)S(1)}, pred[8,3]{0,1:T(4,128)(4,1)}, u32[]{:S(2)}) copy-start(pred[8,3]{0,1:T(4,128)(4,1)} %constant.49) | copy-start | bytes 76
  23.4 3.5 %collective-permute-start.4 = (bf16[1,16,16,256]{3,1,2,0:T(8,128)(2,1)S(1)}, bf16[1,16,16,256]{3,1,2,0:T(8,128)(2,1)S(1)}, u32[]{:S(2)}, u32[]{:S(2)}) collective-permute-start(bf16[1,16,16,256]{3,1,2,0:T(8,128)(2,1)S(1)} %get-tuple-element.16), channel_id=1, source_target_pairs={{0,1},{1,0},{2,3},{3,2},{4,5},{5,4},{6,7},{7,6},{8,9},{9,8},{10,11... | collective-permute-start | bytes 393224 | tf_op jit(solution)/shard_map/ppermute | solution.py:21
  26.3 1.5 %collective-permute-start.3 = (bf16[1,16,16,256]{3,1,2,0:T(8,128)(2,1)S(1)}, bf16[1,16,16,256]{3,1,2,0:T(8,128)(2,1)S(1)}, u32[]{:S(2)}, u32[]{:S(2)}) collective-permute-start(bf16[1,16,16,256]{3,1,2,0:T(8,128)(2,1)S(1)} %get-tuple-element.14), channel_id=1, source_target_pairs={{0,1},{1,0},{2,3},{3,2},{4,5},{5,4},{6,7},{7,6},{8,9},{9,8},{10,11... | collective-permute-start | bytes 393224 | tf_op jit(solution)/shard_map/ppermute | solution.py:21

commit v4 on v1

--- a/solution.py
+++ b/solution.py
@@ -78,40 +78,47 @@
 
     feat_own = features_of(conv_weight, mod_own)
     feat_other = features_of(conv_other, mod_other)
-    part_own, part_other = swap((feat_own, feat_other), "low")
-    first = l_idx == 0
-    half_a = jnp.where(first, jnp.concatenate([feat_own, part_other], 0), jnp.concatenate([part_other, feat_own], 0))
-    half_b = jnp.where(first, jnp.concatenate([feat_other, part_own], 0), jnp.concatenate([part_own, feat_other], 0))
+    nat_own = lax.dynamic_slice_in_dim(
+        jnp.concatenate([feat_own, feat_other, feat_own], axis=3), l_idx * half, 2 * half, 3
+    )
+    nat_part = swap(nat_own, "low")
+    features = lax.dynamic_slice_in_dim(
+        jnp.concatenate([nat_own, nat_part, nat_own], axis=0), l_idx * per_core, per_tile, 0
+    )
+    rows_total, cols_total = features.shape[1], features.shape[2]
+    tokens = rows_total * cols_total
 
-    rows_total, cols_total = half_a.shape[1], half_a.shape[2]
-    tokens = rows_total * cols_total
-    weight_a = lax.dynamic_slice_in_dim(attend_weight, l_idx * half, half, 1)
-    weight_b = lax.dynamic_slice_in_dim(attend_weight, (1 - l_idx) * half, half, 1)
+    def project(part, which):
+        return jnp.dot(part, attend_weight[which], preferred_element_type=jnp.float32).astype(jnp.bfloat16)
 
-    def project(part_a, part_b, which):
-        return (
-            jnp.dot(part_a, weight_a[which], preferred_element_type=jnp.float32)
-            + jnp.dot(part_b, weight_b[which], preferred_element_type=jnp.float32)
-        ).astype(jnp.bfloat16)
-
-    col_start = c_idx * col_local
-    own_a = lax.dynamic_slice_in_dim(half_a, col_start, col_local, 2)
-    own_b = lax.dynamic_slice_in_dim(half_b, col_start, col_local, 2)
-    queries = project(own_a.reshape(per_tile, -1, half), own_b.reshape(per_tile, -1, half), 0)
-    keys = project(half_a.reshape(per_tile, tokens, half), half_b.reshape(per_tile, tokens, half), 1)
-    values = project(half_a.reshape(per_tile, tokens, half), half_b.reshape(per_tile, tokens, half), 2)
+    own_cols = lax.dynamic_slice_in_dim(features, c_idx * col_local, col_local, 2)
+    flat = features.reshape(per_tile, tokens, width)
+    queries = project(own_cols.reshape(per_tile, -1, width), 0)
+    keys = project(flat, 1)
+    values = project(flat, 2)
+    query_count = queries.shape[1]
+    if tokens * query_count * 4 * per_tile * heads_local <= (8 << 20):
+        split = lambda x: x.reshape(per_tile, x.shape[1], heads_local, HEAD)
+        q4, k4, v4 = split(queries), split(keys), split(values)
+        scores = jnp.einsum("bqhd,bkhd->bhqk", q4, k4, preferred_element_type=jnp.float32)
+        scores = scores * HEAD ** (-0.5)
+        row_peak = jnp.max(scores, axis=3, keepdims=True)
+        weights = jnp.exp(scores - row_peak)
+        totals = jnp.sum(weights, axis=3)
+        summed = jnp.einsum(
+            "bhqk,bkhd->bqhd", weights.astype(jnp.bfloat16), v4, preferred_element_type=jnp.float32
+        )
+        out = (summed / totals.transpose(0, 2, 1)[..., None]).astype(jnp.bfloat16)
+        return out.reshape(per_tile, rows_total, col_local, heads_local * HEAD)
 
     def by_head(x):
         n, k, _ = x.shape
         return x.reshape(n, k, heads_local, HEAD).transpose(0, 2, 1, 3).reshape(n * heads_local, k, HEAD)
 
     q_heads, k_heads, v_heads = by_head(queries), by_head(keys), by_head(values)
-    if tokens * tokens * 4 * q_heads.shape[0] <= (8 << 20):
-        out = attend(q_heads, k_heads, v_heads)
-    else:
-        out = lax.map(lambda trio: attend(*(x[None] for x in trio))[0], (q_heads, k_heads, v_heads))
-    out = out.reshape(per_tile, heads_local, row_local * tiles, col_local, HEAD)
-    return out.transpose(0, 2, 3, 1, 4).reshape(per_tile, row_local * tiles, col_local, heads_local * HEAD)
+    out = lax.map(lambda trio: attend(*(x[None] for x in trio))[0], (q_heads, k_heads, v_heads))
+    out = out.reshape(per_tile, heads_local, rows_total, col_local, HEAD)
+    return out.transpose(0, 2, 3, 1, 4).reshape(per_tile, rows_total, col_local, heads_local * HEAD)
 
 
 def solution(mesh):

time: 32 us -> 28.4 us (0.89)
  matrix products: 7.33 us -> 5.18 us
  local copies, waits for them, and re-layouts: 5.76 us -> 4.41 us
  starting transfers between devices: 7.46 us -> 6.92 us
  waiting for transfers between devices: 3.81 us -> 4.32 us
    conv_general_dilated x2, matrix products: 3.88 us -> 2.25 us  [convolve(): lax.conv_general_dilated(joined, weight, window_strides=(1, 1), padding=(...]
    dynamic_slice x1, local copies, waits for them, and re-layouts: 0.91 us -> 0.01 us  [per_device(): lax.dynamic_slice_in_dim(latent_map.reshape(tiles, per_tile, row_local, c...]
    ppermute x4 -> x3, waiting for transfers between devices: 0.85 us -> 1.56 us  [swap(): return lax.ppermute(tree, axis, [(0, 1), (1, 0)])]
    another operation x4 -> x0, local copies, waits for them, and re-layouts: 0.59 us -> none
    ppermute x4 -> x3, starting transfers between devices: 1.16 us -> 0.6 us  [swap(): return lax.ppermute(tree, axis, [(0, 1), (1, 0)])]
    dot_general x8 -> x5, matrix products: 2.27 us -> 1.76 us  [the longest x3 0.94 us: project(): jnp.dot(part, attend_weight[which], preferred_element_type=jnp.float32)]
    unnamed x9 -> x11, local copies, waits for them, and re-layouts: 0.74 us -> 1.17 us
    reshape x3 -> x1, local copies, waits for them, and re-layouts: 1.08 us -> 0.87 us  [per_device(): return out.reshape(per_tile, rows_total, col_local, heads_local * HEAD)]
  transfers between devices with their start and end apart: 5 -> 4, of which waited for: 2 -> 2; matrix products, arithmetic and copies ran while one was open for 27% -> 17% of each run, Pallas kernels for 0% -> 0%
where the time goes in v4:
time: 28.4 us; the launch traced here: 28.2 us
  starting transfers between devices  6.92 us (24%)
  blocking collectives  5.78 us (20%)
  matrix products  5.18 us (18%)
  local copies, waits for them, and re-layouts  4.41 us (16%)
  waiting for transfers between devices  4.32 us (15%)
  between operations  0.94 us (3%)
  other arithmetic  0.62 us (2%)
    all_to_all x1, starting transfers between devices, per_device(): lax.all_to_all(outgoing, 'tile', split_axis=0, concat_axis=1, tiled=True)  6.32 us
    all_gather x1, blocking collectives, per_device(): whole = lax.all_gather(joined, 'chan', axis=2, tiled=True)  5.78 us
    all_to_all x1, waiting for transfers between devices, per_device(): lax.all_to_all(outgoing, 'tile', split_axis=0, concat_axis=1, tiled=True)  2.76 us
    conv_general_dilated x2, matrix products, convolve(): lax.conv_general_dilated(joined, weight, window_strides=(1, 1), padding=(...  2.25 us
    ppermute x3, waiting for transfers between devices, swap(): return lax.ppermute(tree, axis, [(0, 1), (1, 0)])  1.56 us
    dynamic_slice x1, local copies, waits for them, and re-layouts, per_device(): lax.dynamic_slice_in_dim(timestep, t_idx * per_tile + start, per_core, 0)  1.32 us
    unnamed x11, local copies, waits for them, and re-layouts  1.17 us
    dot_general x1, matrix products, per_device(): jnp.dot(embedded, time_weight.astype(jnp.float32), precision=lax.Precisio...  1.04 us
  transfers between devices with their start and end apart: 4, of which 2 were waited for; matrix products, arithmetic and copies ran while one was open for 17% of the time, Pallas kernels for 0%

profile of v4, /device:TPU:0, one launch (start us, length us, event | category | flops | bytes accessed | tf_op | source)
XLA Modules:
  0.0 28.2 jit_solution(10098414527430775406)
XLA Ops:
  0.0 0.5 %collective-permute-start = (bf16[3,3,512,256]{3,2,1,0:T(8,128)(2,1)}, bf16[3,3,512,256]{3,2,1,0:T(8,128)(2,1)S(1)}, u32[]{:S(2)}, u32[]{:S(2)}) collective-permute-start(bf16[3,3,512,256]{3,2,1,0:T(8,128)(2,1)} %param.9), channel_id=1, source_target_pairs={{0,1},{1,0},{2,3},{3,2},{4,5},{5,4},{6,7},{7,6},{8,9},{9,8},{10,11... | collective-permute-start | bytes 7077896 | tf_op jit(solution)/shard_map/ppermute | solution.py:21
  0.5 0.1 collective-permute-start.1
  0.5 0.4 %copy-done = bf16[8,4,8,512]{3,2,1,0:T(8,128)(2,1)S(1)} copy-done((bf16[8,4,8,512]{3,2,1,0:T(8,128)(2,1)S(1)}, bf16[8,4,8,512]{3,2,1,0:T(8,128)(2,1)}, u32[]{:S(2)}) %copy-start) | copy-done | bytes 262168
  1.0 0.7 %copy.57 = bf16[4,1,4,8,512]{4,2,3,0,1:T(4,128)(2,1)} copy(bf16[4,1,4,8,512]{4,3,2,1,0:T(8,128)(2,1)S(1)} %constant_dynamic-slice_fusion.2) | data formatting | bytes 262144
  1.7 6.3 %all-to-all-start = ((bf16[4,4,8,512]{3,1,2,0:T(4,128)(2,1)}), bf16[4,4,8,512]{3,1,2,0:T(4,128)(2,1)S(1)}, u32[]{:S(2)}, u32[]{:S(2)}) async-start(bf16[4,4,8,512]{3,1,2,0:T(4,128)(2,1)} %bitcast.62), calls=%async_computation | async-start | bytes 262144 | tf_op jit(solution)/shard_map/all_to_all | solution.py:65
  8.0 1.3 %dynamic_slice.21 = s32[1]{0:T(128)} dynamic-slice(s32[8]{0:T(128)} %param.8, s32[]{:T(128)S(6)} %select_n.21), dynamic_slice_sizes={1} | dynamic-slice | bytes 12 | tf_op jit(solution)/shard_map/dynamic_slice | solution.py:70
  10.0 0.1 fusion.23
  10.1 1.0 %fusion.32 = f32[1,256]{1,0:T(1,128)S(1)} fusion(bf16[256,256]{1,0:T(8,128)(2,1)} %param.10, f32[1,128]{1,0:T(1,128)S(1)} %get-tuple-element.7, f32[1,128]{1,0:T(1,128)S(1)} %get-tuple-element.8), kind=kOutput, calls=%fused_computation.52 | convolution fusion | flops 786688 | bytes 133120 | tf_op jit(solution)/shard_map/dot_general | solution.py:72
  11.1 0.0 collective-permute-done.1
  11.2 0.1 fusion.31
  11.3 2.8 %all-to-all-done = bf16[4,4,8,512]{3,1,2,0:T(4,128)(2,1)S(1)} async-done(((bf16[4,4,8,512]{3,1,2,0:T(4,128)(2,1)}), bf16[4,4,8,512]{3,1,2,0:T(4,128)(2,1)S(1)}, u32[]{:S(2)}, u32[]{:S(2)}) %all-to-all-start) | async-done | bytes 131104 | tf_op jit(solution)/shard_map/all_to_all | solution.py:65
  14.2 0.0 copy-start.3
  14.2 0.0 copy-start.4
  14.2 5.8 %all_gather.3 = bf16[1,16,16,512]{3,1,0,2:T(8,128)(2,1)S(1)} all-gather(bf16[1,16,8,512]{3,1,0,2:T(8,128)(2,1)S(1)} %copy.42), channel_id=1, replica_groups=mesh['groups'=2,'tile'=4,'chan'=2,'low'=2] {'chan'}, dimensions={2}, use_global_device_ids=true | all-gather | bytes 393216 | tf_op jit(solution)/shard_map/all_gather | solution.py:68
  20.1 0.2 copy.44
  20.3 0.1 slice.15
  20.4 1.1 %multiply_convert_fusion.1 = bf16[16,8,3,256]{3,1,2,0:T(8,128)(2,1)S(1)} fusion(bf16[3,3,512,256]{3,2,1,0:T(8,128)(2,1)S(1)} %copy-done.3, bf16[16,1,7,2,512]{4,2,3,0,1:T(8,128)(2,1)S(1)} %slice.15, bf16[16,1,8,3,512]{4,2,3,0,1:T(8,128)(2,1)S(1)} %copy.44, f32[256]{0:T(256)S(1)} %broadcast_add_fusion.1, pred[8,3]{0,1:T(4,128)(4,1)S(1)} %copy-done.4), kind=kOutput, calls=%fused_computation.22 | convolution fusion | flops 870875136 | bytes 3179544 | tf_op jit(solution)/shard_map/conv_general_dilated | solution.py:25
  21.5 1.1 %multiply_convert_fusion = bf16[16,8,3,256]{3,1,2,0:T(8,128)(2,1)S(1)} fusion(bf16[3,3,512,256]{3,2,1,0:T(8,128)(2,1)S(1)} %collective-permute-done, bf16[16,1,7,2,512]{4,2,3,0,1:T(8,128)(2,1)S(1)} %slice.15, bf16[16,1,8,3,512]{4,2,3,0,1:T(8,128)(2,1)S(1)} %copy.44, f32[256]{0:T(256)S(1)} %broadcast_add_fusion, pred[8,3]{0,1:T(4,128)(4,1)S(1)} %copy-done.4), kind=kOutput, calls=%fused_computation.21 | convolution fusion | flops 870875136 | bytes 3179544 | tf_op jit(solution)/shard_map/conv_general_dilated | solution.py:25
  22.7 0.1 copy.45
  22.9 0.2 copy.56
  23.0 0.1 collective-permute-start.2
  23.1 1.5 %collective-permute-done.2 = bf16[1,16,16,512]{3,2,1,0:T(8,128)(2,1)S(1)} collective-permute-done((bf16[1,16,16,512]{3,2,1,0:T(8,128)(2,1)S(1)}, bf16[1,16,16,512]{3,2,1,0:T(8,128)(2,1)S(1)}, u32[]{:S(2)}, u32[]{:S(2)}) %collective-permute-start.2) | collective-permute-done | bytes 262176 | tf_op jit(solution)/shard_map/ppermute | solution.py:21
  24.6 0.1 pad_maximum_fusion
  24.8 0.3 %convolution_convert_fusion = bf16[2,256,256]{1,2,0:T(8,128)(2,1)S(1)} fusion(bf16[2,256,512]{2,1,0:T(8,128)(2,1)S(1)} %bitcast.65, bf16[3,512,256]{2,1,0:T(8,128)(2,1)S(1)} %copy-done.1), kind=kOutput, calls=%fused_computation.3 | convolution fusion | flops 134348800 | bytes 1048576 | tf_op jit(solution)/shard_map/dot_general | solution.py:92
  25.1 0.3 %convolution_convert_fusion.1 = bf16[2,256,256]{1,2,0:T(8,128)(2,1)S(1)} fusion(bf16[2,256,512]{2,1,0:T(8,128)(2,1)S(1)} %bitcast.66, bf16[3,512,256]{2,1,0:T(8,128)(2,1)S(1)} %copy-done.1), kind=kOutput, calls=%fused_computation.4 | convolution fusion | flops 134348800 | bytes 1048576 | tf_op jit(solution)/shard_map/dot_general | solution.py:92
  25.5 0.2 convolution_convert_fusion.2
  25.8 0.1 copy.48
  25.9 0.4 %fusion.33 = (f32[2,4,128]{2,1,0:T(4,128)S(1)}, f32[2,4,128,256]{3,2,1,0:T(8,128)S(1)}) fusion(bf16[2,128,4,64]{1,3,2,0:T(8,128)(2,1)S(1)} %bitcast.74, bf16[2,256,4,64]{1,3,2,0:T(8,128)(2,1)S(1)} %bitcast.72), kind=kOutput, calls=%fused_computation.53 | convolution fusion | flops 34077696 | bytes 1445888 | tf_op jit(solution)/shard_map/bqhd,bkhd->bhqk/dot_general | solution.py:103
  26.3 0.4 %fusion.5 = f32[2,4,128]{2,1,0:T(4,128)S(1)} fusion(f32[2,4,128,256]{3,2,1,0:T(8,128)S(1)} %get-tuple-element.6, f32[2,4,128]{2,1,0:T(4,128)S(1)} %get-tuple-element.5), kind=kLoop, calls=%fused_computation.14 | loop fusion | flops 523264 | bytes 1056768 | tf_op jit(solution)/shard_map/reduce_sum | solution.py:107
  26.7 0.4 %fusion.4 = bf16[2,128,4,64]{1,3,2,0:T(8,128)(2,1)S(1)} fusion(bf16[2,256,4,64]{1,3,2,0:T(8,128)(2,1)S(1)} %bitcast.75, f32[2,4,128,256]{3,2,1,0:T(8,128)S(1)} %get-tuple-element.6, f32[2,4,128]{2,1,0:T(4,128)S(1)} %get-tuple-element.5, f32[2,128,4]{1,2,0:T(4,128)S(1)} %bitcast.76), kind=kOutput, calls=%fused_computation.11 | convolution fusion | flops 34209792 | bytes 1449984 | tf_op jit(solution)/shard_map/bhqk,bkhd->bqhd/dot_general | solution.py:108
  27.1 0.2 copy.50
  27.3 0.9 %reshape.93 = bf16[2,16,8,256]{3,2,1,0:T(8,128)(2,1)} reshape(bf16[2,128,4,64]{3,2,1,0:T(4,128)(2,1)S(1)} %copy.50) | data formatting | bytes 262144 | tf_op jit(solution)/shard_map/reshape | solution.py:112
  (19 shorter events, 0.3 us)
Async XLA Ops:
  0.0 1.0 %copy-start = (bf16[8,4,8,512]{3,2,1,0:T(8,128)(2,1)S(1)}, bf16[8,4,8,512]{3,2,1,0:T(8,128)(2,1)}, u32[]{:S(2)}) copy-start(bf16[8,4,8,512]{3,2,1,0:T(8,128)(2,1)} %param.6) | copy-start | bytes 786436
  0.0 14.1 %copy-start.2 = (bf16[2,16,8,512]{3,2,1,0:T(8,128)(2,1)S(1)}, bf16[2,16,8,512]{3,2,1,0:T(8,128)(2,1)}, u32[]{:S(2)}) copy-start(bf16[2,16,8,512]{3,2,1,0:T(8,128)(2,1)} %param.7) | copy-start | bytes 786436
  0.0 21.5 %collective-permute-start = (bf16[3,3,512,256]{3,2,1,0:T(8,128)(2,1)}, bf16[3,3,512,256]{3,2,1,0:T(8,128)(2,1)S(1)}, u32[]{:S(2)}, u32[]{:S(2)}) collective-permute-start(bf16[3,3,512,256]{3,2,1,0:T(8,128)(2,1)} %param.9), channel_id=1, source_target_pairs={{0,1},{1,0},{2,3},{3,2},{4,5},{5,4},{6,7},{7,6},{8,9},{9,8},{10,11... | collective-permute-start | bytes 7077896 | tf_op jit(solution)/shard_map/ppermute | solution.py:21
  0.5 10.7 %collective-permute-start.1 = (bf16[256,256]{1,0:T(8,128)(2,1)}, bf16[256,256]{1,0:T(8,128)(2,1)S(1)}, u32[]{:S(2)}, u32[]{:S(2)}) collective-permute-start(bf16[256,256]{1,0:T(8,128)(2,1)} %param.10), channel_id=1, source_target_pairs={{0,1},{1,0},{2,3},{3,2},{4,5},{5,4},{6,7},{7,6},{8,9},{9,8},{10,11... | collective-permute-start | bytes 393224 | tf_op jit(solution)/shard_map/ppermute | solution.py:21
  1.7 12.4 %all-to-all-start = ((bf16[4,4,8,512]{3,1,2,0:T(4,128)(2,1)}), bf16[4,4,8,512]{3,1,2,0:T(4,128)(2,1)S(1)}, u32[]{:S(2)}, u32[]{:S(2)}) async-start(bf16[4,4,8,512]{3,1,2,0:T(4,128)(2,1)} %bitcast.62), calls=%async_computation | async-start | bytes 262144 | tf_op jit(solution)/shard_map/all_to_all | solution.py:65
  14.2 6.2 %copy-start.3 = (bf16[3,3,512,256]{3,2,1,0:T(8,128)(2,1)S(1)}, bf16[3,3,512,256]{3,2,1,0:T(8,128)(2,1)}, u32[]{:S(2)}) copy-start(bf16[3,3,512,256]{3,2,1,0:T(8,128)(2,1)} %param.9) | copy-start | bytes 7077892
  14.2 6.2 %copy-start.4 = (pred[8,3]{0,1:T(4,128)(4,1)S(1)}, pred[8,3]{0,1:T(4,128)(4,1)}, u32[]{:S(2)}) copy-start(pred[8,3]{0,1:T(4,128)(4,1)} %constant.67) | copy-start | bytes 76
  23.0 1.8 %copy-start.1 = (bf16[3,512,256]{2,1,0:T(8,128)(2,1)S(1)}, bf16[3,512,256]{2,1,0:T(8,128)(2,1)}, u32[]{:S(2)}) copy-start(bf16[3,512,256]{2,1,0:T(8,128)(2,1)} %param.11) | copy-start | bytes 2359300
  23.0 1.6 %collective-permute-start.2 = (bf16[1,16,16,512]{3,2,1,0:T(8,128)(2,1)S(1)}, bf16[1,16,16,512]{3,2,1,0:T(8,128)(2,1)S(1)}, u32[]{:S(2)}, u32[]{:S(2)}) collective-permute-start(bf16[1,16,16,512]{3,2,1,0:T(8,128)(2,1)S(1)} %bitcast.69), channel_id=1, source_target_pairs={{0,1},{1,0},{2,3},{3,2},{4,5},{5,4},{6,7},{7,6},{8,9},{9,8},{10,11... | collective-permute-start | bytes 786440 | tf_op jit(solution)/shard_map/ppermute | solution.py:21

commit v5 on v4

--- a/solution.py
+++ b/solution.py
@@ -98,18 +98,21 @@
     values = project(flat, 2)
     query_count = queries.shape[1]
     if tokens * query_count * 4 * per_tile * heads_local <= (8 << 20):
-        split = lambda x: x.reshape(per_tile, x.shape[1], heads_local, HEAD)
-        q4, k4, v4 = split(queries), split(keys), split(values)
-        scores = jnp.einsum("bqhd,bkhd->bhqk", q4, k4, preferred_element_type=jnp.float32)
-        scores = scores * HEAD ** (-0.5)
+        lanes = heads_local * HEAD
+        row_head = jnp.arange(heads_local * tokens)[:, None] // tokens
+        lane_head = jnp.arange(lanes)[None, :] // HEAD
+        own_head = row_head == lane_head
+        key_blocks = jnp.where(own_head, jnp.tile(keys, (1, heads_local, 1)), 0)
+        value_blocks = jnp.where(own_head, jnp.tile(values, (1, heads_local, 1)), 0)
+        scores = jnp.einsum("bqc,bjc->bqj", queries, key_blocks, preferred_element_type=jnp.float32)
+        scores = (scores * HEAD ** (-0.5)).reshape(per_tile, query_count, heads_local, tokens)
         row_peak = jnp.max(scores, axis=3, keepdims=True)
         weights = jnp.exp(scores - row_peak)
         totals = jnp.sum(weights, axis=3)
-        summed = jnp.einsum(
-            "bhqk,bkhd->bqhd", weights.astype(jnp.bfloat16), v4, preferred_element_type=jnp.float32
-        )
-        out = (summed / totals.transpose(0, 2, 1)[..., None]).astype(jnp.bfloat16)
-        return out.reshape(per_tile, rows_total, col_local, heads_local * HEAD)
+        rounded = weights.astype(jnp.bfloat16).reshape(per_tile, query_count, heads_local * tokens)
+        summed = jnp.einsum("bqj,bjc->bqc", rounded, value_blocks, preferred_element_type=jnp.float32)
+        out = (summed / jnp.repeat(totals, HEAD, axis=2)).astype(jnp.bfloat16)
+        return out.reshape(per_tile, rows_total, col_local, lanes)
 
     def by_head(x):
         n, k, _ = x.shape

time: 28.4 us -> 37.4 us (1.32)
  local copies, waits for them, and re-layouts: 4.41 us -> 9.13 us
  matrix products: 5.18 us -> 7.71 us
  other arithmetic: 0.62 us -> 2.38 us
    sub x0 -> x2, local copies, waits for them, and re-layouts: none -> 3.06 us  [per_device(): weights = jnp.exp(scores - row_peak)]
    dot_general x2, matrix products: 0.82 us -> 3.73 us  [the longest x1 1.93 us: per_device(): jnp.einsum('bqj,bjc->bqc', rounded, value_blocks, preferred_element_type=...]
    reduce_sum x0 -> x1, local copies, waits for them, and re-layouts: none -> 0.98 us  [per_device(): totals = jnp.sum(weights, axis=3)]
    reduce_sum x1, other arithmetic: 0.39 us -> 1.37 us  [per_device(): totals = jnp.sum(weights, axis=3)]
    unnamed x11 -> x13, local copies, waits for them, and re-layouts: 1.17 us -> 1.75 us
    reshape x1 -> x2, local copies, waits for them, and re-layouts: 0.87 us -> 1.33 us  [the longest x1 0.84 us: per_device(): out = (summed / jnp.repeat(totals, HEAD, axis=2)).astype(jnp.bfloat16)]
    dot_general x3 -> x2, matrix products: 0.94 us -> 0.58 us  [project(): jnp.dot(part, attend_weight[which], preferred_element_type=jnp.float32)]
  transfers between devices with their start and end apart: 4 -> 4, of which waited for: 2 -> 2; matrix products, arithmetic and copies ran while one was open for 17% -> 13% of each run, Pallas kernels for 0% -> 0%
where the time goes in v5:
time: 37.4 us; the launch traced here: 37 us
  local copies, waits for them, and re-layouts  9.13 us (24%)
  matrix products  7.71 us (21%)
  starting transfers between devices  6.84 us (18%)
  blocking collectives  5.78 us (15%)
  waiting for transfers between devices  4.25 us (11%)
  other arithmetic  2.38 us (6%)
  between operations  0.88 us (2%)
    all_to_all x1, starting transfers between devices, per_device(): lax.all_to_all(outgoing, 'tile', split_axis=0, concat_axis=1, tiled=True)  6.32 us
    all_gather x1, blocking collectives, per_device(): whole = lax.all_gather(joined, 'chan', axis=2, tiled=True)  5.78 us
    sub x2, local copies, waits for them, and re-layouts, per_device(): weights = jnp.exp(scores - row_peak)  3.06 us
    all_to_all x1, waiting for transfers between devices, per_device(): lax.all_to_all(outgoing, 'tile', split_axis=0, concat_axis=1, tiled=True)  2.97 us
    conv_general_dilated x2, matrix products, convolve(): lax.conv_general_dilated(joined, weight, window_strides=(1, 1), padding=(...  2.21 us
    dot_general x1, matrix products, per_device(): jnp.einsum('bqj,bjc->bqc', rounded, value_blocks, preferred_element_type=...  1.93 us
    dot_general x1, matrix products, per_device(): jnp.einsum('bqc,bjc->bqj', queries, key_blocks, preferred_element_type=jn...  1.8 us
    unnamed x13, local copies, waits for them, and re-layouts  1.75 us
  transfers between devices with their start and end apart: 4, of which 2 were waited for; matrix products, arithmetic and copies ran while one was open for 13% of the time, Pallas kernels for 0%

profile of v5, /device:TPU:0, one launch (start us, length us, event | category | flops | bytes accessed | tf_op | source)
XLA Modules:
  0.0 37.0 jit_solution(7897686608325787325)
XLA Ops:
  0.0 0.5 %collective-permute-start = (bf16[3,3,512,256]{3,2,1,0:T(8,128)(2,1)}, bf16[3,3,512,256]{3,2,1,0:T(8,128)(2,1)S(1)}, u32[]{:S(2)}, u32[]{:S(2)}) collective-permute-start(bf16[3,3,512,256]{3,2,1,0:T(8,128)(2,1)} %param.9), channel_id=1, source_target_pairs={{0,1},{1,0},{2,3},{3,2},{4,5},{5,4},{6,7},{7,6},{8,9},{9,8},{10,11... | collective-permute-start | bytes 7077896 | tf_op jit(solution)/shard_map/ppermute | solution.py:21
  0.5 0.5 %copy-done = bf16[8,4,8,512]{3,2,1,0:T(8,128)(2,1)S(1)} copy-done((bf16[8,4,8,512]{3,2,1,0:T(8,128)(2,1)S(1)}, bf16[8,4,8,512]{3,2,1,0:T(8,128)(2,1)}, u32[]{:S(2)}) %copy-start) | copy-done | bytes 262168
  1.0 0.7 %copy.41 = bf16[4,1,4,8,512]{4,2,3,0,1:T(4,128)(2,1)} copy(bf16[4,1,4,8,512]{4,3,2,1,0:T(8,128)(2,1)S(1)} %constant_dynamic-slice_fusion.2) | data formatting | bytes 262144
  1.7 6.3 %all-to-all-start = ((bf16[4,4,8,512]{3,1,2,0:T(4,128)(2,1)}), bf16[4,4,8,512]{3,1,2,0:T(4,128)(2,1)S(1)}, u32[]{:S(2)}, u32[]{:S(2)}) async-start(bf16[4,4,8,512]{3,1,2,0:T(4,128)(2,1)} %bitcast.58), calls=%async_computation | async-start | bytes 262144 | tf_op jit(solution)/shard_map/all_to_all | solution.py:65
  8.0 1.2 %dynamic_slice.21 = s32[1]{0:T(128)} dynamic-slice(s32[8]{0:T(128)} %param.8, s32[]{:T(128)S(6)} %select_n.52), dynamic_slice_sizes={1} | dynamic-slice | bytes 12 | tf_op jit(solution)/shard_map/dynamic_slice | solution.py:70
  9.9 1.0 %fusion.36 = f32[1,256]{1,0:T(1,128)S(1)} fusion(bf16[256,256]{1,0:T(8,128)(2,1)} %param.10, f32[1,128]{1,0:T(1,128)S(1)} %get-tuple-element.7, f32[1,128]{1,0:T(1,128)S(1)} %get-tuple-element.8), kind=kOutput, calls=%fused_computation.64 | convolution fusion | flops 786688 | bytes 133120 | tf_op jit(solution)/shard_map/dot_general | solution.py:72
  11.0 0.1 fusion.35
  11.1 3.0 %all-to-all-done = bf16[4,4,8,512]{3,1,2,0:T(4,128)(2,1)S(1)} async-done(((bf16[4,4,8,512]{3,1,2,0:T(4,128)(2,1)}), bf16[4,4,8,512]{3,1,2,0:T(4,128)(2,1)S(1)}, u32[]{:S(2)}, u32[]{:S(2)}) %all-to-all-start) | async-done | bytes 131104 | tf_op jit(solution)/shard_map/all_to_all | solution.py:65
  14.2 5.8 %all_gather.3 = bf16[1,16,16,512]{3,1,0,2:T(8,128)(2,1)S(1)} all-gather(bf16[1,16,8,512]{3,1,0,2:T(8,128)(2,1)S(1)} %copy.30), channel_id=1, replica_groups=mesh['groups'=2,'tile'=4,'chan'=2,'low'=2] {'chan'}, dimensions={2}, use_global_device_ids=true | all-gather | bytes 393216 | tf_op jit(solution)/shard_map/all_gather | solution.py:68
  20.1 0.2 copy.32
  20.3 0.1 slice.15
  20.4 1.1 %multiply_convert_fusion.1 = bf16[16,8,3,256]{3,1,2,0:T(8,128)(2,1)S(1)} fusion(bf16[3,3,512,256]{3,2,1,0:T(8,128)(2,1)S(1)} %copy-done.4, bf16[16,1,7,2,512]{4,2,3,0,1:T(8,128)(2,1)S(1)} %slice.15, bf16[16,1,8,3,512]{4,2,3,0,1:T(8,128)(2,1)S(1)} %copy.32, f32[256]{0:T(256)S(1)} %broadcast_add_fusion.1, pred[8,3]{0,1:T(4,128)(4,1)S(1)} %copy-done.5), kind=kOutput, calls=%fused_computation.23 | convolution fusion | flops 870875136 | bytes 3179544 | tf_op jit(solution)/shard_map/conv_general_dilated | solution.py:25
  21.5 1.1 %multiply_convert_fusion = bf16[16,8,3,256]{3,1,2,0:T(8,128)(2,1)S(1)} fusion(bf16[3,3,512,256]{3,2,1,0:T(8,128)(2,1)S(1)} %collective-permute-done, bf16[16,1,7,2,512]{4,2,3,0,1:T(8,128)(2,1)S(1)} %slice.15, bf16[16,1,8,3,512]{4,2,3,0,1:T(8,128)(2,1)S(1)} %copy.32, f32[256]{0:T(256)S(1)} %broadcast_add_fusion, pred[8,3]{0,1:T(4,128)(4,1)S(1)} %copy-done.5), kind=kOutput, calls=%fused_computation.22 | convolution fusion | flops 870875136 | bytes 3179544 | tf_op jit(solution)/shard_map/conv_general_dilated | solution.py:25
  22.7 0.1 copy.33
  22.8 0.2 copy.40
  23.0 0.1 collective-permute-start.2
  23.1 0.2 broadcast_compare_fusion
  23.3 1.3 %collective-permute-done.2 = bf16[1,16,16,512]{3,2,1,0:T(8,128)(2,1)S(1)} collective-permute-done((bf16[1,16,16,512]{3,2,1,0:T(8,128)(2,1)S(1)}, bf16[1,16,16,512]{3,2,1,0:T(8,128)(2,1)S(1)}, u32[]{:S(2)}, u32[]{:S(2)}) %collective-permute-start.2) | collective-permute-done | bytes 262176 | tf_op jit(solution)/shard_map/ppermute | solution.py:21
  24.6 0.1 pad_maximum_fusion
  24.8 0.3 convolution_convert_fusion
  25.1 0.5 %copy-done.1 = bf16[3,16,16,512]{3,2,1,0:T(8,128)(2,1)} copy-done((bf16[3,16,16,512]{3,2,1,0:T(8,128)(2,1)}, bf16[3,16,16,512]{3,2,1,0:T(8,128)(2,1)S(1)}, u32[]{:S(2)}) %copy-start.1) | copy-done | bytes 786456
  25.6 0.3 convolution_convert_fusion.1
  25.9 0.2 bitcast_select_fusion
  26.1 1.8 %convolution_multiply_fusion = f32[2,128,1024]{2,1,0:T(8,128)S(1)} fusion(bf16[2,1024,256]{2,1,0:T(8,128)(2,1)S(1)} %get-tuple-element.6, bf16[3,512,256]{2,1,0:T(8,128)(2,1)} %param.11, bf16[3,16,16,512]{3,2,1,0:T(8,128)(2,1)} %copy-done.1, s32[]{:T(128)S(6)} %select_n.55, s32[]{:T(128)S(6)} %select_n.57), kind=kOutput, calls=%fused_computation | convolution fusion | flops 201654272 | bytes 2621448 | tf_op jit(solution)/shard_map/bqc,bjc->bqj/dot_general | solution.py:107
  27.9 0.5 %reshape.170 = f32[2,128,4,256]{3,2,1,0:T(4,128)S(1)} reshape(f32[2,128,1024]{2,1,0:T(8,128)S(1)} %convolution_multiply_fusion) | data formatting | bytes 2097152 | tf_op jit(solution)/shard_map/reshape | solution.py:108
  28.4 0.3 reduce_max.9
  28.7 1.4 %exponential_reduce_fusion = f32[2,128,4]{2,1,0:T(8,128)} fusion(f32[2,128,4,256]{3,2,1,0:T(4,128)S(1)} %reshape.170, f32[2,128,4]{2,1,0:T(8,128)S(1)} %reduce_max.9), kind=kLoop, calls=%fused_computation.15 | loop fusion | flops 523264 | bytes 1056768 | tf_op jit(solution)/shard_map/reduce_sum | solution.py:111
  30.1 1.0 %copy.35 = f32[2,128,4]{1,2,0:T(4,128)S(1)} copy(f32[2,128,4]{2,1,0:T(8,128)} %exponential_reduce_fusion) | data formatting | bytes 8192 | tf_op jit(solution)/shard_map/reduce_sum | solution.py:111
  31.1 0.8 %copy.36 = f32[2,128,256]{2,1,0:T(8,128)} copy(f32[2,128,256]{1,2,0:T(8,128)S(1)} %bitcast.66) | data formatting | bytes 524288 | tf_op jit(solution)/shard_map/reshape | solution.py:114
  32.0 1.3 %sub.31 = f32[2,128,4,256]{3,2,1,0:T(4,128)} broadcast(f32[2,128,4]{2,1,0:T(8,128)S(1)} %reduce_max.9), dimensions={0,1,2} | broadcast | bytes 1052672 | tf_op jit(solution)/shard_map/sub | solution.py:110
  33.3 1.8 %sub.32 = f32[2,128,1024]{2,1,0:T(8,128)S(1)} reshape(f32[2,128,4,256]{3,2,1,0:T(4,128)} %sub.31) | data formatting | bytes 2097152 | tf_op jit(solution)/shard_map/sub | solution.py:110
  35.0 1.9 %fusion.4 = bf16[2,16,8,256]{3,2,1,0:T(8,128)(2,1)} fusion(f32[2,128,256]{2,1,0:T(8,128)} %copy.36, bf16[2,1024,256]{2,1,0:T(8,128)(2,1)S(1)} %get-tuple-element.5, f32[2,128,1024]{2,1,0:T(8,128)S(1)} %convolution_multiply_fusion, f32[2,128,1024]{2,1,0:T(8,128)S(1)} %sub.32), kind=kOutput, calls=%fused_computation.12 | convolution fusion | flops 134873088 | bytes 3538944 | tf_op jit(solution)/shard_map/bqj,bjc->bqc/dot_general | solution.py:113
  (28 shorter events, 0.4 us)
Async XLA Ops:
  0.0 1.0 %copy-start = (bf16[8,4,8,512]{3,2,1,0:T(8,128)(2,1)S(1)}, bf16[8,4,8,512]{3,2,1,0:T(8,128)(2,1)}, u32[]{:S(2)}) copy-start(bf16[8,4,8,512]{3,2,1,0:T(8,128)(2,1)} %param.6) | copy-start | bytes 786436
  0.0 14.1 %copy-start.3 = (bf16[2,16,8,512]{3,2,1,0:T(8,128)(2,1)S(1)}, bf16[2,16,8,512]{3,2,1,0:T(8,128)(2,1)}, u32[]{:S(2)}) copy-start(bf16[2,16,8,512]{3,2,1,0:T(8,128)(2,1)} %param.7) | copy-start | bytes 786436
  0.0 21.5 %collective-permute-start = (bf16[3,3,512,256]{3,2,1,0:T(8,128)(2,1)}, bf16[3,3,512,256]{3,2,1,0:T(8,128)(2,1)S(1)}, u32[]{:S(2)}, u32[]{:S(2)}) collective-permute-start(bf16[3,3,512,256]{3,2,1,0:T(8,128)(2,1)} %param.9), channel_id=1, source_target_pairs={{0,1},{1,0},{2,3},{3,2},{4,5},{5,4},{6,7},{7,6},{8,9},{9,8},{10,11... | collective-permute-start | bytes 7077896 | tf_op jit(solution)/shard_map/ppermute | solution.py:21
  1.7 12.4 %all-to-all-start = ((bf16[4,4,8,512]{3,1,2,0:T(4,128)(2,1)}), bf16[4,4,8,512]{3,1,2,0:T(4,128)(2,1)S(1)}, u32[]{:S(2)}, u32[]{:S(2)}) async-start(bf16[4,4,8,512]{3,1,2,0:T(4,128)(2,1)} %bitcast.58), calls=%async_computation | async-start | bytes 262144 | tf_op jit(solution)/shard_map/all_to_all | solution.py:65
  8.0 3.0 %collective-permute-start.1 = (bf16[256,256]{1,0:T(8,128)(2,1)}, bf16[256,256]{1,0:T(8,128)(2,1)S(1)}, u32[]{:S(2)}, u32[]{:S(2)}) collective-permute-start(bf16[256,256]{1,0:T(8,128)(2,1)} %param.10), channel_id=1, source_target_pairs={{0,1},{1,0},{2,3},{3,2},{4,5},{5,4},{6,7},{7,6},{8,9},{9,8},{10,11... | collective-permute-start | bytes 393224 | tf_op jit(solution)/shard_map/ppermute | solution.py:21
  14.2 6.2 %copy-start.4 = (bf16[3,3,512,256]{3,2,1,0:T(8,128)(2,1)S(1)}, bf16[3,3,512,256]{3,2,1,0:T(8,128)(2,1)}, u32[]{:S(2)}) copy-start(bf16[3,3,512,256]{3,2,1,0:T(8,128)(2,1)} %param.9) | copy-start | bytes 7077892
  14.2 6.2 %copy-start.5 = (pred[8,3]{0,1:T(4,128)(4,1)S(1)}, pred[8,3]{0,1:T(4,128)(4,1)}, u32[]{:S(2)}) copy-start(pred[8,3]{0,1:T(4,128)(4,1)} %constant.98) | copy-start | bytes 76
  23.0 1.6 %collective-permute-start.2 = (bf16[1,16,16,512]{3,2,1,0:T(8,128)(2,1)S(1)}, bf16[1,16,16,512]{3,2,1,0:T(8,128)(2,1)S(1)}, u32[]{:S(2)}, u32[]{:S(2)}) collective-permute-start(bf16[1,16,16,512]{3,2,1,0:T(8,128)(2,1)S(1)} %bitcast.63), channel_id=1, source_target_pairs={{0,1},{1,0},{2,3},{3,2},{4,5},{5,4},{6,7},{7,6},{8,9},{9,8},{10,11... | collective-permute-start | bytes 786440 | tf_op jit(solution)/shard_map/ppermute | solution.py:21
  23.1 1.7 %copy-start.2 = (bf16[3,512,256]{2,1,0:T(8,128)(2,1)S(1)}, bf16[3,512,256]{2,1,0:T(8,128)(2,1)}, u32[]{:S(2)}) copy-start(bf16[3,512,256]{2,1,0:T(8,128)(2,1)} %param.11) | copy-start | bytes 2359300
  24.7 0.9 %copy-start.1 = (bf16[3,16,16,512]{3,2,1,0:T(8,128)(2,1)}, bf16[3,16,16,512]{3,2,1,0:T(8,128)(2,1)S(1)}, u32[]{:S(2)}) copy-start(bf16[3,16,16,512]{3,2,1,0:T(8,128)(2,1)S(1)} %pad_maximum_fusion) | copy-start | bytes 2359300

commit v6 on v4

--- a/solution.py
+++ b/solution.py
@@ -59,13 +59,30 @@
     conv_other, time_other = swap((conv_weight, time_weight), "low")
 
     start = l_idx * per_core
-    outgoing = lax.dynamic_slice_in_dim(
+    chans = lax.axis_size("chan")
+    blocks = lax.dynamic_slice_in_dim(
         latent_map.reshape(tiles, per_tile, row_local, col_local, width), start, per_core, 1
-    ).reshape(tiles * per_core, row_local, col_local, width)
-    arrived = lax.all_to_all(outgoing, "tile", split_axis=0, concat_axis=1, tiled=True)
+    )
     inner_own = lax.dynamic_slice_in_dim(inner_map, start, per_core, 0)
-    joined = (arrived.astype(jnp.float32) + inner_own.astype(jnp.float32)).astype(jnp.bfloat16)
-    whole = lax.all_gather(joined, "chan", axis=2, tiled=True)
+    if tiles * chans <= 8 and chans == 2:
+        outgoing = jnp.broadcast_to(blocks[:, None], (tiles, chans) + blocks.shape[1:])
+        arrived = lax.all_to_all(
+            outgoing.reshape((tiles * chans,) + blocks.shape[1:]), ("tile", "chan"), 0, 0, tiled=True
+        )
+        arrived = arrived.reshape(tiles, chans, per_core, row_local, col_local, width)
+        latent_whole = arrived.transpose(2, 0, 3, 1, 4, 5).reshape(
+            per_core, tiles * row_local, chans * col_local, width
+        )
+        partner = swap(inner_own, "chan")
+        inner_whole = lax.dynamic_slice_in_dim(
+            jnp.concatenate([inner_own, partner, inner_own], axis=2), c_idx * col_local, 2 * col_local, 2
+        )
+        whole = (latent_whole.astype(jnp.float32) + inner_whole.astype(jnp.float32)).astype(jnp.bfloat16)
+    else:
+        outgoing = blocks.reshape(tiles * per_core, row_local, col_local, width)
+        arrived = lax.all_to_all(outgoing, "tile", split_axis=0, concat_axis=1, tiled=True)
+        joined = (arrived.astype(jnp.float32) + inner_own.astype(jnp.float32)).astype(jnp.bfloat16)
+        whole = lax.all_gather(joined, "chan", axis=2, tiled=True)
 
     stamps = lax.dynamic_slice_in_dim(timestep, t_idx * per_tile + start, per_core, 0)
     embedded = time_embedding(stamps)

time: 28.4 us -> 29 us (1.021)
  blocking collectives: 5.78 us -> 0 us
  waiting for transfers between devices: 4.32 us -> 9.03 us
  starting transfers between devices: 6.92 us -> 8.17 us
  local copies, waits for them, and re-layouts: 4.41 us -> 5.45 us
  matrix products: 5.18 us -> 4.29 us
    all_gather x1 -> x0, blocking collectives: 5.78 us -> none  [per_device(): whole = lax.all_gather(joined, 'chan', axis=2, tiled=True)]
    all_to_all x1, waiting for transfers between devices: 2.76 us -> 7.51 us  [per_device(): lax.all_to_all(outgoing.reshape((tiles * chans,) + blocks.shape[1:]), ('t...]
    ppermute x3 -> x4, starting transfers between devices: 0.6 us -> 3.3 us  [swap(): return lax.ppermute(tree, axis, [(0, 1), (1, 0)])]
    all_to_all x1, starting transfers between devices: 6.32 us -> 4.88 us  [per_device(): lax.all_to_all(outgoing.reshape((tiles * chans,) + blocks.shape[1:]), ('t...]
    dynamic_slice x1, local copies, waits for them, and re-layouts: 0.01 us -> 0.91 us  [per_device(): inner_own = lax.dynamic_slice_in_dim(inner_map, start, per_core, 0)]
    dot_general x1, matrix products: 1.04 us -> 0.14 us  [per_device(): jnp.dot(embedded, time_weight.astype(jnp.float32), precision=lax.Precisio...]
    dynamic_slice x1, local copies, waits for them, and re-layouts: 1.32 us -> 0.59 us  [per_device(): lax.dynamic_slice_in_dim(timestep, t_idx * per_tile + start, per_core, 0)]
    broadcast_in_dim x0 -> x2, local copies, waits for them, and re-layouts: none -> 0.73 us  [per_device(): jnp.broadcast_to(blocks[:, None], (tiles, chans) + blocks.shape[1:])]
  transfers between devices with their start and end apart: 4 -> 5, of which waited for: 2 -> 2; matrix products, arithmetic and copies ran while one was open for 17% -> 15% of each run, Pallas kernels for 0% -> 0%
where the time goes in v6:
time: 29 us; the launch traced here: 28.7 us
  waiting for transfers between devices  9.03 us (31%)
  starting transfers between devices  8.17 us (28%)
  local copies, waits for them, and re-layouts  5.45 us (19%)
  matrix products  4.29 us (15%)
  between operations  0.95 us (3%)
  other arithmetic  0.79 us (3%)
    all_to_all x1, waiting for transfers between devices, per_device(): lax.all_to_all(outgoing.reshape((tiles * chans,) + blocks.shape[1:]), ('t...  7.51 us
    all_to_all x1, starting transfers between devices, per_device(): lax.all_to_all(outgoing.reshape((tiles * chans,) + blocks.shape[1:]), ('t...  4.88 us
    ppermute x4, starting transfers between devices, swap(): return lax.ppermute(tree, axis, [(0, 1), (1, 0)])  3.3 us
    conv_general_dilated x2, matrix products, convolve(): lax.conv_general_dilated(joined, weight, window_strides=(1, 1), padding=(...  2.25 us
    ppermute x4, waiting for transfers between devices, swap(): return lax.ppermute(tree, axis, [(0, 1), (1, 0)])  1.53 us
    unnamed x13, local copies, waits for them, and re-layouts  1.33 us
    dot_general x3, matrix products, project(): jnp.dot(part, attend_weight[which], preferred_element_type=jnp.float32)  0.94 us
    dynamic_slice x1, local copies, waits for them, and re-layouts, per_device(): inner_own = lax.dynamic_slice_in_dim(inner_map, start, per_core, 0)  0.91 us
  transfers between devices with their start and end apart: 5, of which 2 were waited for; matrix products, arithmetic and copies ran while one was open for 15% of the time, Pallas kernels for 0%

profile of v6, /device:TPU:0, one launch (start us, length us, event | category | flops | bytes accessed | tf_op | source)
XLA Modules:
  0.0 28.7 jit_solution(16822601567323438145)
XLA Ops:
  0.0 0.5 %collective-permute-start.1 = (bf16[3,3,512,256]{3,2,1,0:T(8,128)(2,1)}, bf16[3,3,512,256]{3,2,1,0:T(8,128)(2,1)S(1)}, u32[]{:S(2)}, u32[]{:S(2)}) collective-permute-start(bf16[3,3,512,256]{3,2,1,0:T(8,128)(2,1)} %param.9), channel_id=1, source_target_pairs={{0,1},{1,0},{2,3},{3,2},{4,5},{5,4},{6,7},{7,6},{8,9},{9,8},{10,11... | collective-permute-start | bytes 7077896 | tf_op jit(solution)/shard_map/ppermute | solution.py:21
  0.5 0.9 %constant_dynamic-slice_fusion.2 = bf16[1,16,8,512]{3,2,1,0:T(8,128)(2,1)S(1)} fusion(bf16[2,16,8,512]{3,2,1,0:T(8,128)(2,1)} %param.7, s32[]{:T(128)S(6)} %select_n.23), kind=kLoop, calls=%fused_computation.44 | loop fusion | bytes 262148 | tf_op jit(solution)/shard_map/dynamic_slice | solution.py:66
  1.4 2.6 %collective-permute-start = (bf16[1,16,8,512]{3,2,1,0:T(8,128)(2,1)S(1)}, bf16[1,16,8,512]{3,2,1,0:T(8,128)(2,1)S(1)}, u32[]{:S(2)}, u32[]{:S(2)}) collective-permute-start(bf16[1,16,8,512]{3,2,1,0:T(8,128)(2,1)S(1)} %constant_dynamic-slice_fusion.2), channel_id=1, source_target_pairs={{0,2},{2,0},{1,3},{3,1},{4,6},{6,4},{5,7},{7,5},{8,10},{10,8},{9,1... | collective-permute-start | bytes 393224 | tf_op jit(solution)/shard_map/ppermute | solution.py:21
  4.1 0.7 %broadcast_in_dim.7 = bf16[4,2,4,8,512]{4,3,2,1,0:T(8,128)(2,1)} broadcast(bf16[4,4,8,512]{3,2,1,0:T(8,128)(2,1)S(1)} %dynamic-slice_bitcast_fusion), dimensions={0,2,3,4} | broadcast | bytes 393216 | tf_op jit(solution)/shard_map/broadcast_in_dim | solution.py:68
  4.8 4.9 %all-to-all-start = ((bf16[8,1,4,8,512]{4,3,2,1,0:T(8,128)(2,1)}), bf16[8,1,4,8,512]{4,3,2,1,0:T(8,128)(2,1)S(1)}, u32[]{:S(2)}, u32[]{:S(2)}) async-start(bf16[8,1,4,8,512]{4,3,2,1,0:T(8,128)(2,1)} %bitcast.2), calls=%async_computation | async-start | bytes 524288 | tf_op jit(solution)/shard_map/all_to_all | solution.py:69
  9.7 0.1 collective-permute-start.2
  9.8 0.6 %dynamic_slice.25 = s32[1]{0:T(128)} dynamic-slice(s32[8]{0:T(128)S(1)} %copy-done.4, s32[]{:T(128)S(6)} %select_n.25), dynamic_slice_sizes={1} | dynamic-slice | bytes 12 | tf_op jit(solution)/shard_map/dynamic_slice | solution.py:87
  11.0 0.1 fusion.25
  11.1 0.1 fusion.34
  11.3 0.1 fusion.33
  11.4 7.5 %all-to-all-done = bf16[8,1,4,8,512]{4,3,2,1,0:T(8,128)(2,1)S(1)} async-done(((bf16[8,1,4,8,512]{4,3,2,1,0:T(8,128)(2,1)}), bf16[8,1,4,8,512]{4,3,2,1,0:T(8,128)(2,1)S(1)}, u32[]{:S(2)}, u32[]{:S(2)}) %all-to-all-start) | async-done | bytes 262176 | tf_op jit(solution)/shard_map/all_to_all | solution.py:69
  19.1 0.2 fusion.23
  19.2 0.2 copy.42
  19.4 0.2 copy.33
  19.7 0.1 slice.15
  19.7 1.2 %copy-done.3 = bf16[3,3,512,256]{3,2,1,0:T(8,128)(2,1)S(1)} copy-done((bf16[3,3,512,256]{3,2,1,0:T(8,128)(2,1)S(1)}, bf16[3,3,512,256]{3,2,1,0:T(8,128)(2,1)}, u32[]{:S(2)}) %copy-start.3) | copy-done | bytes 2359320
  20.9 1.1 %multiply_convert_fusion.1 = bf16[16,8,3,256]{3,1,2,0:T(8,128)(2,1)S(1)} fusion(bf16[3,3,512,256]{3,2,1,0:T(8,128)(2,1)S(1)} %copy-done.3, bf16[16,1,7,2,512]{4,2,3,0,1:T(8,128)(2,1)S(1)} %slice.15, bf16[16,1,8,3,512]{4,2,3,0,1:T(8,128)(2,1)S(1)} %copy.33, f32[256]{0:T(256)S(1)} %broadcast_add_fusion.1, pred[8,3]{0,1:T(4,128)(4,1)S(1)} %copy-done.5), kind=kOutput, calls=%fused_computation.27 | convolution fusion | flops 870875136 | bytes 3179544 | tf_op jit(solution)/shard_map/conv_general_dilated | solution.py:25
  22.0 1.1 %multiply_convert_fusion = bf16[16,8,3,256]{3,1,2,0:T(8,128)(2,1)S(1)} fusion(bf16[3,3,512,256]{3,2,1,0:T(8,128)(2,1)S(1)} %collective-permute-done.1, bf16[16,1,7,2,512]{4,2,3,0,1:T(8,128)(2,1)S(1)} %slice.15, bf16[16,1,8,3,512]{4,2,3,0,1:T(8,128)(2,1)S(1)} %copy.33, f32[256]{0:T(256)S(1)} %broadcast_add_fusion, pred[8,3]{0,1:T(4,128)(4,1)S(1)} %copy-done.5), kind=kOutput, calls=%fused_computation.26 | convolution fusion | flops 870875136 | bytes 3179544 | tf_op jit(solution)/shard_map/conv_general_dilated | solution.py:25
  23.2 0.1 copy.34
  23.4 0.2 copy.44
  23.6 0.1 collective-permute-start.3
  23.6 1.5 %collective-permute-done.3 = bf16[1,16,16,512]{3,2,1,0:T(8,128)(2,1)S(1)} collective-permute-done((bf16[1,16,16,512]{3,2,1,0:T(8,128)(2,1)S(1)}, bf16[1,16,16,512]{3,2,1,0:T(8,128)(2,1)S(1)}, u32[]{:S(2)}, u32[]{:S(2)}) %collective-permute-start.3) | collective-permute-done | bytes 262176 | tf_op jit(solution)/shard_map/ppermute | solution.py:21
  25.2 0.1 pad_maximum_fusion
  25.3 0.3 %convolution_convert_fusion = bf16[2,256,256]{1,2,0:T(8,128)(2,1)S(1)} fusion(bf16[2,256,512]{2,1,0:T(8,128)(2,1)S(1)} %bitcast.69, bf16[3,512,256]{2,1,0:T(8,128)(2,1)S(1)} %copy-done.1), kind=kOutput, calls=%fused_computation.3 | convolution fusion | flops 134348800 | bytes 1048576 | tf_op jit(solution)/shard_map/dot_general | solution.py:109
  25.7 0.3 %convolution_convert_fusion.1 = bf16[2,256,256]{1,2,0:T(8,128)(2,1)S(1)} fusion(bf16[2,256,512]{2,1,0:T(8,128)(2,1)S(1)} %bitcast.70, bf16[3,512,256]{2,1,0:T(8,128)(2,1)S(1)} %copy-done.1), kind=kOutput, calls=%fused_computation.4 | convolution fusion | flops 134348800 | bytes 1048576 | tf_op jit(solution)/shard_map/dot_general | solution.py:109
  26.0 0.2 convolution_convert_fusion.2
  26.3 0.1 copy.37
  26.4 0.4 %fusion.35 = (f32[2,4,128]{2,1,0:T(4,128)S(1)}, f32[2,4,128,256]{3,2,1,0:T(8,128)S(1)}) fusion(bf16[2,128,4,64]{1,3,2,0:T(8,128)(2,1)S(1)} %bitcast.78, bf16[2,256,4,64]{1,3,2,0:T(8,128)(2,1)S(1)} %bitcast.77), kind=kOutput, calls=%fused_computation.59 | convolution fusion | flops 34077696 | bytes 1445888 | tf_op jit(solution)/shard_map/bqhd,bkhd->bhqk/dot_general | solution.py:120
  26.8 0.4 %fusion.5 = f32[2,4,128]{2,1,0:T(4,128)S(1)} fusion(f32[2,4,128,256]{3,2,1,0:T(8,128)S(1)} %get-tuple-element.6, f32[2,4,128]{2,1,0:T(4,128)S(1)} %get-tuple-element.5), kind=kLoop, calls=%fused_computation.14 | loop fusion | flops 523264 | bytes 1056768 | tf_op jit(solution)/shard_map/reduce_sum | solution.py:124
  27.2 0.4 %fusion.4 = bf16[2,128,4,64]{1,3,2,0:T(8,128)(2,1)S(1)} fusion(bf16[2,256,4,64]{1,3,2,0:T(8,128)(2,1)S(1)} %bitcast.79, f32[2,4,128,256]{3,2,1,0:T(8,128)S(1)} %get-tuple-element.6, f32[2,4,128]{2,1,0:T(4,128)S(1)} %get-tuple-element.5, f32[2,128,4]{1,2,0:T(4,128)S(1)} %bitcast.80), kind=kOutput, calls=%fused_computation.11 | convolution fusion | flops 34209792 | bytes 1449984 | tf_op jit(solution)/shard_map/bhqk,bkhd->bqhd/dot_general | solution.py:125
  27.6 0.2 copy.39
  27.8 0.9 %reshape.97 = bf16[2,16,8,256]{3,2,1,0:T(8,128)(2,1)} reshape(bf16[2,128,4,64]{3,2,1,0:T(4,128)(2,1)S(1)} %copy.39) | data formatting | bytes 262144 | tf_op jit(solution)/shard_map/reshape | solution.py:129
  (24 shorter events, 0.3 us)
Async XLA Ops:
  0.0 4.1 %copy-start = (bf16[8,4,8,512]{3,2,1,0:T(8,128)(2,1)S(1)}, bf16[8,4,8,512]{3,2,1,0:T(8,128)(2,1)}, u32[]{:S(2)}) copy-start(bf16[8,4,8,512]{3,2,1,0:T(8,128)(2,1)} %param.6) | copy-start | bytes 786436
  0.0 9.7 %copy-start.2 = (bf16[256,256]{1,0:T(8,128)(2,1)S(1)}, bf16[256,256]{1,0:T(8,128)(2,1)}, u32[]{:S(2)}) copy-start(bf16[256,256]{1,0:T(8,128)(2,1)} %param.10) | copy-start | bytes 393220
  0.0 9.8 %copy-start.4 = (s32[8]{0:T(128)S(1)}, s32[8]{0:T(128)}, u32[]{:S(2)}) copy-start(s32[8]{0:T(128)} %param.8) | copy-start | bytes 100
  0.0 22.0 %collective-permute-start.1 = (bf16[3,3,512,256]{3,2,1,0:T(8,128)(2,1)}, bf16[3,3,512,256]{3,2,1,0:T(8,128)(2,1)S(1)}, u32[]{:S(2)}, u32[]{:S(2)}) collective-permute-start(bf16[3,3,512,256]{3,2,1,0:T(8,128)(2,1)} %param.9), channel_id=1, source_target_pairs={{0,1},{1,0},{2,3},{3,2},{4,5},{5,4},{6,7},{7,6},{8,9},{9,8},{10,11... | collective-permute-start | bytes 7077896 | tf_op jit(solution)/shard_map/ppermute | solution.py:21
  1.4 17.6 %collective-permute-start = (bf16[1,16,8,512]{3,2,1,0:T(8,128)(2,1)S(1)}, bf16[1,16,8,512]{3,2,1,0:T(8,128)(2,1)S(1)}, u32[]{:S(2)}, u32[]{:S(2)}) collective-permute-start(bf16[1,16,8,512]{3,2,1,0:T(8,128)(2,1)S(1)} %constant_dynamic-slice_fusion.2), channel_id=1, source_target_pairs={{0,2},{2,0},{1,3},{3,1},{4,6},{6,4},{5,7},{7,5},{8,10},{10,8},{9,1... | collective-permute-start | bytes 393224 | tf_op jit(solution)/shard_map/ppermute | solution.py:21
  4.8 14.1 %all-to-all-start = ((bf16[8,1,4,8,512]{4,3,2,1,0:T(8,128)(2,1)}), bf16[8,1,4,8,512]{4,3,2,1,0:T(8,128)(2,1)S(1)}, u32[]{:S(2)}, u32[]{:S(2)}) async-start(bf16[8,1,4,8,512]{4,3,2,1,0:T(8,128)(2,1)} %bitcast.2), calls=%async_computation | async-start | bytes 524288 | tf_op jit(solution)/shard_map/all_to_all | solution.py:69
  9.7 1.5 %collective-permute-start.2 = (bf16[256,256]{1,0:T(8,128)(2,1)S(1)}, bf16[256,256]{1,0:T(8,128)(2,1)S(1)}, u32[]{:S(2)}, u32[]{:S(2)}) collective-permute-start(bf16[256,256]{1,0:T(8,128)(2,1)S(1)} %copy-done.2), channel_id=1, source_target_pairs={{0,1},{1,0},{2,3},{3,2},{4,5},{5,4},{6,7},{7,6},{8,9},{9,8},{10,11... | collective-permute-start | bytes 393224 | tf_op jit(solution)/shard_map/ppermute | solution.py:21
  19.2 1.7 %copy-start.3 = (bf16[3,3,512,256]{3,2,1,0:T(8,128)(2,1)S(1)}, bf16[3,3,512,256]{3,2,1,0:T(8,128)(2,1)}, u32[]{:S(2)}) copy-start(bf16[3,3,512,256]{3,2,1,0:T(8,128)(2,1)} %param.9) | copy-start | bytes 7077892
  19.2 1.7 %copy-start.5 = (pred[8,3]{0,1:T(4,128)(4,1)S(1)}, pred[8,3]{0,1:T(4,128)(4,1)}, u32[]{:S(2)}) copy-start(pred[8,3]{0,1:T(4,128)(4,1)} %constant.69) | copy-start | bytes 76
  23.5 1.8 %copy-start.1 = (bf16[3,512,256]{2,1,0:T(8,128)(2,1)S(1)}, bf16[3,512,256]{2,1,0:T(8,128)(2,1)}, u32[]{:S(2)}) copy-start(bf16[3,512,256]{2,1,0:T(8,128)(2,1)} %param.11) | copy-start | bytes 2359300
  23.6 1.6 %collective-permute-start.3 = (bf16[1,16,16,512]{3,2,1,0:T(8,128)(2,1)S(1)}, bf16[1,16,16,512]{3,2,1,0:T(8,128)(2,1)S(1)}, u32[]{:S(2)}, u32[]{:S(2)}) collective-permute-start(bf16[1,16,16,512]{3,2,1,0:T(8,128)(2,1)S(1)} %bitcast.75), channel_id=1, source_target_pairs={{0,1},{1,0},{2,3},{3,2},{4,5},{5,4},{6,7},{7,6},{8,9},{9,8},{10,11... | collective-permute-start | bytes 786440 | tf_op jit(solution)/shard_map/ppermute | solution.py:21

commit v7 on v4

--- a/solution.py
+++ b/solution.py
@@ -106,9 +106,11 @@
         weights = jnp.exp(scores - row_peak)
         totals = jnp.sum(weights, axis=3)
         summed = jnp.einsum(
-            "bhqk,bkhd->bqhd", weights.astype(jnp.bfloat16), v4, preferred_element_type=jnp.float32
+            "bhqk,bkc->bhqc", weights.astype(jnp.bfloat16), values, preferred_element_type=jnp.float32
         )
-        out = (summed / totals.transpose(0, 2, 1)[..., None]).astype(jnp.bfloat16)
+        lane_head = jnp.arange(heads_local * HEAD)[None, :] // HEAD == jnp.arange(heads_local)[:, None]
+        scaled = summed / totals[..., None]
+        out = jnp.sum(jnp.where(lane_head[None, :, None, :], scaled, 0.0), axis=1).astype(jnp.bfloat16)
         return out.reshape(per_tile, rows_total, col_local, heads_local * HEAD)
 
     def by_head(x):

time: 28.4 us -> 29.2 us (1.028)
  matrix products: 5.18 us -> 7.35 us
  local copies, waits for them, and re-layouts: 4.41 us -> 3.29 us
  other arithmetic: 0.62 us -> 0.24 us
    dot_general x1, matrix products: 0.39 us -> 1.69 us  [per_device(): jnp.einsum('bhqk,bkc->bhqc', weights.astype(jnp.bfloat16), values, prefer...]
    div x0 -> x1, matrix products: none -> 1.21 us  [per_device(): scaled = summed / totals[..., None]]
    reshape x1 -> x0, local copies, waits for them, and re-layouts: 0.87 us -> none  [per_device(): return out.reshape(per_tile, rows_total, col_local, heads_local * HEAD)]
    reduce_sum x1 -> x0, other arithmetic: 0.39 us -> none  [per_device(): totals = jnp.sum(weights, axis=3)]
    dot_general x3 -> x2, matrix products: 0.94 us -> 0.59 us  [project(): jnp.dot(part, attend_weight[which], preferred_element_type=jnp.float32)]
where the time goes in v7:
time: 29.2 us; the launch traced here: 28.9 us
  matrix products  7.35 us (25%)
  starting transfers between devices  6.92 us (24%)
  blocking collectives  5.78 us (20%)
  waiting for transfers between devices  4.42 us (15%)
  local copies, waits for them, and re-layouts  3.29 us (11%)
  between operations  0.85 us (3%)
    all_to_all x1, starting transfers between devices, per_device(): lax.all_to_all(outgoing, 'tile', split_axis=0, concat_axis=1, tiled=True)  6.32 us
    all_gather x1, blocking collectives, per_device(): whole = lax.all_gather(joined, 'chan', axis=2, tiled=True)  5.78 us
    all_to_all x1, waiting for transfers between devices, per_device(): lax.all_to_all(outgoing, 'tile', split_axis=0, concat_axis=1, tiled=True)  2.89 us
    conv_general_dilated x2, matrix products, convolve(): lax.conv_general_dilated(joined, weight, window_strides=(1, 1), padding=(...  2.25 us
    dot_general x1, matrix products, per_device(): jnp.einsum('bhqk,bkc->bhqc', weights.astype(jnp.bfloat16), values, prefer...  1.69 us
    ppermute x3, waiting for transfers between devices, swap(): return lax.ppermute(tree, axis, [(0, 1), (1, 0)])  1.53 us
    dynamic_slice x1, local copies, waits for them, and re-layouts, per_device(): lax.dynamic_slice_in_dim(timestep, t_idx * per_tile + start, per_core, 0)  1.27 us
    div x1, matrix products, per_device(): scaled = summed / totals[..., None]  1.21 us
  transfers between devices with their start and end apart: 4, of which 2 were waited for; matrix products, arithmetic and copies ran while one was open for 17% of the time, Pallas kernels for 0%

profile of v7, /device:TPU:0, one launch (start us, length us, event | category | flops | bytes accessed | tf_op | source)
XLA Modules:
  0.0 28.9 jit_solution(11733059109082163753)
XLA Ops:
  0.0 0.0 copy-start
  0.0 0.5 %collective-permute-start = (bf16[3,3,512,256]{3,2,1,0:T(8,128)(2,1)}, bf16[3,3,512,256]{3,2,1,0:T(8,128)(2,1)S(1)}, u32[]{:S(2)}, u32[]{:S(2)}) collective-permute-start(bf16[3,3,512,256]{3,2,1,0:T(8,128)(2,1)} %param.9), channel_id=1, source_target_pairs={{0,1},{1,0},{2,3},{3,2},{4,5},{5,4},{6,7},{7,6},{8,9},{9,8},{10,11... | collective-permute-start | bytes 7077896 | tf_op jit(solution)/shard_map/ppermute | solution.py:21
  0.5 0.1 collective-permute-start.1
  0.5 0.4 %copy-done = bf16[8,4,8,512]{3,2,1,0:T(8,128)(2,1)S(1)} copy-done((bf16[8,4,8,512]{3,2,1,0:T(8,128)(2,1)S(1)}, bf16[8,4,8,512]{3,2,1,0:T(8,128)(2,1)}, u32[]{:S(2)}) %copy-start) | copy-done | bytes 262168
  1.0 0.7 %copy.47 = bf16[4,1,4,8,512]{4,2,3,0,1:T(4,128)(2,1)} copy(bf16[4,1,4,8,512]{4,3,2,1,0:T(8,128)(2,1)S(1)} %constant_dynamic-slice_fusion.2) | data formatting | bytes 262144
  1.7 6.3 %all-to-all-start = ((bf16[4,4,8,512]{3,1,2,0:T(4,128)(2,1)}), bf16[4,4,8,512]{3,1,2,0:T(4,128)(2,1)S(1)}, u32[]{:S(2)}, u32[]{:S(2)}) async-start(bf16[4,4,8,512]{3,1,2,0:T(4,128)(2,1)} %bitcast.64), calls=%async_computation | async-start | bytes 262144 | tf_op jit(solution)/shard_map/all_to_all | solution.py:65
  8.0 1.3 %dynamic_slice.21 = s32[1]{0:T(128)} dynamic-slice(s32[8]{0:T(128)} %param.8, s32[]{:T(128)S(6)} %select_n.36), dynamic_slice_sizes={1} | dynamic-slice | bytes 12 | tf_op jit(solution)/shard_map/dynamic_slice | solution.py:70
  9.9 0.1 fusion.29
  9.9 1.0 %fusion.39 = f32[1,256]{1,0:T(1,128)S(1)} fusion(bf16[256,256]{1,0:T(8,128)(2,1)} %param.10, f32[1,128]{1,0:T(1,128)S(1)} %get-tuple-element.7, f32[1,128]{1,0:T(1,128)S(1)} %get-tuple-element.8), kind=kOutput, calls=%fused_computation.62 | convolution fusion | flops 786688 | bytes 133120 | tf_op jit(solution)/shard_map/dot_general | solution.py:72
  11.0 0.0 collective-permute-done.1
  11.0 0.1 fusion.38
  11.2 2.9 %all-to-all-done = bf16[4,4,8,512]{3,1,2,0:T(4,128)(2,1)S(1)} async-done(((bf16[4,4,8,512]{3,1,2,0:T(4,128)(2,1)}), bf16[4,4,8,512]{3,1,2,0:T(4,128)(2,1)S(1)}, u32[]{:S(2)}, u32[]{:S(2)}) %all-to-all-start) | async-done | bytes 131104 | tf_op jit(solution)/shard_map/all_to_all | solution.py:65
  14.2 0.0 copy-start.3
  14.2 0.0 copy-start.4
  14.2 5.8 %all_gather.3 = bf16[1,16,16,512]{3,1,0,2:T(8,128)(2,1)S(1)} all-gather(bf16[1,16,8,512]{3,1,0,2:T(8,128)(2,1)S(1)} %copy.34), channel_id=1, replica_groups=mesh['groups'=2,'tile'=4,'chan'=2,'low'=2] {'chan'}, dimensions={2}, use_global_device_ids=true | all-gather | bytes 393216 | tf_op jit(solution)/shard_map/all_gather | solution.py:68
  20.1 0.2 copy.36
  20.3 0.1 slice.15
  20.4 1.1 %multiply_convert_fusion.1 = bf16[16,8,3,256]{3,1,2,0:T(8,128)(2,1)S(1)} fusion(bf16[3,3,512,256]{3,2,1,0:T(8,128)(2,1)S(1)} %copy-done.3, bf16[16,1,7,2,512]{4,2,3,0,1:T(8,128)(2,1)S(1)} %slice.15, bf16[16,1,8,3,512]{4,2,3,0,1:T(8,128)(2,1)S(1)} %copy.36, f32[256]{0:T(256)S(1)} %broadcast_add_fusion.1, pred[8,3]{0,1:T(4,128)(4,1)S(1)} %copy-done.4), kind=kOutput, calls=%fused_computation.25 | convolution fusion | flops 870875136 | bytes 3179544 | tf_op jit(solution)/shard_map/conv_general_dilated | solution.py:25
  21.5 0.0 collective-permute-done
  21.5 1.1 %multiply_convert_fusion = bf16[16,8,3,256]{3,1,2,0:T(8,128)(2,1)S(1)} fusion(bf16[3,3,512,256]{3,2,1,0:T(8,128)(2,1)S(1)} %collective-permute-done, bf16[16,1,7,2,512]{4,2,3,0,1:T(8,128)(2,1)S(1)} %slice.15, bf16[16,1,8,3,512]{4,2,3,0,1:T(8,128)(2,1)S(1)} %copy.36, f32[256]{0:T(256)S(1)} %broadcast_add_fusion, pred[8,3]{0,1:T(4,128)(4,1)S(1)} %copy-done.4), kind=kOutput, calls=%fused_computation.24 | convolution fusion | flops 870875136 | bytes 3179544 | tf_op jit(solution)/shard_map/conv_general_dilated | solution.py:25
  22.7 0.1 copy.37
  22.9 0.2 copy.46
  23.0 0.0 copy-start.1
  23.0 0.1 collective-permute-start.2
  23.2 1.5 %collective-permute-done.2 = bf16[1,16,16,512]{3,2,1,0:T(8,128)(2,1)S(1)} collective-permute-done((bf16[1,16,16,512]{3,2,1,0:T(8,128)(2,1)S(1)}, bf16[1,16,16,512]{3,2,1,0:T(8,128)(2,1)S(1)}, u32[]{:S(2)}, u32[]{:S(2)}) %collective-permute-start.2) | collective-permute-done | bytes 262176 | tf_op jit(solution)/shard_map/ppermute | solution.py:21
  24.6 0.1 pad_maximum_fusion
  24.8 0.3 %convolution_convert_fusion.1 = bf16[2,256,256]{1,2,0:T(8,128)(2,1)S(1)} fusion(bf16[2,256,512]{2,1,0:T(8,128)(2,1)S(1)} %bitcast.67, bf16[3,512,256]{2,1,0:T(8,128)(2,1)S(1)} %copy-done.1), kind=kOutput, calls=%fused_computation.7 | convolution fusion | flops 134348800 | bytes 1048576 | tf_op jit(solution)/shard_map/dot_general | solution.py:92
  25.1 0.2 convolution_convert_fusion.2
  25.4 0.1 copy.39
  25.5 0.4 %fusion.40 = (f32[2,4,128]{2,1,0:T(4,128)S(1)}, f32[2,4,128,256]{3,2,1,0:T(8,128)S(1)}) fusion(bf16[2,128,4,64]{1,3,2,0:T(8,128)(2,1)S(1)} %bitcast.77, bf16[2,256,4,64]{1,3,2,0:T(8,128)(2,1)S(1)} %bitcast.74), kind=kOutput, calls=%fused_computation.63 | convolution fusion | flops 34077696 | bytes 1445888 | tf_op jit(solution)/shard_map/bqhd,bkhd->bhqk/dot_general | solution.py:103
  25.9 1.7 %fusion.9 = f32[2,4,128,256]{3,2,1,0:T(8,128)S(1)} fusion(bf16[2,256,512]{2,1,0:T(8,128)(2,1)S(1)} %bitcast.68, f32[2,4,128,256]{3,2,1,0:T(8,128)S(1)} %get-tuple-element.6, f32[2,4,128]{2,1,0:T(4,128)S(1)} %get-tuple-element.5, bf16[3,512,256]{2,1,0:T(8,128)(2,1)} %param.11), kind=kOutput, calls=%fused_computation.18 | convolution fusion | flops 269090816 | bytes 2887680 | tf_op jit(solution)/shard_map/bhqk,bkc->bhqc/dot_general | solution.py:108
  27.6 1.2 %fusion.41 = bf16[2,128,256]{2,1,0:T(8,128)(2,1)} fusion(f32[2,4,128,256]{3,2,1,0:T(8,128)S(1)} %fusion.9, f32[2,4,128]{2,1,0:T(4,128)S(1)} %get-tuple-element.5, bf16[2,128,4,64]{1,3,2,0:T(8,128)(2,1)S(1)} %bitcast.78, bf16[2,256,4,64]{1,3,2,0:T(8,128)(2,1)S(1)} %bitcast.75, pred[4,256]{1,0:T(4,128)(4,1)S(1)} %iota_compare_fusion.1), kind=kOutput, calls=%fused_computation.64 | convolution fusion | flops 34800896 | bytes 1577984 | tf_op jit(solution)/shard_map/div | solution.py:112
  (18 shorter events, 0.3 us)
Async XLA Ops:
  0.0 1.0 %copy-start = (bf16[8,4,8,512]{3,2,1,0:T(8,128)(2,1)S(1)}, bf16[8,4,8,512]{3,2,1,0:T(8,128)(2,1)}, u32[]{:S(2)}) copy-start(bf16[8,4,8,512]{3,2,1,0:T(8,128)(2,1)} %param.6) | copy-start | bytes 786436
  0.0 14.1 %copy-start.2 = (bf16[2,16,8,512]{3,2,1,0:T(8,128)(2,1)S(1)}, bf16[2,16,8,512]{3,2,1,0:T(8,128)(2,1)}, u32[]{:S(2)}) copy-start(bf16[2,16,8,512]{3,2,1,0:T(8,128)(2,1)} %param.7) | copy-start | bytes 786436
  0.0 21.5 %collective-permute-start = (bf16[3,3,512,256]{3,2,1,0:T(8,128)(2,1)}, bf16[3,3,512,256]{3,2,1,0:T(8,128)(2,1)S(1)}, u32[]{:S(2)}, u32[]{:S(2)}) collective-permute-start(bf16[3,3,512,256]{3,2,1,0:T(8,128)(2,1)} %param.9), channel_id=1, source_target_pairs={{0,1},{1,0},{2,3},{3,2},{4,5},{5,4},{6,7},{7,6},{8,9},{9,8},{10,11... | collective-permute-start | bytes 7077896 | tf_op jit(solution)/shard_map/ppermute | solution.py:21
  0.5 10.6 %collective-permute-start.1 = (bf16[256,256]{1,0:T(8,128)(2,1)}, bf16[256,256]{1,0:T(8,128)(2,1)S(1)}, u32[]{:S(2)}, u32[]{:S(2)}) collective-permute-start(bf16[256,256]{1,0:T(8,128)(2,1)} %param.10), channel_id=1, source_target_pairs={{0,1},{1,0},{2,3},{3,2},{4,5},{5,4},{6,7},{7,6},{8,9},{9,8},{10,11... | collective-permute-start | bytes 393224 | tf_op jit(solution)/shard_map/ppermute | solution.py:21
  1.7 12.4 %all-to-all-start = ((bf16[4,4,8,512]{3,1,2,0:T(4,128)(2,1)}), bf16[4,4,8,512]{3,1,2,0:T(4,128)(2,1)S(1)}, u32[]{:S(2)}, u32[]{:S(2)}) async-start(bf16[4,4,8,512]{3,1,2,0:T(4,128)(2,1)} %bitcast.64), calls=%async_computation | async-start | bytes 262144 | tf_op jit(solution)/shard_map/all_to_all | solution.py:65
  14.2 6.2 %copy-start.3 = (bf16[3,3,512,256]{3,2,1,0:T(8,128)(2,1)S(1)}, bf16[3,3,512,256]{3,2,1,0:T(8,128)(2,1)}, u32[]{:S(2)}) copy-start(bf16[3,3,512,256]{3,2,1,0:T(8,128)(2,1)} %param.9) | copy-start | bytes 7077892
  14.2 6.2 %copy-start.4 = (pred[8,3]{0,1:T(4,128)(4,1)S(1)}, pred[8,3]{0,1:T(4,128)(4,1)}, u32[]{:S(2)}) copy-start(pred[8,3]{0,1:T(4,128)(4,1)} %constant.83) | copy-start | bytes 76
  23.0 1.8 %copy-start.1 = (bf16[3,512,256]{2,1,0:T(8,128)(2,1)S(1)}, bf16[3,512,256]{2,1,0:T(8,128)(2,1)}, u32[]{:S(2)}) copy-start(bf16[3,512,256]{2,1,0:T(8,128)(2,1)} %param.11) | copy-start | bytes 2359300
  23.0 1.6 %collective-permute-start.2 = (bf16[1,16,16,512]{3,2,1,0:T(8,128)(2,1)S(1)}, bf16[1,16,16,512]{3,2,1,0:T(8,128)(2,1)S(1)}, u32[]{:S(2)}, u32[]{:S(2)}) collective-permute-start(bf16[1,16,16,512]{3,2,1,0:T(8,128)(2,1)S(1)} %bitcast.71), channel_id=1, source_target_pairs={{0,1},{1,0},{2,3},{3,2},{4,5},{5,4},{6,7},{7,6},{8,9},{9,8},{10,11... | collective-permute-start | bytes 786440 | tf_op jit(solution)/shard_map/ppermute | solution.py:21

commit v8 on v4

--- a/solution.py
+++ b/solution.py
@@ -60,9 +60,11 @@
 
     start = l_idx * per_core
     outgoing = lax.dynamic_slice_in_dim(
-        latent_map.reshape(tiles, per_tile, row_local, col_local, width), start, per_core, 1
-    ).reshape(tiles * per_core, row_local, col_local, width)
-    arrived = lax.all_to_all(outgoing, "tile", split_axis=0, concat_axis=1, tiled=True)
+        latent_map.reshape(tiles, per_tile, row_local * col_local, width), start, per_core, 1
+    ).reshape(tiles * per_core, row_local * col_local, width)
+    arrived = lax.all_to_all(outgoing, "tile", split_axis=0, concat_axis=0, tiled=True)
+    arrived = arrived.reshape(tiles, per_core, row_local, col_local, width).transpose(1, 0, 2, 3, 4)
+    arrived = arrived.reshape(per_core, tiles * row_local, col_local, width)
     inner_own = lax.dynamic_slice_in_dim(inner_map, start, per_core, 0)
     joined = (arrived.astype(jnp.float32) + inner_own.astype(jnp.float32)).astype(jnp.bfloat16)
     whole = lax.all_gather(joined, "chan", axis=2, tiled=True)

time: 28.4 us -> 30.4 us (1.070)
  local copies, waits for them, and re-layouts: 4.41 us -> 5.51 us
  other arithmetic: 0.62 us -> 1.52 us
    convert_element_type x1, other arithmetic: 0.04 us -> 0.94 us  [per_device(): (arrived.astype(jnp.float32) + inner_own.astype(jnp.float32)).astype(jnp....]
    reshape x0 -> x1, local copies, waits for them, and re-layouts: none -> 0.66 us  [per_device(): outgoing = lax.dynamic_slice_in_dim(latent_map.reshape(tiles, per_tile, r...]
    unnamed x11 -> x9, local copies, waits for them, and re-layouts: 1.17 us -> 1.76 us
  transfers between devices with their start and end apart: 4 -> 4, of which waited for: 2 -> 2; matrix products, arithmetic and copies ran while one was open for 17% -> 19% of each run, Pallas kernels for 0% -> 0%
where the time goes in v8:
time: 30.4 us; the launch traced here: 30.1 us
  starting transfers between devices  6.91 us (23%)
  blocking collectives  5.64 us (19%)
  local copies, waits for them, and re-layouts  5.51 us (18%)
  matrix products  5.19 us (17%)
  waiting for transfers between devices  4.53 us (15%)
  other arithmetic  1.52 us (5%)
  between operations  0.76 us (2%)
    all_to_all x1, starting transfers between devices, per_device(): lax.all_to_all(outgoing, 'tile', split_axis=0, concat_axis=0, tiled=True)  6.32 us
    all_gather x1, blocking collectives, per_device(): whole = lax.all_gather(joined, 'chan', axis=2, tiled=True)  5.64 us
    all_to_all x1, waiting for transfers between devices, per_device(): lax.all_to_all(outgoing, 'tile', split_axis=0, concat_axis=0, tiled=True)  2.98 us
    conv_general_dilated x2, matrix products, convolve(): lax.conv_general_dilated(joined, weight, window_strides=(1, 1), padding=(...  2.25 us
    unnamed x9, local copies, waits for them, and re-layouts  1.76 us
    ppermute x3, waiting for transfers between devices, swap(): return lax.ppermute(tree, axis, [(0, 1), (1, 0)])  1.56 us
    dynamic_slice x1, local copies, waits for them, and re-layouts, per_device(): lax.dynamic_slice_in_dim(timestep, t_idx * per_tile + start, per_core, 0)  1.23 us
    dot_general x1, matrix products, per_device(): jnp.dot(embedded, time_weight.astype(jnp.float32), precision=lax.Precisio...  1.04 us
  transfers between devices with their start and end apart: 4, of which 2 were waited for; matrix products, arithmetic and copies ran while one was open for 19% of the time, Pallas kernels for 0%

profile of v8, /device:TPU:0, one launch (start us, length us, event | category | flops | bytes accessed | tf_op | source)
XLA Modules:
  0.0 30.1 jit_solution(15998531172332568760)
XLA Ops:
  0.0 0.5 %collective-permute-start = (bf16[3,3,512,256]{3,2,1,0:T(8,128)(2,1)}, bf16[3,3,512,256]{3,2,1,0:T(8,128)(2,1)S(1)}, u32[]{:S(2)}, u32[]{:S(2)}) collective-permute-start(bf16[3,3,512,256]{3,2,1,0:T(8,128)(2,1)} %param.9), channel_id=1, source_target_pairs={{0,1},{1,0},{2,3},{3,2},{4,5},{5,4},{6,7},{7,6},{8,9},{9,8},{10,11... | collective-permute-start | bytes 7077896 | tf_op jit(solution)/shard_map/ppermute | solution.py:21
  0.5 0.1 collective-permute-start.1
  0.5 0.4 %copy-done = bf16[8,4,8,512]{3,2,1,0:T(8,128)(2,1)S(1)} copy-done((bf16[8,4,8,512]{3,2,1,0:T(8,128)(2,1)S(1)}, bf16[8,4,8,512]{3,2,1,0:T(8,128)(2,1)}, u32[]{:S(2)}) %copy-start) | copy-done | bytes 262168
  1.0 0.7 %dynamic-slice_bitcast_fusion = bf16[4,32,512]{2,1,0:T(8,128)(2,1)} fusion(bf16[4,2,32,512]{3,2,1,0:T(8,128)(2,1)S(1)} %bitcast.63, s32[]{:T(128)S(6)} %select_n.20), kind=kLoop, calls=%fused_computation.34 | loop fusion | bytes 262148 | tf_op jit(solution)/shard_map/reshape | solution.py:64
  1.6 6.3 %all-to-all-start = ((bf16[4,32,512]{2,1,0:T(8,128)(2,1)}), bf16[4,32,512]{2,1,0:T(8,128)(2,1)S(1)}, u32[]{:S(2)}, u32[]{:S(2)}) async-start(bf16[4,32,512]{2,1,0:T(8,128)(2,1)} %dynamic-slice_bitcast_fusion), calls=%async_computation | async-start | bytes 262144 | tf_op jit(solution)/shard_map/all_to_all | solution.py:65
  7.9 1.2 %dynamic_slice.21 = s32[1]{0:T(128)} dynamic-slice(s32[8]{0:T(128)} %param.8, s32[]{:T(128)S(6)} %select_n.21), dynamic_slice_sizes={1} | dynamic-slice | bytes 12 | tf_op jit(solution)/shard_map/dynamic_slice | solution.py:72
  9.7 0.1 fusion.23
  9.8 1.0 %fusion.32 = f32[1,256]{1,0:T(1,128)S(1)} fusion(bf16[256,256]{1,0:T(8,128)(2,1)} %param.10, f32[1,128]{1,0:T(1,128)S(1)} %get-tuple-element.7, f32[1,128]{1,0:T(1,128)S(1)} %get-tuple-element.8), kind=kOutput, calls=%fused_computation.51 | convolution fusion | flops 786688 | bytes 133120 | tf_op jit(solution)/shard_map/dot_general | solution.py:74
  10.9 0.1 fusion.31
  11.0 3.0 %all-to-all-done = bf16[4,32,512]{2,1,0:T(8,128)(2,1)S(1)} async-done(((bf16[4,32,512]{2,1,0:T(8,128)(2,1)}), bf16[4,32,512]{2,1,0:T(8,128)(2,1)S(1)}, u32[]{:S(2)}, u32[]{:S(2)}) %all-to-all-start) | async-done | bytes 131104 | tf_op jit(solution)/shard_map/all_to_all | solution.py:65
  14.0 0.9 %fusion.15 = bf16[1,16,8,512]{3,2,1,0:T(8,128)(2,1)S(1)} fusion(bf16[1,16,8,512]{3,2,1,0:T(8,128)(2,1)S(1)} %bitcast.72, bf16[2,16,8,512]{3,2,1,0:T(8,128)(2,1)} %param.7, s32[]{:T(128)S(6)} %select_n.20), kind=kLoop, calls=%fused_computation.26 | loop fusion | flops 262144 | bytes 393220 | tf_op jit(solution)/shard_map/convert_element_type | solution.py:69
  14.9 5.6 %all_gather.3 = bf16[1,16,16,512]{3,2,1,0:T(8,128)(2,1)S(1)} all-gather(bf16[1,16,8,512]{3,2,1,0:T(8,128)(2,1)S(1)} %fusion.15), channel_id=1, replica_groups=mesh['groups'=2,'tile'=4,'chan'=2,'low'=2] {'chan'}, dimensions={2}, use_global_device_ids=true | all-gather | bytes 393216 | tf_op jit(solution)/shard_map/all_gather | solution.py:70
  20.6 0.1 copy.32
  20.8 0.2 copy.22
  21.0 0.1 slice.15
  21.1 1.2 %copy-done.2 = bf16[3,3,512,256]{3,2,1,0:T(8,128)(2,1)S(1)} copy-done((bf16[3,3,512,256]{3,2,1,0:T(8,128)(2,1)S(1)}, bf16[3,3,512,256]{3,2,1,0:T(8,128)(2,1)}, u32[]{:S(2)}) %copy-start.2) | copy-done | bytes 2359320
  22.3 1.1 %multiply_convert_fusion.1 = bf16[16,8,3,256]{3,1,2,0:T(8,128)(2,1)S(1)} fusion(bf16[3,3,512,256]{3,2,1,0:T(8,128)(2,1)S(1)} %copy-done.2, bf16[16,1,7,2,512]{4,2,3,0,1:T(8,128)(2,1)S(1)} %slice.15, bf16[16,1,8,3,512]{4,2,3,0,1:T(8,128)(2,1)S(1)} %copy.22, f32[256]{0:T(256)S(1)} %broadcast_add_fusion.1, pred[8,3]{0,1:T(4,128)(4,1)S(1)} %copy-done.3), kind=kOutput, calls=%fused_computation.22 | convolution fusion | flops 870875136 | bytes 3179544 | tf_op jit(solution)/shard_map/conv_general_dilated | solution.py:25
  23.4 1.1 %multiply_convert_fusion = bf16[16,8,3,256]{3,1,2,0:T(8,128)(2,1)S(1)} fusion(bf16[3,3,512,256]{3,2,1,0:T(8,128)(2,1)S(1)} %collective-permute-done, bf16[16,1,7,2,512]{4,2,3,0,1:T(8,128)(2,1)S(1)} %slice.15, bf16[16,1,8,3,512]{4,2,3,0,1:T(8,128)(2,1)S(1)} %copy.22, f32[256]{0:T(256)S(1)} %broadcast_add_fusion, pred[8,3]{0,1:T(4,128)(4,1)S(1)} %copy-done.3), kind=kOutput, calls=%fused_computation.21 | convolution fusion | flops 870875136 | bytes 3179544 | tf_op jit(solution)/shard_map/conv_general_dilated | solution.py:25
  24.6 0.1 copy.23
  24.8 0.2 copy.34
  24.9 0.1 collective-permute-start.2
  25.0 1.5 %collective-permute-done.2 = bf16[1,16,16,512]{3,2,1,0:T(8,128)(2,1)S(1)} collective-permute-done((bf16[1,16,16,512]{3,2,1,0:T(8,128)(2,1)S(1)}, bf16[1,16,16,512]{3,2,1,0:T(8,128)(2,1)S(1)}, u32[]{:S(2)}, u32[]{:S(2)}) %collective-permute-start.2) | collective-permute-done | bytes 262176 | tf_op jit(solution)/shard_map/ppermute | solution.py:21
  26.5 0.1 pad_maximum_fusion
  26.7 0.3 %convolution_convert_fusion = bf16[2,256,256]{1,2,0:T(8,128)(2,1)S(1)} fusion(bf16[2,256,512]{2,1,0:T(8,128)(2,1)S(1)} %bitcast.64, bf16[3,512,256]{2,1,0:T(8,128)(2,1)S(1)} %copy-done.1), kind=kOutput, calls=%fused_computation.3 | convolution fusion | flops 134348800 | bytes 1048576 | tf_op jit(solution)/shard_map/dot_general | solution.py:94
  27.0 0.3 %convolution_convert_fusion.1 = bf16[2,256,256]{1,2,0:T(8,128)(2,1)S(1)} fusion(bf16[2,256,512]{2,1,0:T(8,128)(2,1)S(1)} %bitcast.65, bf16[3,512,256]{2,1,0:T(8,128)(2,1)S(1)} %copy-done.1), kind=kOutput, calls=%fused_computation.4 | convolution fusion | flops 134348800 | bytes 1048576 | tf_op jit(solution)/shard_map/dot_general | solution.py:94
  27.4 0.2 convolution_convert_fusion.2
  27.6 0.1 copy.26
  27.8 0.4 %fusion.33 = (f32[2,4,128]{2,1,0:T(4,128)S(1)}, f32[2,4,128,256]{3,2,1,0:T(8,128)S(1)}) fusion(bf16[2,128,4,64]{1,3,2,0:T(8,128)(2,1)S(1)} %bitcast.73, bf16[2,256,4,64]{1,3,2,0:T(8,128)(2,1)S(1)} %bitcast.71), kind=kOutput, calls=%fused_computation.52 | convolution fusion | flops 34077696 | bytes 1445888 | tf_op jit(solution)/shard_map/bqhd,bkhd->bhqk/dot_general | solution.py:105
  28.2 0.4 %fusion.5 = f32[2,4,128]{2,1,0:T(4,128)S(1)} fusion(f32[2,4,128,256]{3,2,1,0:T(8,128)S(1)} %get-tuple-element.6, f32[2,4,128]{2,1,0:T(4,128)S(1)} %get-tuple-element.5), kind=kLoop, calls=%fused_computation.14 | loop fusion | flops 523264 | bytes 1056768 | tf_op jit(solution)/shard_map/reduce_sum | solution.py:109
  28.6 0.4 %fusion.4 = bf16[2,128,4,64]{1,3,2,0:T(8,128)(2,1)S(1)} fusion(bf16[2,256,4,64]{1,3,2,0:T(8,128)(2,1)S(1)} %bitcast.74, f32[2,4,128,256]{3,2,1,0:T(8,128)S(1)} %get-tuple-element.6, f32[2,4,128]{2,1,0:T(4,128)S(1)} %get-tuple-element.5, f32[2,128,4]{1,2,0:T(4,128)S(1)} %bitcast.75), kind=kOutput, calls=%fused_computation.11 | convolution fusion | flops 34209792 | bytes 1449984 | tf_op jit(solution)/shard_map/bhqk,bkhd->bqhd/dot_general | solution.py:110
  29.0 0.2 copy.28
  29.2 0.9 %reshape.90 = bf16[2,16,8,256]{3,2,1,0:T(8,128)(2,1)} reshape(bf16[2,128,4,64]{3,2,1,0:T(4,128)(2,1)S(1)} %copy.28) | data formatting | bytes 262144 | tf_op jit(solution)/shard_map/reshape | solution.py:114
  (15 shorter events, 0.2 us)
Async XLA Ops:
  0.0 1.0 %copy-start = (bf16[8,4,8,512]{3,2,1,0:T(8,128)(2,1)S(1)}, bf16[8,4,8,512]{3,2,1,0:T(8,128)(2,1)}, u32[]{:S(2)}) copy-start(bf16[8,4,8,512]{3,2,1,0:T(8,128)(2,1)} %param.6) | copy-start | bytes 786436
  0.0 23.4 %collective-permute-start = (bf16[3,3,512,256]{3,2,1,0:T(8,128)(2,1)}, bf16[3,3,512,256]{3,2,1,0:T(8,128)(2,1)S(1)}, u32[]{:S(2)}, u32[]{:S(2)}) collective-permute-start(bf16[3,3,512,256]{3,2,1,0:T(8,128)(2,1)} %param.9), channel_id=1, source_target_pairs={{0,1},{1,0},{2,3},{3,2},{4,5},{5,4},{6,7},{7,6},{8,9},{9,8},{10,11... | collective-permute-start | bytes 7077896 | tf_op jit(solution)/shard_map/ppermute | solution.py:21
  0.5 10.4 %collective-permute-start.1 = (bf16[256,256]{1,0:T(8,128)(2,1)}, bf16[256,256]{1,0:T(8,128)(2,1)S(1)}, u32[]{:S(2)}, u32[]{:S(2)}) collective-permute-start(bf16[256,256]{1,0:T(8,128)(2,1)} %param.10), channel_id=1, source_target_pairs={{0,1},{1,0},{2,3},{3,2},{4,5},{5,4},{6,7},{7,6},{8,9},{9,8},{10,11... | collective-permute-start | bytes 393224 | tf_op jit(solution)/shard_map/ppermute | solution.py:21
  1.6 12.4 %all-to-all-start = ((bf16[4,32,512]{2,1,0:T(8,128)(2,1)}), bf16[4,32,512]{2,1,0:T(8,128)(2,1)S(1)}, u32[]{:S(2)}, u32[]{:S(2)}) async-start(bf16[4,32,512]{2,1,0:T(8,128)(2,1)} %dynamic-slice_bitcast_fusion), calls=%async_computation | async-start | bytes 262144 | tf_op jit(solution)/shard_map/all_to_all | solution.py:65
  20.6 1.7 %copy-start.2 = (bf16[3,3,512,256]{3,2,1,0:T(8,128)(2,1)S(1)}, bf16[3,3,512,256]{3,2,1,0:T(8,128)(2,1)}, u32[]{:S(2)}) copy-start(bf16[3,3,512,256]{3,2,1,0:T(8,128)(2,1)} %param.9) | copy-start | bytes 7077892
  20.6 1.7 %copy-start.3 = (pred[8,3]{0,1:T(4,128)(4,1)S(1)}, pred[8,3]{0,1:T(4,128)(4,1)}, u32[]{:S(2)}) copy-start(pred[8,3]{0,1:T(4,128)(4,1)} %constant.67) | copy-start | bytes 76
  24.9 1.8 %copy-start.1 = (bf16[3,512,256]{2,1,0:T(8,128)(2,1)S(1)}, bf16[3,512,256]{2,1,0:T(8,128)(2,1)}, u32[]{:S(2)}) copy-start(bf16[3,512,256]{2,1,0:T(8,128)(2,1)} %param.11) | copy-start | bytes 2359300
  24.9 1.6 %collective-permute-start.2 = (bf16[1,16,16,512]{3,2,1,0:T(8,128)(2,1)S(1)}, bf16[1,16,16,512]{3,2,1,0:T(8,128)(2,1)S(1)}, u32[]{:S(2)}, u32[]{:S(2)}) collective-permute-start(bf16[1,16,16,512]{3,2,1,0:T(8,128)(2,1)S(1)} %bitcast.68), channel_id=1, source_target_pairs={{0,1},{1,0},{2,3},{3,2},{4,5},{5,4},{6,7},{7,6},{8,9},{9,8},{10,11... | collective-permute-start | bytes 786440 | tf_op jit(solution)/shard_map/ppermute | solution.py:21

commit v9 on v4

--- a/solution.py
+++ b/solution.py
@@ -56,7 +56,10 @@
     half = conv_weight.shape[3]
     heads_local = attend_weight.shape[2] // HEAD
 
-    conv_other, time_other = swap((conv_weight, time_weight), "low")
+    conv_other, time_other, attend_other = swap((conv_weight, time_weight, attend_weight), "low")
+    attend_full = lax.dynamic_slice_in_dim(
+        jnp.concatenate([attend_weight, attend_other, attend_weight], axis=2), l_idx * half, 2 * half, 2
+    )
 
     start = l_idx * per_core
     outgoing = lax.dynamic_slice_in_dim(
@@ -81,24 +84,22 @@
     nat_own = lax.dynamic_slice_in_dim(
         jnp.concatenate([feat_own, feat_other, feat_own], axis=3), l_idx * half, 2 * half, 3
     )
-    nat_part = swap(nat_own, "low")
-    features = lax.dynamic_slice_in_dim(
-        jnp.concatenate([nat_own, nat_part, nat_own], axis=0), l_idx * per_core, per_tile, 0
-    )
+    features = nat_own
     rows_total, cols_total = features.shape[1], features.shape[2]
     tokens = rows_total * cols_total
+    heads_all = attend_full.shape[2] // HEAD
 
     def project(part, which):
-        return jnp.dot(part, attend_weight[which], preferred_element_type=jnp.float32).astype(jnp.bfloat16)
+        return jnp.dot(part, attend_full[which], preferred_element_type=jnp.float32).astype(jnp.bfloat16)
 
     own_cols = lax.dynamic_slice_in_dim(features, c_idx * col_local, col_local, 2)
-    flat = features.reshape(per_tile, tokens, width)
-    queries = project(own_cols.reshape(per_tile, -1, width), 0)
+    flat = features.reshape(per_core, tokens, width)
+    queries = project(own_cols.reshape(per_core, -1, width), 0)
     keys = project(flat, 1)
     values = project(flat, 2)
     query_count = queries.shape[1]
-    if tokens * query_count * 4 * per_tile * heads_local <= (8 << 20):
-        split = lambda x: x.reshape(per_tile, x.shape[1], heads_local, HEAD)
+    if tokens * query_count * 4 * per_core * heads_all <= (8 << 20):
+        split = lambda x: x.reshape(per_core, x.shape[1], heads_all, HEAD)
         q4, k4, v4 = split(queries), split(keys), split(values)
         scores = jnp.einsum("bqhd,bkhd->bhqk", q4, k4, preferred_element_type=jnp.float32)
         scores = scores * HEAD ** (-0.5)
@@ -109,16 +110,21 @@
             "bhqk,bkhd->bqhd", weights.astype(jnp.bfloat16), v4, preferred_element_type=jnp.float32
         )
         out = (summed / totals.transpose(0, 2, 1)[..., None]).astype(jnp.bfloat16)
-        return out.reshape(per_tile, rows_total, col_local, heads_local * HEAD)
+    else:
+        def by_head(x):
+            n, k, _ = x.shape
+            return x.reshape(n, k, heads_all, HEAD).transpose(0, 2, 1, 3).reshape(n * heads_all, k, HEAD)
 
-    def by_head(x):
-        n, k, _ = x.shape
-        return x.reshape(n, k, heads_local, HEAD).transpose(0, 2, 1, 3).reshape(n * heads_local, k, HEAD)
-
-    q_heads, k_heads, v_heads = by_head(queries), by_head(keys), by_head(values)
-    out = lax.map(lambda trio: attend(*(x[None] for x in trio))[0], (q_heads, k_heads, v_heads))
-    out = out.reshape(per_tile, heads_local, rows_total, col_local, HEAD)
-    return out.transpose(0, 2, 3, 1, 4).reshape(per_tile, rows_total, col_local, heads_local * HEAD)
+        trio = (by_head(queries), by_head(keys), by_head(values))
+        out = lax.map(lambda one: attend(*(x[None] for x in one))[0], trio)
+        out = out.reshape(per_core, heads_all, query_count, HEAD).transpose(0, 2, 1, 3)
+    out = out.reshape(per_core, rows_total, col_local, heads_all * HEAD)
+    kept = lax.dynamic_slice_in_dim(out, l_idx * half, half, 3)
+    given = lax.dynamic_slice_in_dim(out, (1 - l_idx) * half, half, 3)
+    got = swap(given, "low")
+    return lax.dynamic_slice_in_dim(
+        jnp.concatenate([kept, got, kept], axis=0), l_idx * per_core, per_tile, 0
+    )
 
 
 def solution(mesh):

time: 28.4 us -> 31.9 us (1.12)
  other arithmetic: 0.62 us -> 3.1 us
  matrix products: 5.18 us -> 6.76 us
  local copies, waits for them, and re-layouts: 4.41 us -> 4.07 us
    conv_general_dilated x2, matrix products: 2.25 us -> 3.95 us  [convolve(): lax.conv_general_dilated(joined, weight, window_strides=(1, 1), padding=(...]
    concatenate x1 -> x2, other arithmetic: 0.09 us -> 1.52 us  [the longest x1 0.8 us: per_device(): jnp.concatenate([attend_weight, attend_other, attend_weight], axis=2)]
    convert_element_type x1, other arithmetic: 0.04 us -> 1.09 us  [per_device(): (arrived.astype(jnp.float32) + inner_own.astype(jnp.float32)).astype(jnp....]
    reshape x1, local copies, waits for them, and re-layouts: 0.87 us -> 0.21 us  [per_device(): out = out.reshape(per_core, rows_total, col_local, heads_all * HEAD)]
    ppermute x3 -> x4, waiting for transfers between devices: 1.56 us -> 1.29 us  [swap(): return lax.ppermute(tree, axis, [(0, 1), (1, 0)])]
    unnamed x11 -> x9, local copies, waits for them, and re-layouts: 1.17 us -> 1.17 us
  transfers between devices with their start and end apart: 4 -> 5, of which waited for: 2 -> 2; matrix products, arithmetic and copies ran while one was open for 17% -> 21% of each run, Pallas kernels for 0% -> 0%
where the time goes in v9:
time: 31.9 us; the launch traced here: 31.5 us
  starting transfers between devices  6.91 us (22%)
  matrix products  6.76 us (21%)
  blocking collectives  5.64 us (18%)
  waiting for transfers between devices  4.13 us (13%)
  local copies, waits for them, and re-layouts  4.07 us (13%)
  other arithmetic  3.1 us (10%)
  between operations  0.9 us (3%)
    all_to_all x1, starting transfers between devices, per_device(): lax.all_to_all(outgoing, 'tile', split_axis=0, concat_axis=1, tiled=True)  6.32 us
    all_gather x1, blocking collectives, per_device(): whole = lax.all_gather(joined, 'chan', axis=2, tiled=True)  5.64 us
    conv_general_dilated x2, matrix products, convolve(): lax.conv_general_dilated(joined, weight, window_strides=(1, 1), padding=(...  3.95 us
    all_to_all x1, waiting for transfers between devices, per_device(): lax.all_to_all(outgoing, 'tile', split_axis=0, concat_axis=1, tiled=True)  2.84 us
    ppermute x4, waiting for transfers between devices, swap(): return lax.ppermute(tree, axis, [(0, 1), (1, 0)])  1.29 us
    dynamic_slice x1, local copies, waits for them, and re-layouts, per_device(): lax.dynamic_slice_in_dim(timestep, t_idx * per_tile + start, per_core, 0)  1.29 us
    unnamed x9, local copies, waits for them, and re-layouts  1.17 us
    convert_element_type x1, other arithmetic, per_device(): (arrived.astype(jnp.float32) + inner_own.astype(jnp.float32)).astype(jnp....  1.09 us
  transfers between devices with their start and end apart: 5, of which 2 were waited for; matrix products, arithmetic and copies ran while one was open for 21% of the time, Pallas kernels for 0%

profile of v9, /device:TPU:0, one launch (start us, length us, event | category | flops | bytes accessed | tf_op | source)
XLA Modules:
  0.0 31.5 jit_solution(4185874538683745441)
XLA Ops:
  0.0 0.5 %collective-permute-start = (bf16[3,3,512,256]{3,2,1,0:T(8,128)(2,1)}, bf16[3,3,512,256]{3,2,1,0:T(8,128)(2,1)}, u32[]{:S(2)}, u32[]{:S(2)}) collective-permute-start(bf16[3,3,512,256]{3,2,1,0:T(8,128)(2,1)} %param.9), channel_id=1, source_target_pairs={{0,1},{1,0},{2,3},{3,2},{4,5},{5,4},{6,7},{7,6},{8,9},{9,8},{10,11... | collective-permute-start | bytes 7077896 | tf_op jit(solution)/shard_map/ppermute | solution.py:21
  0.5 0.1 collective-permute-start.1
  0.5 0.4 %copy-done = bf16[8,4,8,512]{3,2,1,0:T(8,128)(2,1)S(1)} copy-done((bf16[8,4,8,512]{3,2,1,0:T(8,128)(2,1)S(1)}, bf16[8,4,8,512]{3,2,1,0:T(8,128)(2,1)}, u32[]{:S(2)}) %copy-start) | copy-done | bytes 262168
  1.0 0.7 %copy.61 = bf16[4,1,4,8,512]{4,2,3,0,1:T(4,128)(2,1)} copy(bf16[4,1,4,8,512]{4,3,2,1,0:T(8,128)(2,1)S(1)} %constant_dynamic-slice_fusion.4) | data formatting | bytes 262144
  1.7 6.3 %all-to-all-start = ((bf16[4,4,8,512]{3,1,2,0:T(4,128)(2,1)}), bf16[4,4,8,512]{3,1,2,0:T(4,128)(2,1)S(1)}, u32[]{:S(2)}, u32[]{:S(2)}) async-start(bf16[4,4,8,512]{3,1,2,0:T(4,128)(2,1)} %bitcast.62), calls=%async_computation | async-start | bytes 262144 | tf_op jit(solution)/shard_map/all_to_all | solution.py:68
  8.0 1.3 %dynamic_slice.30 = s32[1]{0:T(128)} dynamic-slice(s32[8]{0:T(128)} %param.8, s32[]{:T(128)S(6)} %select_n.28), dynamic_slice_sizes={1} | dynamic-slice | bytes 12 | tf_op jit(solution)/shard_map/dynamic_slice | solution.py:73
  10.0 1.0 %fusion.29 = f32[1,256]{1,0:T(1,128)S(1)} fusion(bf16[256,256]{1,0:T(8,128)(2,1)} %param.10, f32[1,128]{1,0:T(1,128)S(1)} %get-tuple-element.9, f32[1,128]{1,0:T(1,128)S(1)} %get-tuple-element.10), kind=kOutput, calls=%fused_computation.58 | convolution fusion | flops 786688 | bytes 133120 | tf_op jit(solution)/shard_map/dot_general | solution.py:75
  11.1 0.1 fusion.28
  11.2 2.8 %all-to-all-done = bf16[4,4,8,512]{3,1,2,0:T(4,128)(2,1)S(1)} async-done(((bf16[4,4,8,512]{3,1,2,0:T(4,128)(2,1)}), bf16[4,4,8,512]{3,1,2,0:T(4,128)(2,1)S(1)}, u32[]{:S(2)}, u32[]{:S(2)}) %all-to-all-start) | async-done | bytes 131104 | tf_op jit(solution)/shard_map/all_to_all | solution.py:68
  14.1 1.1 %fusion.15 = bf16[1,16,8,512]{3,2,1,0:T(8,128)(2,1)S(1)} fusion(bf16[2,16,8,512]{3,2,1,0:T(8,128)(2,1)} %param.7, s32[]{:T(128)S(6)} %select_n.27, bf16[1,16,8,512]{3,2,1,0:T(8,128)(2,1)S(1)} %bitcast.69), kind=kLoop, calls=%fused_computation.31 | loop fusion | flops 262144 | bytes 393220 | tf_op jit(solution)/shard_map/convert_element_type | solution.py:70
  15.3 5.6 %all_gather.3 = bf16[1,16,16,512]{3,1,0,2:T(8,128)(2,1)S(1)} all-gather(bf16[1,16,8,512]{3,1,0,2:T(8,128)(2,1)S(1)} %copy.45), channel_id=1, replica_groups=mesh['groups'=2,'tile'=4,'chan'=2,'low'=2] {'chan'}, dimensions={2}, use_global_device_ids=true | all-gather | bytes 393216 | tf_op jit(solution)/shard_map/all_gather | solution.py:71
  21.0 0.2 copy.47
  21.3 1.2 %multiply_convert_fusion.1 = bf16[16,8,3,256]{3,1,2,0:T(8,128)(2,1)S(1)} fusion(bf16[3,3,512,256]{3,2,1,0:T(8,128)(2,1)S(1)} %copy-done.2, bf16[16,1,7,2,512]{4,2,3,0,1:T(8,128)(2,1)S(1)} %slice.15, bf16[16,1,8,3,512]{4,2,3,0,1:T(8,128)(2,1)S(1)} %copy.47, f32[256]{0:T(256)S(1)} %broadcast_add_fusion.1, pred[8,3]{0,1:T(4,128)(4,1)S(1)} %copy-done.3), kind=kOutput, calls=%fused_computation.29 | convolution fusion | flops 870875136 | bytes 3179544 | tf_op jit(solution)/shard_map/conv_general_dilated | solution.py:25
  22.5 0.8 %fusion.1 = bf16[3,512,512]{2,1,0:T(8,128)(2,1)S(1)} fusion(s32[]{:T(128)S(6)} %select_n.29, bf16[3,512,256]{2,1,0:T(8,128)(2,1)S(1)} %copy-done.1, bf16[3,512,256]{2,1,0:T(8,128)(2,1)S(1)} %collective-permute-done.2), kind=kLoop, calls=%fused_computation.4 | loop fusion | flops 4718592 | bytes 3145732 | tf_op jit(solution)/shard_map/concatenate | solution.py:61
  23.3 2.8 %multiply_convert_fusion = bf16[16,8,3,256]{3,1,2,0:T(8,128)(2,1)S(1)} fusion(bf16[3,3,512,256]{3,2,1,0:T(8,128)(2,1)} %collective-permute-done, bf16[16,1,7,2,512]{4,2,3,0,1:T(8,128)(2,1)S(1)} %slice.15, bf16[16,1,8,3,512]{4,2,3,0,1:T(8,128)(2,1)S(1)} %copy.47, f32[256]{0:T(256)S(1)} %broadcast_add_fusion, pred[8,3]{0,1:T(4,128)(4,1)S(1)} %copy-done.3), kind=kOutput, calls=%fused_computation.28 | convolution fusion | flops 870875136 | bytes 3179544 | tf_op jit(solution)/shard_map/conv_general_dilated | solution.py:25
  26.1 0.1 copy.48
  26.3 0.2 copy.49
  26.5 0.3 convolution_convert_fusion
  26.8 0.3 convolution_convert_fusion.1
  27.1 0.1 copy.53
  27.2 0.1 constant_dynamic-slice_fusion.2
  27.3 0.2 convolution_convert_fusion.2
  27.6 0.1 copy.52
  27.7 0.1 copy.50
  27.9 0.4 %fusion.30 = (f32[8,128]{1,0:T(8,128)S(1)}, f32[8,128,256]{2,1,0:T(8,128)S(1)}) fusion(bf16[128,8,64]{0,2,1:T(8,128)(2,1)S(1)} %bitcast.70, bf16[256,8,64]{0,2,1:T(8,128)(2,1)S(1)} %bitcast.68), kind=kOutput, calls=%fused_computation.59 | convolution fusion | flops 34077696 | bytes 1445888 | tf_op jit(solution)/shard_map/bqhd,bkhd->bhqk/dot_general | solution.py:104
  28.3 0.4 %fusion.7 = f32[8,128]{1,0:T(8,128)S(1)} fusion(f32[8,128,256]{2,1,0:T(8,128)S(1)} %get-tuple-element.8, f32[8,128]{1,0:T(8,128)S(1)} %get-tuple-element.7), kind=kLoop, calls=%fused_computation.19 | loop fusion | flops 523264 | bytes 1056768 | tf_op jit(solution)/shard_map/reduce_sum | solution.py:108
  28.7 0.4 %fusion.6 = bf16[1,128,8,64]{1,3,2,0:T(8,128)(2,1)S(1)} fusion(bf16[256,8,64]{0,2,1:T(8,128)(2,1)S(1)} %bitcast.71, f32[8,128,256]{2,1,0:T(8,128)S(1)} %get-tuple-element.8, f32[8,128]{1,0:T(8,128)S(1)} %get-tuple-element.7, f32[128,8]{0,1:T(8,128)S(1)} %bitcast.74), kind=kOutput, calls=%fused_computation.17 | convolution fusion | flops 34209792 | bytes 1449984 | tf_op jit(solution)/shard_map/bhqk,bkhd->bqhd/dot_general | solution.py:109
  29.0 0.2 copy.54
  29.2 0.2 reshape.129
  29.5 0.1 collective-permute-start.3
  29.6 1.2 %collective-permute-done.3 = bf16[1,16,8,256]{3,2,1,0:T(8,128)(2,1)S(1)} collective-permute-done((bf16[1,16,8,256]{3,2,1,0:T(8,128)(2,1)S(1)}, bf16[1,16,8,256]{3,2,1,0:T(8,128)(2,1)S(1)}, u32[]{:S(2)}, u32[]{:S(2)}) %collective-permute-start.3) | collective-permute-done | bytes 65568 | tf_op jit(solution)/shard_map/ppermute | solution.py:21
  30.8 0.7 %fusion.17 = bf16[2,16,8,256]{3,2,1,0:T(8,128)(2,1)} fusion(s32[]{:T(128)S(6)} %select_n.35, bf16[1,16,8,256]{3,2,1,0:T(8,128)(2,1)S(1)} %get-tuple-element.6, bf16[1,16,8,256]{3,2,1,0:T(8,128)(2,1)S(1)} %collective-permute-done.3), kind=kLoop, calls=%fused_computation.36 | loop fusion | flops 131072 | bytes 262148 | tf_op jit(solution)/shard_map/concatenate | solution.py:126
  (23 shorter events, 0.4 us)
Async XLA Ops:
  0.0 1.0 %copy-start = (bf16[8,4,8,512]{3,2,1,0:T(8,128)(2,1)S(1)}, bf16[8,4,8,512]{3,2,1,0:T(8,128)(2,1)}, u32[]{:S(2)}) copy-start(bf16[8,4,8,512]{3,2,1,0:T(8,128)(2,1)} %param.6) | copy-start | bytes 786436
  0.0 23.3 %collective-permute-start = (bf16[3,3,512,256]{3,2,1,0:T(8,128)(2,1)}, bf16[3,3,512,256]{3,2,1,0:T(8,128)(2,1)}, u32[]{:S(2)}, u32[]{:S(2)}) collective-permute-start(bf16[3,3,512,256]{3,2,1,0:T(8,128)(2,1)} %param.9), channel_id=1, source_target_pairs={{0,1},{1,0},{2,3},{3,2},{4,5},{5,4},{6,7},{7,6},{8,9},{9,8},{10,11... | collective-permute-start | bytes 7077896 | tf_op jit(solution)/shard_map/ppermute | solution.py:21
  0.5 10.6 %collective-permute-start.1 = (bf16[256,256]{1,0:T(8,128)(2,1)}, bf16[256,256]{1,0:T(8,128)(2,1)S(1)}, u32[]{:S(2)}, u32[]{:S(2)}) collective-permute-start(bf16[256,256]{1,0:T(8,128)(2,1)} %param.10), channel_id=1, source_target_pairs={{0,1},{1,0},{2,3},{3,2},{4,5},{5,4},{6,7},{7,6},{8,9},{9,8},{10,11... | collective-permute-start | bytes 393224 | tf_op jit(solution)/shard_map/ppermute | solution.py:21
  1.7 12.4 %all-to-all-start = ((bf16[4,4,8,512]{3,1,2,0:T(4,128)(2,1)}), bf16[4,4,8,512]{3,1,2,0:T(4,128)(2,1)S(1)}, u32[]{:S(2)}, u32[]{:S(2)}) async-start(bf16[4,4,8,512]{3,1,2,0:T(4,128)(2,1)} %bitcast.62), calls=%async_computation | async-start | bytes 262144 | tf_op jit(solution)/shard_map/all_to_all | solution.py:68
  8.0 14.5 %collective-permute-start.2 = (bf16[3,512,256]{2,1,0:T(8,128)(2,1)}, bf16[3,512,256]{2,1,0:T(8,128)(2,1)S(1)}, u32[]{:S(2)}, u32[]{:S(2)}) collective-permute-start(bf16[3,512,256]{2,1,0:T(8,128)(2,1)} %param.11), channel_id=1, source_target_pairs={{0,1},{1,0},{2,3},{3,2},{4,5},{5,4},{6,7},{7,6},{8,9},{9,8},{10,11... | collective-permute-start | bytes 2359304 | tf_op jit(solution)/shard_map/ppermute | solution.py:21
  14.1 7.1 %copy-start.2 = (bf16[3,3,512,256]{3,2,1,0:T(8,128)(2,1)S(1)}, bf16[3,3,512,256]{3,2,1,0:T(8,128)(2,1)}, u32[]{:S(2)}) copy-start(bf16[3,3,512,256]{3,2,1,0:T(8,128)(2,1)} %param.9) | copy-start | bytes 7077892
  14.1 7.1 %copy-start.3 = (pred[8,3]{0,1:T(4,128)(4,1)S(1)}, pred[8,3]{0,1:T(4,128)(4,1)}, u32[]{:S(2)}) copy-start(pred[8,3]{0,1:T(4,128)(4,1)} %constant.70) | copy-start | bytes 76
  21.3 1.2 %copy-start.1 = (bf16[3,512,256]{2,1,0:T(8,128)(2,1)S(1)}, bf16[3,512,256]{2,1,0:T(8,128)(2,1)}, u32[]{:S(2)}) copy-start(bf16[3,512,256]{2,1,0:T(8,128)(2,1)} %param.11) | copy-start | bytes 2359300
  29.5 1.3 %collective-permute-start.3 = (bf16[1,16,8,256]{3,2,1,0:T(8,128)(2,1)S(1)}, bf16[1,16,8,256]{3,2,1,0:T(8,128)(2,1)S(1)}, u32[]{:S(2)}, u32[]{:S(2)}) collective-permute-start(bf16[1,16,8,256]{3,2,1,0:T(8,128)(2,1)S(1)} %get-tuple-element.5), channel_id=1, source_target_pairs={{0,1},{1,0},{2,3},{3,2},{4,5},{5,4},{6,7},{7,6},{8,9},{9,8},{10,11... | collective-permute-start | bytes 196616 | tf_op jit(solution)/shard_map/ppermute | solution.py:21

commit v10 on v4

--- a/solution.py
+++ b/solution.py
@@ -3,6 +3,8 @@
 import jax
 import jax.numpy as jnp
 from jax import lax
+from jax.experimental import pallas as pl
+from jax.experimental.pallas import tpu as pltpu
 from jax.sharding import PartitionSpec as P
 
 HEAD = 64
@@ -42,6 +44,42 @@
         "nqk,nkd->nqd", weights.astype(jnp.bfloat16), values, preferred_element_type=jnp.float32
     )
     return (summed / totals).astype(jnp.bfloat16)
+
+
+def attention_kernel(q_ref, k_ref, v_ref, o_ref):
+    samples, _, lanes = q_ref.shape
+    for sample in range(samples):
+        for head in range(lanes // HEAD):
+            part = slice(head * HEAD, (head + 1) * HEAD)
+            queries = q_ref[sample, :, part]
+            keys = k_ref[sample, :, part]
+            scores = lax.dot_general(
+                queries, keys, (((1,), (1,)), ((), ())), preferred_element_type=jnp.float32
+            )
+            scores = scores * HEAD ** (-0.5)
+            row_peak = jnp.max(scores, axis=1, keepdims=True)
+            weights = jnp.exp(scores - row_peak)
+            totals = jnp.sum(weights, axis=1, keepdims=True)
+            summed = jnp.dot(
+                weights.astype(jnp.bfloat16), v_ref[sample, :, part], preferred_element_type=jnp.float32
+            )
+            o_ref[sample, :, part] = (summed / totals).astype(o_ref.dtype)
+
+
+def attention_call(queries, keys, values):
+    samples, query_count, lanes = queries.shape
+    key_count = keys.shape[1]
+    flops = 4 * samples * query_count * key_count * lanes
+    moved = 2 * (2 * queries.size + keys.size + values.size)
+    return pl.pallas_call(
+        attention_kernel,
+        out_shape=jax.ShapeDtypeStruct(queries.shape, jnp.bfloat16),
+        in_specs=[pl.BlockSpec(memory_space=pltpu.VMEM)] * 3,
+        out_specs=pl.BlockSpec(memory_space=pltpu.VMEM),
+        cost_estimate=pl.CostEstimate(
+            flops=flops, transcendentals=samples * query_count * key_count * lanes // HEAD, bytes_accessed=moved
+        ),
+    )(queries, keys, values)
 
 
 def per_device(latent_map, inner_map, timestep, conv_weight, time_weight, attend_weight):
@@ -98,17 +136,7 @@
     values = project(flat, 2)
     query_count = queries.shape[1]
     if tokens * query_count * 4 * per_tile * heads_local <= (8 << 20):
-        split = lambda x: x.reshape(per_tile, x.shape[1], heads_local, HEAD)
-        q4, k4, v4 = split(queries), split(keys), split(values)
-        scores = jnp.einsum("bqhd,bkhd->bhqk", q4, k4, preferred_element_type=jnp.float32)
-        scores = scores * HEAD ** (-0.5)
-        row_peak = jnp.max(scores, axis=3, keepdims=True)
-        weights = jnp.exp(scores - row_peak)
-        totals = jnp.sum(weights, axis=3)
-        summed = jnp.einsum(
-            "bhqk,bkhd->bqhd", weights.astype(jnp.bfloat16), v4, preferred_element_type=jnp.float32
-        )
-        out = (summed / totals.transpose(0, 2, 1)[..., None]).astype(jnp.bfloat16)
+        out = attention_call(queries, keys, values)
         return out.reshape(per_tile, rows_total, col_local, heads_local * HEAD)
 
     def by_head(x):

time: 28.4 us -> 40.7 us (1.43)
  matrix products: 5.18 us -> 14.4 us
  Pallas kernels: 0 us -> 3.11 us
  blocking collectives: 5.78 us -> 7.18 us
  waiting for transfers between devices: 4.32 us -> 3.45 us
  local copies, waits for them, and re-layouts: 4.41 us -> 3.75 us
    conv_general_dilated x2, matrix products: 2.25 us -> 10.3 us  [convolve(): lax.conv_general_dilated(joined, weight, window_strides=(1, 1), padding=(...]
    pallas_call x0 -> x1, Pallas kernels: none -> 3.11 us  [attention_call(): pl.pallas_call(attention_kernel, out_shape=jax.ShapeDtypeStruct(queries.s...]
    dot_general x3, matrix products: 0.94 us -> 2.88 us  [project(): jnp.dot(part, attend_weight[which], preferred_element_type=jnp.float32)]
    all_gather x1, blocking collectives: 5.78 us -> 7.18 us  [per_device(): whole = lax.all_gather(joined, 'chan', axis=2, tiled=True)]
    all_to_all x1, waiting for transfers between devices: 2.76 us -> 1.93 us  [per_device(): lax.all_to_all(outgoing, 'tile', split_axis=0, concat_axis=1, tiled=True)]
    dot_general x2 -> x0, matrix products: 0.82 us -> none  [the longest x1 0.43 us: per_device(): jnp.einsum('bqhd,bkhd->bhqk', q4, k4, preferred_element_type=jnp.float32)]
    dynamic_slice x3 -> x1, local copies, waits for them, and re-layouts: 0.19 us -> 0.96 us  [per_device(): inner_own = lax.dynamic_slice_in_dim(inner_map, start, per_core, 0)]
    unnamed x11 -> x4, local copies, waits for them, and re-layouts: 1.17 us -> 0.43 us
  transfers between devices with their start and end apart: 4 -> 4, of which waited for: 2 -> 2; matrix products, arithmetic and copies ran while one was open for 17% -> 25% of each run, Pallas kernels for 0% -> 0%
where the time goes in v10:
time: 40.7 us; the launch traced here: 40.3 us
  matrix products  14.4 us (35%)
  blocking collectives  7.18 us (18%)
  starting transfers between devices  6.91 us (17%)
  local copies, waits for them, and re-layouts  3.75 us (9%)
  waiting for transfers between devices  3.45 us (8%)
  Pallas kernels  3.11 us (8%)
  between operations  0.77 us (2%)
  other arithmetic  0.74 us (2%)
    conv_general_dilated x2, matrix products, convolve(): lax.conv_general_dilated(joined, weight, window_strides=(1, 1), padding=(...  10.3 us
    all_gather x1, blocking collectives, per_device(): whole = lax.all_gather(joined, 'chan', axis=2, tiled=True)  7.18 us
    all_to_all x1, starting transfers between devices, per_device(): lax.all_to_all(outgoing, 'tile', split_axis=0, concat_axis=1, tiled=True)  6.32 us
    pallas_call x1, Pallas kernels, attention_call(): pl.pallas_call(attention_kernel, out_shape=jax.ShapeDtypeStruct(queries.s...  3.11 us
    dot_general x3, matrix products, project(): jnp.dot(part, attend_weight[which], preferred_element_type=jnp.float32)  2.88 us
    all_to_all x1, waiting for transfers between devices, per_device(): lax.all_to_all(outgoing, 'tile', split_axis=0, concat_axis=1, tiled=True)  1.93 us
    ppermute x3, waiting for transfers between devices, swap(): return lax.ppermute(tree, axis, [(0, 1), (1, 0)])  1.51 us
    dynamic_slice x1, local copies, waits for them, and re-layouts, per_device(): lax.dynamic_slice_in_dim(timestep, t_idx * per_tile + start, per_core, 0)  1.29 us
  transfers between devices with their start and end apart: 4, of which 2 were waited for; matrix products, arithmetic and copies ran while one was open for 25% of the time, Pallas kernels for 0%

profile of v10, /device:TPU:0, one launch (start us, length us, event | category | flops | bytes accessed | tf_op | source)
XLA Modules:
  0.0 40.3 jit_solution(6932622638809118807)
XLA Ops:
  0.0 0.0 copy-start
  0.0 0.5 %collective-permute-start = (bf16[3,3,512,256]{3,2,1,0:T(8,128)(2,1)}, bf16[3,3,512,256]{3,2,1,0:T(8,128)(2,1)}, u32[]{:S(2)}, u32[]{:S(2)}) collective-permute-start(bf16[3,3,512,256]{3,2,1,0:T(8,128)(2,1)} %param.9), channel_id=1, source_target_pairs={{0,1},{1,0},{2,3},{3,2},{4,5},{5,4},{6,7},{7,6},{8,9},{9,8},{10,11... | collective-permute-start | bytes 7077896 | tf_op jit(solution)/shard_map/ppermute | solution.py:23
  0.5 0.1 collective-permute-start.1
  0.5 0.4 %copy-done = bf16[8,4,8,512]{3,2,1,0:T(8,128)(2,1)S(1)} copy-done((bf16[8,4,8,512]{3,2,1,0:T(8,128)(2,1)S(1)}, bf16[8,4,8,512]{3,2,1,0:T(8,128)(2,1)}, u32[]{:S(2)}) %copy-start) | copy-done | bytes 262168
  1.0 0.7 %dynamic-slice_bitcast_fusion = bf16[4,4,8,512]{3,2,1,0:T(8,128)(2,1)} fusion(bf16[4,2,4,8,512]{4,3,2,1,0:T(8,128)(2,1)S(1)} %bitcast.39, s32[]{:T(128)S(6)} %select_n.20), kind=kLoop, calls=%fused_computation.24 | loop fusion | bytes 262148 | tf_op jit(solution)/shard_map/reshape | solution.py:102
  1.6 6.3 %all-to-all-start = ((bf16[4,4,8,512]{3,2,1,0:T(8,128)(2,1)}), bf16[4,4,8,512]{3,2,1,0:T(8,128)(2,1)S(1)}, u32[]{:S(2)}, u32[]{:S(2)}) async-start(bf16[4,4,8,512]{3,2,1,0:T(8,128)(2,1)} %dynamic-slice_bitcast_fusion), calls=%async_computation | async-start | bytes 262144 | tf_op jit(solution)/shard_map/all_to_all | solution.py:103
  7.9 1.3 %dynamic_slice.21 = s32[1]{0:T(128)} dynamic-slice(s32[8]{0:T(128)} %param.8, s32[]{:T(128)S(6)} %select_n.21), dynamic_slice_sizes={1} | dynamic-slice | bytes 12 | tf_op jit(solution)/shard_map/dynamic_slice | solution.py:108
  9.9 0.1 fusion.13
  9.9 1.0 %fusion.16 = f32[1,256]{1,0:T(1,128)S(1)} fusion(bf16[256,256]{1,0:T(8,128)(2,1)} %param.10, f32[1,128]{1,0:T(1,128)S(1)} %get-tuple-element.5, f32[1,128]{1,0:T(1,128)S(1)} %get-tuple-element.6), kind=kOutput, calls=%fused_computation.35 | convolution fusion | flops 786688 | bytes 133120 | tf_op jit(solution)/shard_map/dot_general | solution.py:110
  11.0 1.0 %constant_dynamic-slice_fusion.1 = bf16[1,16,8,512]{3,2,1,0:T(8,128)(2,1)S(1)} fusion(bf16[2,16,8,512]{3,2,1,0:T(8,128)(2,1)} %param.7, s32[]{:T(128)S(6)} %select_n.20), kind=kLoop, calls=%fused_computation.27 | loop fusion | bytes 262148 | tf_op jit(solution)/shard_map/dynamic_slice | solution.py:104
  11.9 0.0 collective-permute-done.1
  11.9 0.1 fusion.15
  12.1 1.9 %all-to-all-done = bf16[4,4,8,512]{3,2,1,0:T(8,128)(2,1)S(1)} async-done(((bf16[4,4,8,512]{3,2,1,0:T(8,128)(2,1)}), bf16[4,4,8,512]{3,2,1,0:T(8,128)(2,1)S(1)}, u32[]{:S(2)}, u32[]{:S(2)}) %all-to-all-start) | async-done | bytes 131104 | tf_op jit(solution)/shard_map/all_to_all | solution.py:103
  14.0 0.4 reshape.80
  14.4 0.3 fusion.3
  14.7 7.2 %all_gather.3 = bf16[1,16,16,512]{3,0,2,1:T(2,128)(2,1)S(1)} all-gather(bf16[1,16,8,512]{3,0,2,1:T(2,128)(2,1)S(1)} %fusion.3), channel_id=1, replica_groups=mesh['groups'=2,'tile'=4,'chan'=2,'low'=2] {'chan'}, dimensions={2}, use_global_device_ids=true | all-gather | bytes 393216 | tf_op jit(solution)/shard_map/all_gather | solution.py:106
  21.9 5.2 %fusion.17 = f32[1,16,16,256]{3,0,2,1:T(1,128)S(1)} fusion(bf16[1,16,16,512]{3,0,2,1:T(2,128)(2,1)S(1)} %all_gather.3, bf16[3,3,512,256]{3,2,1,0:T(8,128)(2,1)} %param.9), kind=kOutput, calls=%fused_computation.36 | convolution fusion | flops 554696704 | bytes 2883584 | tf_op jit(solution)/shard_map/conv_general_dilated | solution.py:27
  27.0 0.1 multiply_convert_fusion.1
  27.1 0.0 collective-permute-done
  27.1 5.2 %fusion.18 = f32[1,16,16,256]{3,0,2,1:T(1,128)S(1)} fusion(bf16[1,16,16,512]{3,0,2,1:T(2,128)(2,1)S(1)} %all_gather.3, bf16[3,3,512,256]{3,2,1,0:T(8,128)(2,1)} %collective-permute-done), kind=kOutput, calls=%fused_computation.37 | convolution fusion | flops 554696704 | bytes 2883584 | tf_op jit(solution)/shard_map/conv_general_dilated | solution.py:27
  32.3 0.0 copy-start.1
  32.3 0.1 multiply_convert_fusion
  32.4 0.1 fusion.1
  32.6 0.1 collective-permute-start.2
  32.7 1.5 %collective-permute-done.2 = bf16[1,16,16,512]{3,2,1,0:T(8,128)(2,1)S(1)} collective-permute-done((bf16[1,16,16,512]{3,2,1,0:T(8,128)(2,1)S(1)}, bf16[1,16,16,512]{3,2,1,0:T(8,128)(2,1)S(1)}, u32[]{:S(2)}, u32[]{:S(2)}) %collective-permute-start.2) | collective-permute-done | bytes 262176 | tf_op jit(solution)/shard_map/ppermute | solution.py:23
  34.2 0.1 pad_maximum_fusion
  34.3 0.0 copy-done.1
  34.3 1.0 %convolution_convert_fusion.v_ref = bf16[2,256,256]{2,1,0:T(8,128)(2,1)} fusion(bf16[2,256,512]{2,1,0:T(8,128)(2,1)S(1)} %bitcast.40, bf16[3,512,256]{2,1,0:T(8,128)(2,1)S(1)} %copy-done.1), kind=kOutput, calls=%fused_computation | convolution fusion | flops 134348800 | bytes 1048576 | tf_op jit(solution)/shard_map/dot_general | solution.py:130
  35.3 1.0 %convolution_convert_fusion.1.k_ref = bf16[2,256,256]{2,1,0:T(8,128)(2,1)} fusion(bf16[2,256,512]{2,1,0:T(8,128)(2,1)S(1)} %bitcast.41, bf16[3,512,256]{2,1,0:T(8,128)(2,1)S(1)} %copy-done.1), kind=kOutput, calls=%fused_computation.1 | convolution fusion | flops 134348800 | bytes 1048576 | tf_op jit(solution)/shard_map/dot_general | solution.py:130
  36.3 0.9 %convolution_convert_fusion.2.q_ref = bf16[2,128,256]{2,1,0:T(8,128)(2,1)} fusion(bf16[3,512,256]{2,1,0:T(8,128)(2,1)S(1)} %copy-done.1, bf16[3,16,16,512]{3,2,1,0:T(8,128)(2,1)S(1)} %pad_maximum_fusion, s32[]{:T(128)S(6)} %select_n.24, s32[]{:T(128)S(6)} %select_n.26), kind=kOutput, calls=%fused_computation.2 | convolution fusion | flops 67174400 | bytes 655368 | tf_op jit(solution)/shard_map/dot_general | solution.py:130
  37.2 3.1 %shard_map.64 = bf16[2,128,256]{2,1,0:T(8,128)(2,1)} custom-call(bf16[2,128,256]{2,1,0:T(8,128)(2,1)} %convolution_convert_fusion.2.q_ref, bf16[2,256,256]{2,1,0:T(8,128)(2,1)} %convolution_convert_fusion.1.k_ref, bf16[2,256,256]{2,1,0:T(8,128)(2,1)} %convolution_convert_fusion.v_ref), custom_call_target="tpu_custom_call" | custom-call | flops 67108864 | bytes 786432 | tf_op jit(solution)/shard_map/pallas_call | solution.py:74
  (3 shorter events, 0.1 us)
Async XLA Ops:
  0.0 1.0 %copy-start = (bf16[8,4,8,512]{3,2,1,0:T(8,128)(2,1)S(1)}, bf16[8,4,8,512]{3,2,1,0:T(8,128)(2,1)}, u32[]{:S(2)}) copy-start(bf16[8,4,8,512]{3,2,1,0:T(8,128)(2,1)} %param.6) | copy-start | bytes 786436
  0.0 27.1 %collective-permute-start = (bf16[3,3,512,256]{3,2,1,0:T(8,128)(2,1)}, bf16[3,3,512,256]{3,2,1,0:T(8,128)(2,1)}, u32[]{:S(2)}, u32[]{:S(2)}) collective-permute-start(bf16[3,3,512,256]{3,2,1,0:T(8,128)(2,1)} %param.9), channel_id=1, source_target_pairs={{0,1},{1,0},{2,3},{3,2},{4,5},{5,4},{6,7},{7,6},{8,9},{9,8},{10,11... | collective-permute-start | bytes 7077896 | tf_op jit(solution)/shard_map/ppermute | solution.py:23
  0.5 11.5 %collective-permute-start.1 = (bf16[256,256]{1,0:T(8,128)(2,1)}, bf16[256,256]{1,0:T(8,128)(2,1)S(1)}, u32[]{:S(2)}, u32[]{:S(2)}) collective-permute-start(bf16[256,256]{1,0:T(8,128)(2,1)} %param.10), channel_id=1, source_target_pairs={{0,1},{1,0},{2,3},{3,2},{4,5},{5,4},{6,7},{7,6},{8,9},{9,8},{10,11... | collective-permute-start | bytes 393224 | tf_op jit(solution)/shard_map/ppermute | solution.py:23
  1.6 12.4 %all-to-all-start = ((bf16[4,4,8,512]{3,2,1,0:T(8,128)(2,1)}), bf16[4,4,8,512]{3,2,1,0:T(8,128)(2,1)S(1)}, u32[]{:S(2)}, u32[]{:S(2)}) async-start(bf16[4,4,8,512]{3,2,1,0:T(8,128)(2,1)} %dynamic-slice_bitcast_fusion), calls=%async_computation | async-start | bytes 262144 | tf_op jit(solution)/shard_map/all_to_all | solution.py:103
  32.3 2.0 %copy-start.1 = (bf16[3,512,256]{2,1,0:T(8,128)(2,1)S(1)}, bf16[3,512,256]{2,1,0:T(8,128)(2,1)}, u32[]{:S(2)}) copy-start(bf16[3,512,256]{2,1,0:T(8,128)(2,1)} %param.11) | copy-start | bytes 2359300
  32.6 1.6 %collective-permute-start.2 = (bf16[1,16,16,512]{3,2,1,0:T(8,128)(2,1)S(1)}, bf16[1,16,16,512]{3,2,1,0:T(8,128)(2,1)S(1)}, u32[]{:S(2)}, u32[]{:S(2)}) collective-permute-start(bf16[1,16,16,512]{3,2,1,0:T(8,128)(2,1)S(1)} %fusion.1), channel_id=1, source_target_pairs={{0,1},{1,0},{2,3},{3,2},{4,5},{5,4},{6,7},{7,6},{8,9},{9,8},{10,11... | collective-permute-start | bytes 786440 | tf_op jit(solution)/shard_map/ppermute | solution.py:23

commit v11 on v6

--- a/solution.py
+++ b/solution.py
@@ -59,6 +59,12 @@
     conv_other, time_other = swap((conv_weight, time_weight), "low")
 
     start = l_idx * per_core
+    stamps = lax.dynamic_slice_in_dim(timestep, t_idx * per_tile + start, per_core, 0)
+    embedded = time_embedding(stamps)
+    mod_own = jnp.dot(embedded, time_weight.astype(jnp.float32), precision=lax.Precision.HIGHEST)
+    mod_other = jnp.dot(embedded, time_other.astype(jnp.float32), precision=lax.Precision.HIGHEST)
+
+    start = l_idx * per_core
     chans = lax.axis_size("chan")
     blocks = lax.dynamic_slice_in_dim(
         latent_map.reshape(tiles, per_tile, row_local, col_local, width), start, per_core, 1
@@ -73,7 +79,8 @@
         latent_whole = arrived.transpose(2, 0, 3, 1, 4, 5).reshape(
             per_core, tiles * row_local, chans * col_local, width
         )
-        partner = swap(inner_own, "chan")
+        inner_gated, mod_own, mod_other = lax.optimization_barrier((inner_own, mod_own, mod_other))
+        partner = swap(inner_gated, "chan")
         inner_whole = lax.dynamic_slice_in_dim(
             jnp.concatenate([inner_own, partner, inner_own], axis=2), c_idx * col_local, 2 * col_local, 2
         )
@@ -83,11 +90,6 @@
         arrived = lax.all_to_all(outgoing, "tile", split_axis=0, concat_axis=1, tiled=True)
         joined = (arrived.astype(jnp.float32) + inner_own.astype(jnp.float32)).astype(jnp.bfloat16)
         whole = lax.all_gather(joined, "chan", axis=2, tiled=True)
-
-    stamps = lax.dynamic_slice_in_dim(timestep, t_idx * per_tile + start, per_core, 0)
-    embedded = time_embedding(stamps)
-    mod_own = jnp.dot(embedded, time_weight.astype(jnp.float32), precision=lax.Precision.HIGHEST)
-    mod_other = jnp.dot(embedded, time_other.astype(jnp.float32), precision=lax.Precision.HIGHEST)
 
     def features_of(weight, modulation):
         convolved = convolve(whole, weight)

time: 29 us -> 28.1 us (0.969)
  waiting for transfers between devices: 9.03 us -> 5.39 us
  starting transfers between devices: 8.17 us -> 9.92 us
  matrix products: 4.29 us -> 5.18 us
    all_to_all x1, waiting for transfers between devices: 7.51 us -> 3.75 us  [per_device(): lax.all_to_all(outgoing.reshape((tiles * chans,) + blocks.shape[1:]), ('t...]
    all_to_all x1, starting transfers between devices: 4.88 us -> 7.25 us  [per_device(): lax.all_to_all(outgoing.reshape((tiles * chans,) + blocks.shape[1:]), ('t...]
    dot_general x1, matrix products: 0.14 us -> 1.04 us  [per_device(): jnp.dot(embedded, time_weight.astype(jnp.float32), precision=lax.Precisio...]
    dynamic_slice x1, local copies, waits for them, and re-layouts: 0.91 us -> 0.06 us  [per_device(): inner_own = lax.dynamic_slice_in_dim(inner_map, start, per_core, 0)]
    dynamic_slice x1, local copies, waits for them, and re-layouts: 0.59 us -> 1.24 us  [per_device(): lax.dynamic_slice_in_dim(timestep, t_idx * per_tile + start, per_core, 0)]
    ppermute x4, starting transfers between devices: 3.3 us -> 2.67 us  [swap(): return lax.ppermute(tree, axis, [(0, 1), (1, 0)])]
    unnamed x13 -> x11, local copies, waits for them, and re-layouts: 1.33 us -> 1.74 us
  transfers between devices with their start and end apart: 5 -> 5, of which waited for: 2 -> 3; matrix products, arithmetic and copies ran while one was open for 15% -> 18% of each run, Pallas kernels for 0% -> 0%
where the time goes in v11:
time: 28.1 us; the launch traced here: 27.8 us
  starting transfers between devices  9.92 us (35%)
  local copies, waits for them, and re-layouts  5.66 us (20%)
  waiting for transfers between devices  5.39 us (19%)
  matrix products  5.18 us (18%)
  between operations  0.89 us (3%)
  other arithmetic  0.77 us (3%)
    all_to_all x1, starting transfers between devices, per_device(): lax.all_to_all(outgoing.reshape((tiles * chans,) + blocks.shape[1:]), ('t...  7.25 us
    all_to_all x1, waiting for transfers between devices, per_device(): lax.all_to_all(outgoing.reshape((tiles * chans,) + blocks.shape[1:]), ('t...  3.75 us
    ppermute x4, starting transfers between devices, swap(): return lax.ppermute(tree, axis, [(0, 1), (1, 0)])  2.67 us
    conv_general_dilated x2, matrix products, convolve(): lax.conv_general_dilated(joined, weight, window_strides=(1, 1), padding=(...  2.25 us
    unnamed x11, local copies, waits for them, and re-layouts  1.74 us
    ppermute x4, waiting for transfers between devices, swap(): return lax.ppermute(tree, axis, [(0, 1), (1, 0)])  1.65 us
    dynamic_slice x1, local copies, waits for them, and re-layouts, per_device(): lax.dynamic_slice_in_dim(timestep, t_idx * per_tile + start, per_core, 0)  1.24 us
    dot_general x1, matrix products, per_device(): jnp.dot(embedded, time_weight.astype(jnp.float32), precision=lax.Precisio...  1.04 us
  transfers between devices with their start and end apart: 5, of which 3 were waited for; matrix products, arithmetic and copies ran while one was open for 18% of the time, Pallas kernels for 0%

profile of v11, /device:TPU:0, one launch (start us, length us, event | category | flops | bytes accessed | tf_op | source)
XLA Modules:
  0.0 27.8 jit_solution(7526167668879524129)
XLA Ops:
  0.0 0.5 %collective-permute-start.2 = (bf16[3,3,512,256]{3,2,1,0:T(8,128)(2,1)}, bf16[3,3,512,256]{3,2,1,0:T(8,128)(2,1)S(1)}, u32[]{:S(2)}, u32[]{:S(2)}) collective-permute-start(bf16[3,3,512,256]{3,2,1,0:T(8,128)(2,1)} %param.9), channel_id=1, source_target_pairs={{0,1},{1,0},{2,3},{3,2},{4,5},{5,4},{6,7},{7,6},{8,9},{9,8},{10,11... | collective-permute-start | bytes 7077896 | tf_op jit(solution)/shard_map/ppermute | solution.py:21
  0.5 0.1 collective-permute-start
  0.5 0.4 %copy-done = bf16[8,4,8,512]{3,2,1,0:T(8,128)(2,1)S(1)} copy-done((bf16[8,4,8,512]{3,2,1,0:T(8,128)(2,1)S(1)}, bf16[8,4,8,512]{3,2,1,0:T(8,128)(2,1)}, u32[]{:S(2)}) %copy-start) | copy-done | bytes 262168
  1.0 0.7 %broadcast_in_dim.7 = bf16[4,2,4,8,512]{4,3,2,1,0:T(8,128)(2,1)} broadcast(bf16[4,4,8,512]{3,2,1,0:T(8,128)(2,1)S(1)} %dynamic-slice_bitcast_fusion), dimensions={0,2,3,4} | broadcast | bytes 393216 | tf_op jit(solution)/shard_map/broadcast_in_dim | solution.py:74
  1.7 7.3 %all-to-all-start = ((bf16[8,1,4,8,512]{4,3,2,1,0:T(8,128)(2,1)}), bf16[8,1,4,8,512]{4,3,2,1,0:T(8,128)(2,1)S(1)}, u32[]{:S(2)}, u32[]{:S(2)}) async-start(bf16[8,1,4,8,512]{4,3,2,1,0:T(8,128)(2,1)} %bitcast.2), calls=%async_computation | async-start | bytes 524288 | tf_op jit(solution)/shard_map/all_to_all | solution.py:75
  8.9 1.2 %dynamic_slice.24 = s32[1]{0:T(128)} dynamic-slice(s32[8]{0:T(128)} %param.8, s32[]{:T(128)S(6)} %select_n.24), dynamic_slice_sizes={1} | dynamic-slice | bytes 12 | tf_op jit(solution)/shard_map/dynamic_slice | solution.py:62
  10.9 1.0 %fusion.34 = f32[1,256]{1,0:T(1,128)S(1)} fusion(bf16[256,256]{1,0:T(8,128)(2,1)} %param.10, f32[1,128]{1,0:T(1,128)S(1)} %get-tuple-element.13, f32[1,128]{1,0:T(1,128)S(1)} %get-tuple-element.14), kind=kOutput, calls=%fused_computation.58 | convolution fusion | flops 786688 | bytes 133120 | tf_op jit(solution)/shard_map/dot_general | solution.py:64
  12.0 0.1 fusion.33
  12.1 2.1 %collective-permute-start.1 = (bf16[1,16,8,512]{3,2,1,0:T(8,128)(2,1)S(1)}, bf16[1,16,8,512]{3,2,1,0:T(8,128)(2,1)S(1)}, u32[]{:S(2)}, u32[]{:S(2)}) collective-permute-start(bf16[1,16,8,512]{3,2,1,0:T(8,128)(2,1)S(1)} %constant_dynamic-slice_fusion.2), channel_id=1, source_target_pairs={{0,2},{2,0},{1,3},{3,1},{4,6},{6,4},{5,7},{7,5},{8,10},{10,8},{9,1... | collective-permute-start | bytes 393224 | tf_op jit(solution)/shard_map/ppermute | solution.py:21
  14.2 3.7 %all-to-all-done = bf16[8,1,4,8,512]{4,3,2,1,0:T(8,128)(2,1)S(1)} async-done(((bf16[8,1,4,8,512]{4,3,2,1,0:T(8,128)(2,1)}), bf16[8,1,4,8,512]{4,3,2,1,0:T(8,128)(2,1)S(1)}, u32[]{:S(2)}, u32[]{:S(2)}) %all-to-all-start) | async-done | bytes 262176 | tf_op jit(solution)/shard_map/all_to_all | solution.py:75
  18.1 0.1 collective-permute-done.1
  18.2 0.1 fusion.23
  18.4 0.2 copy.42
  18.6 0.2 copy.33
  18.8 0.1 slice.15
  18.9 1.2 %copy-done.3 = bf16[3,3,512,256]{3,2,1,0:T(8,128)(2,1)S(1)} copy-done((bf16[3,3,512,256]{3,2,1,0:T(8,128)(2,1)S(1)}, bf16[3,3,512,256]{3,2,1,0:T(8,128)(2,1)}, u32[]{:S(2)}) %copy-start.3) | copy-done | bytes 2359320
  20.0 1.1 %multiply_convert_fusion.1 = bf16[16,8,3,256]{3,1,2,0:T(8,128)(2,1)S(1)} fusion(bf16[3,3,512,256]{3,2,1,0:T(8,128)(2,1)S(1)} %copy-done.3, bf16[16,1,7,2,512]{4,2,3,0,1:T(8,128)(2,1)S(1)} %slice.15, bf16[16,1,8,3,512]{4,2,3,0,1:T(8,128)(2,1)S(1)} %copy.33, f32[256]{0:T(256)S(1)} %bitcast.84, pred[8,3]{0,1:T(4,128)(4,1)S(1)} %copy-done.4), kind=kOutput, calls=%fused_computation.27 | convolution fusion | flops 870875136 | bytes 3179544 | tf_op jit(solution)/shard_map/conv_general_dilated | solution.py:25
  21.1 1.1 %multiply_convert_fusion = bf16[16,8,3,256]{3,1,2,0:T(8,128)(2,1)S(1)} fusion(bf16[3,3,512,256]{3,2,1,0:T(8,128)(2,1)S(1)} %collective-permute-done.2, bf16[16,1,7,2,512]{4,2,3,0,1:T(8,128)(2,1)S(1)} %slice.15, bf16[16,1,8,3,512]{4,2,3,0,1:T(8,128)(2,1)S(1)} %copy.33, f32[256]{0:T(256)S(1)} %bitcast.83, pred[8,3]{0,1:T(4,128)(4,1)S(1)} %copy-done.4), kind=kOutput, calls=%fused_computation.26 | convolution fusion | flops 870875136 | bytes 3179544 | tf_op jit(solution)/shard_map/conv_general_dilated | solution.py:25
  22.3 0.1 copy.34
  22.5 0.2 copy.44
  22.7 0.1 collective-permute-start.3
  22.8 1.5 %collective-permute-done.3 = bf16[1,16,16,512]{3,2,1,0:T(8,128)(2,1)S(1)} collective-permute-done((bf16[1,16,16,512]{3,2,1,0:T(8,128)(2,1)S(1)}, bf16[1,16,16,512]{3,2,1,0:T(8,128)(2,1)S(1)}, u32[]{:S(2)}, u32[]{:S(2)}) %collective-permute-start.3) | collective-permute-done | bytes 262176 | tf_op jit(solution)/shard_map/ppermute | solution.py:21
  24.3 0.1 pad_maximum_fusion
  24.4 0.3 %convolution_convert_fusion = bf16[2,256,256]{1,2,0:T(8,128)(2,1)S(1)} fusion(bf16[2,256,512]{2,1,0:T(8,128)(2,1)S(1)} %bitcast.71, bf16[3,512,256]{2,1,0:T(8,128)(2,1)S(1)} %copy-done.1), kind=kOutput, calls=%fused_computation.3 | convolution fusion | flops 134348800 | bytes 1048576 | tf_op jit(solution)/shard_map/dot_general | solution.py:111
  24.8 0.3 %convolution_convert_fusion.1 = bf16[2,256,256]{1,2,0:T(8,128)(2,1)S(1)} fusion(bf16[2,256,512]{2,1,0:T(8,128)(2,1)S(1)} %bitcast.72, bf16[3,512,256]{2,1,0:T(8,128)(2,1)S(1)} %copy-done.1), kind=kOutput, calls=%fused_computation.4 | convolution fusion | flops 134348800 | bytes 1048576 | tf_op jit(solution)/shard_map/dot_general | solution.py:111
  25.2 0.2 convolution_convert_fusion.2
  25.4 0.1 copy.37
  25.5 0.4 %fusion.35 = (f32[2,4,128]{2,1,0:T(4,128)S(1)}, f32[2,4,128,256]{3,2,1,0:T(8,128)S(1)}) fusion(bf16[2,128,4,64]{1,3,2,0:T(8,128)(2,1)S(1)} %bitcast.80, bf16[2,256,4,64]{1,3,2,0:T(8,128)(2,1)S(1)} %bitcast.79), kind=kOutput, calls=%fused_computation.59 | convolution fusion | flops 34077696 | bytes 1445888 | tf_op jit(solution)/shard_map/bqhd,bkhd->bhqk/dot_general | solution.py:122
  26.0 0.4 %fusion.5 = f32[2,4,128]{2,1,0:T(4,128)S(1)} fusion(f32[2,4,128,256]{3,2,1,0:T(8,128)S(1)} %get-tuple-element.12, f32[2,4,128]{2,1,0:T(4,128)S(1)} %get-tuple-element.11), kind=kLoop, calls=%fused_computation.14 | loop fusion | flops 523264 | bytes 1056768 | tf_op jit(solution)/shard_map/reduce_sum | solution.py:126
  26.3 0.4 %fusion.4 = bf16[2,128,4,64]{1,3,2,0:T(8,128)(2,1)S(1)} fusion(bf16[2,256,4,64]{1,3,2,0:T(8,128)(2,1)S(1)} %bitcast.81, f32[2,4,128,256]{3,2,1,0:T(8,128)S(1)} %get-tuple-element.12, f32[2,4,128]{2,1,0:T(4,128)S(1)} %get-tuple-element.11, f32[2,128,4]{1,2,0:T(4,128)S(1)} %bitcast.82), kind=kOutput, calls=%fused_computation.11 | convolution fusion | flops 34209792 | bytes 1449984 | tf_op jit(solution)/shard_map/bhqk,bkhd->bqhd/dot_general | solution.py:127
  26.7 0.2 copy.39
  26.9 0.9 %reshape.109 = bf16[2,16,8,256]{3,2,1,0:T(8,128)(2,1)} reshape(bf16[2,128,4,64]{3,2,1,0:T(4,128)(2,1)S(1)} %copy.39) | data formatting | bytes 262144 | tf_op jit(solution)/shard_map/reshape | solution.py:131
  (22 shorter events, 0.4 us)
Async XLA Ops:
  0.0 1.0 %copy-start = (bf16[8,4,8,512]{3,2,1,0:T(8,128)(2,1)S(1)}, bf16[8,4,8,512]{3,2,1,0:T(8,128)(2,1)}, u32[]{:S(2)}) copy-start(bf16[8,4,8,512]{3,2,1,0:T(8,128)(2,1)} %param.6) | copy-start | bytes 786436
  0.0 11.9 %copy-start.2 = (bf16[2,16,8,512]{3,2,1,0:T(8,128)(2,1)S(1)}, bf16[2,16,8,512]{3,2,1,0:T(8,128)(2,1)}, u32[]{:S(2)}) copy-start(bf16[2,16,8,512]{3,2,1,0:T(8,128)(2,1)} %param.7) | copy-start | bytes 786436
  0.0 21.1 %collective-permute-start.2 = (bf16[3,3,512,256]{3,2,1,0:T(8,128)(2,1)}, bf16[3,3,512,256]{3,2,1,0:T(8,128)(2,1)S(1)}, u32[]{:S(2)}, u32[]{:S(2)}) collective-permute-start(bf16[3,3,512,256]{3,2,1,0:T(8,128)(2,1)} %param.9), channel_id=1, source_target_pairs={{0,1},{1,0},{2,3},{3,2},{4,5},{5,4},{6,7},{7,6},{8,9},{9,8},{10,11... | collective-permute-start | bytes 7077896 | tf_op jit(solution)/shard_map/ppermute | solution.py:21
  0.5 11.5 %collective-permute-start = (bf16[256,256]{1,0:T(8,128)(2,1)}, bf16[256,256]{1,0:T(8,128)(2,1)S(1)}, u32[]{:S(2)}, u32[]{:S(2)}) collective-permute-start(bf16[256,256]{1,0:T(8,128)(2,1)} %param.10), channel_id=1, source_target_pairs={{0,1},{1,0},{2,3},{3,2},{4,5},{5,4},{6,7},{7,6},{8,9},{9,8},{10,11... | collective-permute-start | bytes 393224 | tf_op jit(solution)/shard_map/ppermute | solution.py:21
  1.7 16.3 %all-to-all-start = ((bf16[8,1,4,8,512]{4,3,2,1,0:T(8,128)(2,1)}), bf16[8,1,4,8,512]{4,3,2,1,0:T(8,128)(2,1)S(1)}, u32[]{:S(2)}, u32[]{:S(2)}) async-start(bf16[8,1,4,8,512]{4,3,2,1,0:T(8,128)(2,1)} %bitcast.2), calls=%async_computation | async-start | bytes 524288 | tf_op jit(solution)/shard_map/all_to_all | solution.py:75
  12.1 6.1 %collective-permute-start.1 = (bf16[1,16,8,512]{3,2,1,0:T(8,128)(2,1)S(1)}, bf16[1,16,8,512]{3,2,1,0:T(8,128)(2,1)S(1)}, u32[]{:S(2)}, u32[]{:S(2)}) collective-permute-start(bf16[1,16,8,512]{3,2,1,0:T(8,128)(2,1)S(1)} %constant_dynamic-slice_fusion.2), channel_id=1, source_target_pairs={{0,2},{2,0},{1,3},{3,1},{4,6},{6,4},{5,7},{7,5},{8,10},{10,8},{9,1... | collective-permute-start | bytes 393224 | tf_op jit(solution)/shard_map/ppermute | solution.py:21
  18.3 1.7 %copy-start.3 = (bf16[3,3,512,256]{3,2,1,0:T(8,128)(2,1)S(1)}, bf16[3,3,512,256]{3,2,1,0:T(8,128)(2,1)}, u32[]{:S(2)}) copy-start(bf16[3,3,512,256]{3,2,1,0:T(8,128)(2,1)} %param.9) | copy-start | bytes 7077892
  18.4 1.7 %copy-start.4 = (pred[8,3]{0,1:T(4,128)(4,1)S(1)}, pred[8,3]{0,1:T(4,128)(4,1)}, u32[]{:S(2)}) copy-start(pred[8,3]{0,1:T(4,128)(4,1)} %constant.69) | copy-start | bytes 76
  22.7 1.8 %copy-start.1 = (bf16[3,512,256]{2,1,0:T(8,128)(2,1)S(1)}, bf16[3,512,256]{2,1,0:T(8,128)(2,1)}, u32[]{:S(2)}) copy-start(bf16[3,512,256]{2,1,0:T(8,128)(2,1)} %param.11) | copy-start | bytes 2359300
  22.7 1.6 %collective-permute-start.3 = (bf16[1,16,16,512]{3,2,1,0:T(8,128)(2,1)S(1)}, bf16[1,16,16,512]{3,2,1,0:T(8,128)(2,1)S(1)}, u32[]{:S(2)}, u32[]{:S(2)}) collective-permute-start(bf16[1,16,16,512]{3,2,1,0:T(8,128)(2,1)S(1)} %bitcast.77), channel_id=1, source_target_pairs={{0,1},{1,0},{2,3},{3,2},{4,5},{5,4},{6,7},{7,6},{8,9},{9,8},{10,11... | collective-permute-start | bytes 786440 | tf_op jit(solution)/shard_map/ppermute | solution.py:21

commit v12 on v11

--- a/solution.py
+++ b/solution.py
@@ -59,7 +59,9 @@
     conv_other, time_other = swap((conv_weight, time_weight), "low")
 
     start = l_idx * per_core
-    stamps = lax.dynamic_slice_in_dim(timestep, t_idx * per_tile + start, per_core, 0)
+    picks = t_idx * per_tile + start + jnp.arange(per_core)
+    chosen = jnp.arange(samples)[None, :] == picks[:, None]
+    stamps = jnp.sum(jnp.where(chosen, timestep[None, :], 0), axis=1)
     embedded = time_embedding(stamps)
     mod_own = jnp.dot(embedded, time_weight.astype(jnp.float32), precision=lax.Precision.HIGHEST)
     mod_other = jnp.dot(embedded, time_other.astype(jnp.float32), precision=lax.Precision.HIGHEST)

time: 28.1 us -> 28.2 us (level)
  other arithmetic: 0.77 us -> 2.06 us
  local copies, waits for them, and re-layouts: 5.66 us -> 4.41 us
    reduce_sum x0 -> x1, other arithmetic: none -> 1.29 us  [per_device(): stamps = jnp.sum(jnp.where(chosen, timestep[None, :], 0), axis=1)]
    dynamic_slice x1 -> x0, local copies, waits for them, and re-layouts: 1.24 us -> none  [per_device(): lax.dynamic_slice_in_dim(timestep, t_idx * per_tile + start, per_core, 0)]
where the time goes in v12:
time: 28.2 us; the launch traced here: 27.9 us
  starting transfers between devices  9.92 us (35%)
  waiting for transfers between devices  5.39 us (19%)
  matrix products  5.18 us (18%)
  local copies, waits for them, and re-layouts  4.41 us (16%)
  other arithmetic  2.06 us (7%)
  between operations  0.89 us (3%)
    all_to_all x1, starting transfers between devices, per_device(): lax.all_to_all(outgoing.reshape((tiles * chans,) + blocks.shape[1:]), ('t...  7.25 us
    all_to_all x1, waiting for transfers between devices, per_device(): lax.all_to_all(outgoing.reshape((tiles * chans,) + blocks.shape[1:]), ('t...  3.69 us
    ppermute x4, starting transfers between devices, swap(): return lax.ppermute(tree, axis, [(0, 1), (1, 0)])  2.67 us
    conv_general_dilated x2, matrix products, convolve(): lax.conv_general_dilated(joined, weight, window_strides=(1, 1), padding=(...  2.25 us
    unnamed x11, local copies, waits for them, and re-layouts  1.74 us
    ppermute x4, waiting for transfers between devices, swap(): return lax.ppermute(tree, axis, [(0, 1), (1, 0)])  1.7 us
    reduce_sum x1, other arithmetic, per_device(): stamps = jnp.sum(jnp.where(chosen, timestep[None, :], 0), axis=1)  1.29 us
    dot_general x1, matrix products, per_device(): jnp.dot(embedded, time_weight.astype(jnp.float32), precision=lax.Precisio...  1.04 us
  transfers between devices with their start and end apart: 5, of which 3 were waited for; matrix products, arithmetic and copies ran while one was open for 18% of the time, Pallas kernels for 0%

profile of v12, /device:TPU:0, one launch (start us, length us, event | category | flops | bytes accessed | tf_op | source)
XLA Modules:
  0.0 27.9 jit_solution(2421367587695052075)
XLA Ops:
  0.0 0.5 %collective-permute-start.2 = (bf16[3,3,512,256]{3,2,1,0:T(8,128)(2,1)}, bf16[3,3,512,256]{3,2,1,0:T(8,128)(2,1)S(1)}, u32[]{:S(2)}, u32[]{:S(2)}) collective-permute-start(bf16[3,3,512,256]{3,2,1,0:T(8,128)(2,1)} %param.9), channel_id=1, source_target_pairs={{0,1},{1,0},{2,3},{3,2},{4,5},{5,4},{6,7},{7,6},{8,9},{9,8},{10,11... | collective-permute-start | bytes 7077896 | tf_op jit(solution)/shard_map/ppermute | solution.py:21
  0.5 0.1 collective-permute-start
  0.5 0.4 %copy-done = bf16[8,4,8,512]{3,2,1,0:T(8,128)(2,1)S(1)} copy-done((bf16[8,4,8,512]{3,2,1,0:T(8,128)(2,1)S(1)}, bf16[8,4,8,512]{3,2,1,0:T(8,128)(2,1)}, u32[]{:S(2)}) %copy-start) | copy-done | bytes 262168
  1.0 0.7 %broadcast_in_dim.11 = bf16[4,2,4,8,512]{4,3,2,1,0:T(8,128)(2,1)} broadcast(bf16[4,4,8,512]{3,2,1,0:T(8,128)(2,1)S(1)} %dynamic-slice_bitcast_fusion), dimensions={0,2,3,4} | broadcast | bytes 393216 | tf_op jit(solution)/shard_map/broadcast_in_dim | solution.py:76
  1.7 7.3 %all-to-all-start = ((bf16[8,1,4,8,512]{4,3,2,1,0:T(8,128)(2,1)}), bf16[8,1,4,8,512]{4,3,2,1,0:T(8,128)(2,1)S(1)}, u32[]{:S(2)}, u32[]{:S(2)}) async-start(bf16[8,1,4,8,512]{4,3,2,1,0:T(8,128)(2,1)} %bitcast.2), calls=%async_computation | async-start | bytes 524288 | tf_op jit(solution)/shard_map/all_to_all | solution.py:77
  8.9 1.3 %fusion.25 = s32[]{:T(128)} fusion(s32[8]{0:T(128)} %param.8, s32[]{:T(128)S(6)} %add.56), kind=kLoop, calls=%fused_computation.47 | loop fusion | flops 23 | bytes 40 | tf_op jit(solution)/shard_map/reduce_sum | solution.py:64
  10.9 1.0 %fusion.35 = f32[1,256]{1,0:T(1,128)S(1)} fusion(bf16[256,256]{1,0:T(8,128)(2,1)} %param.10, f32[1,128]{1,0:T(1,128)S(1)} %get-tuple-element.13, f32[1,128]{1,0:T(1,128)S(1)} %get-tuple-element.14), kind=kOutput, calls=%fused_computation.60 | convolution fusion | flops 786688 | bytes 133120 | tf_op jit(solution)/shard_map/dot_general | solution.py:66
  12.1 0.1 fusion.34
  12.2 2.1 %collective-permute-start.1 = (bf16[1,16,8,512]{3,2,1,0:T(8,128)(2,1)S(1)}, bf16[1,16,8,512]{3,2,1,0:T(8,128)(2,1)S(1)}, u32[]{:S(2)}, u32[]{:S(2)}) collective-permute-start(bf16[1,16,8,512]{3,2,1,0:T(8,128)(2,1)S(1)} %constant_dynamic-slice_fusion.2), channel_id=1, source_target_pairs={{0,2},{2,0},{1,3},{3,1},{4,6},{6,4},{5,7},{7,5},{8,10},{10,8},{9,1... | collective-permute-start | bytes 393224 | tf_op jit(solution)/shard_map/ppermute | solution.py:21
  14.3 3.7 %all-to-all-done = bf16[8,1,4,8,512]{4,3,2,1,0:T(8,128)(2,1)S(1)} async-done(((bf16[8,1,4,8,512]{4,3,2,1,0:T(8,128)(2,1)}), bf16[8,1,4,8,512]{4,3,2,1,0:T(8,128)(2,1)S(1)}, u32[]{:S(2)}, u32[]{:S(2)}) %all-to-all-start) | async-done | bytes 262176 | tf_op jit(solution)/shard_map/all_to_all | solution.py:77
  18.1 0.2 collective-permute-done.1
  18.2 0.1 fusion.23
  18.4 0.2 copy.42
  18.6 0.2 copy.33
  18.8 0.1 slice.15
  18.9 1.2 %copy-done.3 = bf16[3,3,512,256]{3,2,1,0:T(8,128)(2,1)S(1)} copy-done((bf16[3,3,512,256]{3,2,1,0:T(8,128)(2,1)S(1)}, bf16[3,3,512,256]{3,2,1,0:T(8,128)(2,1)}, u32[]{:S(2)}) %copy-start.3) | copy-done | bytes 2359320
  20.1 1.1 %multiply_convert_fusion.1 = bf16[16,8,3,256]{3,1,2,0:T(8,128)(2,1)S(1)} fusion(bf16[3,3,512,256]{3,2,1,0:T(8,128)(2,1)S(1)} %copy-done.3, bf16[16,1,7,2,512]{4,2,3,0,1:T(8,128)(2,1)S(1)} %slice.15, bf16[16,1,8,3,512]{4,2,3,0,1:T(8,128)(2,1)S(1)} %copy.33, f32[256]{0:T(256)S(1)} %bitcast.83, pred[8,3]{0,1:T(4,128)(4,1)S(1)} %copy-done.4), kind=kOutput, calls=%fused_computation.27 | convolution fusion | flops 870875136 | bytes 3179544 | tf_op jit(solution)/shard_map/conv_general_dilated | solution.py:25
  21.2 1.1 %multiply_convert_fusion = bf16[16,8,3,256]{3,1,2,0:T(8,128)(2,1)S(1)} fusion(bf16[3,3,512,256]{3,2,1,0:T(8,128)(2,1)S(1)} %collective-permute-done.2, bf16[16,1,7,2,512]{4,2,3,0,1:T(8,128)(2,1)S(1)} %slice.15, bf16[16,1,8,3,512]{4,2,3,0,1:T(8,128)(2,1)S(1)} %copy.33, f32[256]{0:T(256)S(1)} %bitcast.82, pred[8,3]{0,1:T(4,128)(4,1)S(1)} %copy-done.4), kind=kOutput, calls=%fused_computation.26 | convolution fusion | flops 870875136 | bytes 3179544 | tf_op jit(solution)/shard_map/conv_general_dilated | solution.py:25
  22.4 0.1 copy.34
  22.6 0.2 copy.44
  22.7 0.1 collective-permute-start.3
  22.8 1.5 %collective-permute-done.3 = bf16[1,16,16,512]{3,2,1,0:T(8,128)(2,1)S(1)} collective-permute-done((bf16[1,16,16,512]{3,2,1,0:T(8,128)(2,1)S(1)}, bf16[1,16,16,512]{3,2,1,0:T(8,128)(2,1)S(1)}, u32[]{:S(2)}, u32[]{:S(2)}) %collective-permute-start.3) | collective-permute-done | bytes 262176 | tf_op jit(solution)/shard_map/ppermute | solution.py:21
  24.3 0.1 pad_maximum_fusion
  24.5 0.3 %convolution_convert_fusion = bf16[2,256,256]{1,2,0:T(8,128)(2,1)S(1)} fusion(bf16[2,256,512]{2,1,0:T(8,128)(2,1)S(1)} %bitcast.70, bf16[3,512,256]{2,1,0:T(8,128)(2,1)S(1)} %copy-done.1), kind=kOutput, calls=%fused_computation.3 | convolution fusion | flops 134348800 | bytes 1048576 | tf_op jit(solution)/shard_map/dot_general | solution.py:113
  24.8 0.3 %convolution_convert_fusion.1 = bf16[2,256,256]{1,2,0:T(8,128)(2,1)S(1)} fusion(bf16[2,256,512]{2,1,0:T(8,128)(2,1)S(1)} %bitcast.71, bf16[3,512,256]{2,1,0:T(8,128)(2,1)S(1)} %copy-done.1), kind=kOutput, calls=%fused_computation.4 | convolution fusion | flops 134348800 | bytes 1048576 | tf_op jit(solution)/shard_map/dot_general | solution.py:113
  25.2 0.2 convolution_convert_fusion.2
  25.4 0.1 copy.37
  25.6 0.4 %fusion.36 = (f32[2,4,128]{2,1,0:T(4,128)S(1)}, f32[2,4,128,256]{3,2,1,0:T(8,128)S(1)}) fusion(bf16[2,128,4,64]{1,3,2,0:T(8,128)(2,1)S(1)} %bitcast.79, bf16[2,256,4,64]{1,3,2,0:T(8,128)(2,1)S(1)} %bitcast.78), kind=kOutput, calls=%fused_computation.61 | convolution fusion | flops 34077696 | bytes 1445888 | tf_op jit(solution)/shard_map/bqhd,bkhd->bhqk/dot_general | solution.py:124
  26.0 0.4 %fusion.5 = f32[2,4,128]{2,1,0:T(4,128)S(1)} fusion(f32[2,4,128,256]{3,2,1,0:T(8,128)S(1)} %get-tuple-element.12, f32[2,4,128]{2,1,0:T(4,128)S(1)} %get-tuple-element.11), kind=kLoop, calls=%fused_computation.14 | loop fusion | flops 523264 | bytes 1056768 | tf_op jit(solution)/shard_map/reduce_sum | solution.py:128
  26.4 0.4 %fusion.4 = bf16[2,128,4,64]{1,3,2,0:T(8,128)(2,1)S(1)} fusion(bf16[2,256,4,64]{1,3,2,0:T(8,128)(2,1)S(1)} %bitcast.80, f32[2,4,128,256]{3,2,1,0:T(8,128)S(1)} %get-tuple-element.12, f32[2,4,128]{2,1,0:T(4,128)S(1)} %get-tuple-element.11, f32[2,128,4]{1,2,0:T(4,128)S(1)} %bitcast.81), kind=kOutput, calls=%fused_computation.11 | convolution fusion | flops 34209792 | bytes 1449984 | tf_op jit(solution)/shard_map/bhqk,bkhd->bqhd/dot_general | solution.py:129
  26.8 0.2 copy.39
  27.0 0.9 %reshape.118 = bf16[2,16,8,256]{3,2,1,0:T(8,128)(2,1)} reshape(bf16[2,128,4,64]{3,2,1,0:T(4,128)(2,1)S(1)} %copy.39) | data formatting | bytes 262144 | tf_op jit(solution)/shard_map/reshape | solution.py:133
  (22 shorter events, 0.4 us)
Async XLA Ops:
  0.0 1.0 %copy-start = (bf16[8,4,8,512]{3,2,1,0:T(8,128)(2,1)S(1)}, bf16[8,4,8,512]{3,2,1,0:T(8,128)(2,1)}, u32[]{:S(2)}) copy-start(bf16[8,4,8,512]{3,2,1,0:T(8,128)(2,1)} %param.6) | copy-start | bytes 786436
  0.0 12.0 %copy-start.2 = (bf16[2,16,8,512]{3,2,1,0:T(8,128)(2,1)S(1)}, bf16[2,16,8,512]{3,2,1,0:T(8,128)(2,1)}, u32[]{:S(2)}) copy-start(bf16[2,16,8,512]{3,2,1,0:T(8,128)(2,1)} %param.7) | copy-start | bytes 786436
  0.0 21.2 %collective-permute-start.2 = (bf16[3,3,512,256]{3,2,1,0:T(8,128)(2,1)}, bf16[3,3,512,256]{3,2,1,0:T(8,128)(2,1)S(1)}, u32[]{:S(2)}, u32[]{:S(2)}) collective-permute-start(bf16[3,3,512,256]{3,2,1,0:T(8,128)(2,1)} %param.9), channel_id=1, source_target_pairs={{0,1},{1,0},{2,3},{3,2},{4,5},{5,4},{6,7},{7,6},{8,9},{9,8},{10,11... | collective-permute-start | bytes 7077896 | tf_op jit(solution)/shard_map/ppermute | solution.py:21
  0.5 11.6 %collective-permute-start = (bf16[256,256]{1,0:T(8,128)(2,1)}, bf16[256,256]{1,0:T(8,128)(2,1)S(1)}, u32[]{:S(2)}, u32[]{:S(2)}) collective-permute-start(bf16[256,256]{1,0:T(8,128)(2,1)} %param.10), channel_id=1, source_target_pairs={{0,1},{1,0},{2,3},{3,2},{4,5},{5,4},{6,7},{7,6},{8,9},{9,8},{10,11... | collective-permute-start | bytes 393224 | tf_op jit(solution)/shard_map/ppermute | solution.py:21
  1.7 16.3 %all-to-all-start = ((bf16[8,1,4,8,512]{4,3,2,1,0:T(8,128)(2,1)}), bf16[8,1,4,8,512]{4,3,2,1,0:T(8,128)(2,1)S(1)}, u32[]{:S(2)}, u32[]{:S(2)}) async-start(bf16[8,1,4,8,512]{4,3,2,1,0:T(8,128)(2,1)} %bitcast.2), calls=%async_computation | async-start | bytes 524288 | tf_op jit(solution)/shard_map/all_to_all | solution.py:77
  12.2 6.1 %collective-permute-start.1 = (bf16[1,16,8,512]{3,2,1,0:T(8,128)(2,1)S(1)}, bf16[1,16,8,512]{3,2,1,0:T(8,128)(2,1)S(1)}, u32[]{:S(2)}, u32[]{:S(2)}) collective-permute-start(bf16[1,16,8,512]{3,2,1,0:T(8,128)(2,1)S(1)} %constant_dynamic-slice_fusion.2), channel_id=1, source_target_pairs={{0,2},{2,0},{1,3},{3,1},{4,6},{6,4},{5,7},{7,5},{8,10},{10,8},{9,1... | collective-permute-start | bytes 393224 | tf_op jit(solution)/shard_map/ppermute | solution.py:21
  18.4 1.7 %copy-start.3 = (bf16[3,3,512,256]{3,2,1,0:T(8,128)(2,1)S(1)}, bf16[3,3,512,256]{3,2,1,0:T(8,128)(2,1)}, u32[]{:S(2)}) copy-start(bf16[3,3,512,256]{3,2,1,0:T(8,128)(2,1)} %param.9) | copy-start | bytes 7077892
  18.4 1.7 %copy-start.4 = (pred[8,3]{0,1:T(4,128)(4,1)S(1)}, pred[8,3]{0,1:T(4,128)(4,1)}, u32[]{:S(2)}) copy-start(pred[8,3]{0,1:T(4,128)(4,1)} %constant.69) | copy-start | bytes 76
  22.7 1.8 %copy-start.1 = (bf16[3,512,256]{2,1,0:T(8,128)(2,1)S(1)}, bf16[3,512,256]{2,1,0:T(8,128)(2,1)}, u32[]{:S(2)}) copy-start(bf16[3,512,256]{2,1,0:T(8,128)(2,1)} %param.11) | copy-start | bytes 2359300
  22.7 1.6 %collective-permute-start.3 = (bf16[1,16,16,512]{3,2,1,0:T(8,128)(2,1)S(1)}, bf16[1,16,16,512]{3,2,1,0:T(8,128)(2,1)S(1)}, u32[]{:S(2)}, u32[]{:S(2)}) collective-permute-start(bf16[1,16,16,512]{3,2,1,0:T(8,128)(2,1)S(1)} %bitcast.76), channel_id=1, source_target_pairs={{0,1},{1,0},{2,3},{3,2},{4,5},{5,4},{6,7},{7,6},{8,9},{9,8},{10,11... | collective-permute-start | bytes 786440 | tf_op jit(solution)/shard_map/ppermute | solution.py:21

commit v13 on v11

--- a/solution.py
+++ b/solution.py
@@ -71,12 +71,12 @@
     )
     inner_own = lax.dynamic_slice_in_dim(inner_map, start, per_core, 0)
     if tiles * chans <= 8 and chans == 2:
-        outgoing = jnp.broadcast_to(blocks[:, None], (tiles, chans) + blocks.shape[1:])
+        outgoing = jnp.broadcast_to(blocks[None], (chans,) + blocks.shape)
         arrived = lax.all_to_all(
-            outgoing.reshape((tiles * chans,) + blocks.shape[1:]), ("tile", "chan"), 0, 0, tiled=True
+            outgoing.reshape((chans * tiles,) + blocks.shape[1:]), ("chan", "tile"), 0, 0, tiled=True
         )
-        arrived = arrived.reshape(tiles, chans, per_core, row_local, col_local, width)
-        latent_whole = arrived.transpose(2, 0, 3, 1, 4, 5).reshape(
+        arrived = arrived.reshape(chans, tiles, per_core, row_local, col_local, width)
+        latent_whole = arrived.transpose(2, 1, 3, 0, 4, 5).reshape(
             per_core, tiles * row_local, chans * col_local, width
         )
         inner_gated, mod_own, mod_other = lax.optimization_barrier((inner_own, mod_own, mod_other))

time: 28.1 us -> 28.8 us (1.025)
  waiting for transfers between devices: 5.39 us -> 6.06 us
    all_to_all x1, waiting for transfers between devices: 3.75 us -> 4.54 us  [per_device(): lax.all_to_all(outgoing.reshape((chans * tiles,) + blocks.shape[1:]), ('c...]
  transfers between devices with their start and end apart: 5 -> 5, of which waited for: 3 -> 2; matrix products, arithmetic and copies ran while one was open for 18% -> 18% of each run, Pallas kernels for 0% -> 0%
where the time goes in v13:
time: 28.8 us; the launch traced here: 28.5 us
  starting transfers between devices  9.92 us (34%)
  waiting for transfers between devices  6.06 us (21%)
  local copies, waits for them, and re-layouts  5.66 us (20%)
  matrix products  5.18 us (18%)
  between operations  0.9 us (3%)
  other arithmetic  0.78 us (3%)
    all_to_all x1, starting transfers between devices, per_device(): lax.all_to_all(outgoing.reshape((chans * tiles,) + blocks.shape[1:]), ('c...  7.25 us
    all_to_all x1, waiting for transfers between devices, per_device(): lax.all_to_all(outgoing.reshape((chans * tiles,) + blocks.shape[1:]), ('c...  4.54 us
    ppermute x4, starting transfers between devices, swap(): return lax.ppermute(tree, axis, [(0, 1), (1, 0)])  2.67 us
    conv_general_dilated x2, matrix products, convolve(): lax.conv_general_dilated(joined, weight, window_strides=(1, 1), padding=(...  2.25 us
    unnamed x11, local copies, waits for them, and re-layouts  1.74 us
    ppermute x4, waiting for transfers between devices, swap(): return lax.ppermute(tree, axis, [(0, 1), (1, 0)])  1.52 us
    dynamic_slice x1, local copies, waits for them, and re-layouts, per_device(): lax.dynamic_slice_in_dim(timestep, t_idx * per_tile + start, per_core, 0)  1.24 us
    dot_general x1, matrix products, per_device(): jnp.dot(embedded, time_weight.astype(jnp.float32), precision=lax.Precisio...  1.04 us
  transfers between devices with their start and end apart: 5, of which 2 were waited for; matrix products, arithmetic and copies ran while one was open for 18% of the time, Pallas kernels for 0%

profile of v13, /device:TPU:0, one launch (start us, length us, event | category | flops | bytes accessed | tf_op | source)
XLA Modules:
  0.0 28.5 jit_solution(10846059159388647672)
XLA Ops:
  0.0 0.5 %collective-permute-start.2 = (bf16[3,3,512,256]{3,2,1,0:T(8,128)(2,1)}, bf16[3,3,512,256]{3,2,1,0:T(8,128)(2,1)S(1)}, u32[]{:S(2)}, u32[]{:S(2)}) collective-permute-start(bf16[3,3,512,256]{3,2,1,0:T(8,128)(2,1)} %param.9), channel_id=1, source_target_pairs={{0,1},{1,0},{2,3},{3,2},{4,5},{5,4},{6,7},{7,6},{8,9},{9,8},{10,11... | collective-permute-start | bytes 7077896 | tf_op jit(solution)/shard_map/ppermute | solution.py:21
  0.5 0.1 collective-permute-start
  0.5 0.4 %copy-done = bf16[8,4,8,512]{3,2,1,0:T(8,128)(2,1)S(1)} copy-done((bf16[8,4,8,512]{3,2,1,0:T(8,128)(2,1)S(1)}, bf16[8,4,8,512]{3,2,1,0:T(8,128)(2,1)}, u32[]{:S(2)}) %copy-start) | copy-done | bytes 262168
  1.0 0.7 %broadcast_in_dim.7 = bf16[2,4,4,8,512]{4,3,2,1,0:T(8,128)(2,1)} broadcast(bf16[4,4,8,512]{3,2,1,0:T(8,128)(2,1)S(1)} %dynamic-slice_bitcast_fusion), dimensions={1,2,3,4} | broadcast | bytes 393216 | tf_op jit(solution)/shard_map/broadcast_in_dim | solution.py:74
  1.7 7.3 %all-to-all-start = ((bf16[8,1,4,8,512]{4,3,2,1,0:T(8,128)(2,1)}), bf16[8,1,4,8,512]{4,3,2,1,0:T(8,128)(2,1)S(1)}, u32[]{:S(2)}, u32[]{:S(2)}) async-start(bf16[8,1,4,8,512]{4,3,2,1,0:T(8,128)(2,1)} %bitcast.2), calls=%async_computation | async-start | bytes 524288 | tf_op jit(solution)/shard_map/all_to_all | solution.py:75
  8.9 1.2 %dynamic_slice.24 = s32[1]{0:T(128)} dynamic-slice(s32[8]{0:T(128)} %param.8, s32[]{:T(128)S(6)} %select_n.24), dynamic_slice_sizes={1} | dynamic-slice | bytes 12 | tf_op jit(solution)/shard_map/dynamic_slice | solution.py:62
  10.9 1.0 %fusion.34 = f32[1,256]{1,0:T(1,128)S(1)} fusion(bf16[256,256]{1,0:T(8,128)(2,1)} %param.10, f32[1,128]{1,0:T(1,128)S(1)} %get-tuple-element.13, f32[1,128]{1,0:T(1,128)S(1)} %get-tuple-element.14), kind=kOutput, calls=%fused_computation.58 | convolution fusion | flops 786688 | bytes 133120 | tf_op jit(solution)/shard_map/dot_general | solution.py:64
  11.9 0.1 constant_dynamic-slice_fusion.2
  12.0 0.1 fusion.33
  12.1 2.1 %collective-permute-start.1 = (bf16[1,16,8,512]{3,2,1,0:T(8,128)(2,1)S(1)}, bf16[1,16,8,512]{3,2,1,0:T(8,128)(2,1)S(1)}, u32[]{:S(2)}, u32[]{:S(2)}) collective-permute-start(bf16[1,16,8,512]{3,2,1,0:T(8,128)(2,1)S(1)} %constant_dynamic-slice_fusion.2), channel_id=1, source_target_pairs={{0,2},{2,0},{1,3},{3,1},{4,6},{6,4},{5,7},{7,5},{8,10},{10,8},{9,1... | collective-permute-start | bytes 393224 | tf_op jit(solution)/shard_map/ppermute | solution.py:21
  14.2 4.5 %all-to-all-done = bf16[8,1,4,8,512]{4,3,2,1,0:T(8,128)(2,1)S(1)} async-done(((bf16[8,1,4,8,512]{4,3,2,1,0:T(8,128)(2,1)}), bf16[8,1,4,8,512]{4,3,2,1,0:T(8,128)(2,1)S(1)}, u32[]{:S(2)}, u32[]{:S(2)}) %all-to-all-start) | async-done | bytes 262176 | tf_op jit(solution)/shard_map/all_to_all | solution.py:75
  18.9 0.2 fusion.23
  19.1 0.2 copy.42
  19.3 0.2 copy.33
  19.5 0.1 slice.15
  19.6 1.2 %copy-done.3 = bf16[3,3,512,256]{3,2,1,0:T(8,128)(2,1)S(1)} copy-done((bf16[3,3,512,256]{3,2,1,0:T(8,128)(2,1)S(1)}, bf16[3,3,512,256]{3,2,1,0:T(8,128)(2,1)}, u32[]{:S(2)}) %copy-start.3) | copy-done | bytes 2359320
  20.7 1.1 %multiply_convert_fusion.1 = bf16[16,8,3,256]{3,1,2,0:T(8,128)(2,1)S(1)} fusion(bf16[3,3,512,256]{3,2,1,0:T(8,128)(2,1)S(1)} %copy-done.3, bf16[16,1,7,2,512]{4,2,3,0,1:T(8,128)(2,1)S(1)} %slice.15, bf16[16,1,8,3,512]{4,2,3,0,1:T(8,128)(2,1)S(1)} %copy.33, f32[256]{0:T(256)S(1)} %bitcast.84, pred[8,3]{0,1:T(4,128)(4,1)S(1)} %copy-done.4), kind=kOutput, calls=%fused_computation.27 | convolution fusion | flops 870875136 | bytes 3179544 | tf_op jit(solution)/shard_map/conv_general_dilated | solution.py:25
  21.8 1.1 %multiply_convert_fusion = bf16[16,8,3,256]{3,1,2,0:T(8,128)(2,1)S(1)} fusion(bf16[3,3,512,256]{3,2,1,0:T(8,128)(2,1)S(1)} %collective-permute-done.2, bf16[16,1,7,2,512]{4,2,3,0,1:T(8,128)(2,1)S(1)} %slice.15, bf16[16,1,8,3,512]{4,2,3,0,1:T(8,128)(2,1)S(1)} %copy.33, f32[256]{0:T(256)S(1)} %bitcast.83, pred[8,3]{0,1:T(4,128)(4,1)S(1)} %copy-done.4), kind=kOutput, calls=%fused_computation.26 | convolution fusion | flops 870875136 | bytes 3179544 | tf_op jit(solution)/shard_map/conv_general_dilated | solution.py:25
  23.0 0.1 copy.34
  23.2 0.2 copy.44
  23.4 0.1 collective-permute-start.3
  23.5 1.5 %collective-permute-done.3 = bf16[1,16,16,512]{3,2,1,0:T(8,128)(2,1)S(1)} collective-permute-done((bf16[1,16,16,512]{3,2,1,0:T(8,128)(2,1)S(1)}, bf16[1,16,16,512]{3,2,1,0:T(8,128)(2,1)S(1)}, u32[]{:S(2)}, u32[]{:S(2)}) %collective-permute-start.3) | collective-permute-done | bytes 262176 | tf_op jit(solution)/shard_map/ppermute | solution.py:21
  25.0 0.1 pad_maximum_fusion
  25.1 0.3 %convolution_convert_fusion = bf16[2,256,256]{1,2,0:T(8,128)(2,1)S(1)} fusion(bf16[2,256,512]{2,1,0:T(8,128)(2,1)S(1)} %bitcast.71, bf16[3,512,256]{2,1,0:T(8,128)(2,1)S(1)} %copy-done.1), kind=kOutput, calls=%fused_computation.3 | convolution fusion | flops 134348800 | bytes 1048576 | tf_op jit(solution)/shard_map/dot_general | solution.py:111
  25.5 0.3 %convolution_convert_fusion.1 = bf16[2,256,256]{1,2,0:T(8,128)(2,1)S(1)} fusion(bf16[2,256,512]{2,1,0:T(8,128)(2,1)S(1)} %bitcast.72, bf16[3,512,256]{2,1,0:T(8,128)(2,1)S(1)} %copy-done.1), kind=kOutput, calls=%fused_computation.4 | convolution fusion | flops 134348800 | bytes 1048576 | tf_op jit(solution)/shard_map/dot_general | solution.py:111
  25.8 0.2 convolution_convert_fusion.2
  26.1 0.1 copy.37
  26.2 0.4 %fusion.35 = (f32[2,4,128]{2,1,0:T(4,128)S(1)}, f32[2,4,128,256]{3,2,1,0:T(8,128)S(1)}) fusion(bf16[2,128,4,64]{1,3,2,0:T(8,128)(2,1)S(1)} %bitcast.80, bf16[2,256,4,64]{1,3,2,0:T(8,128)(2,1)S(1)} %bitcast.79), kind=kOutput, calls=%fused_computation.59 | convolution fusion | flops 34077696 | bytes 1445888 | tf_op jit(solution)/shard_map/bqhd,bkhd->bhqk/dot_general | solution.py:122
  26.6 0.4 %fusion.5 = f32[2,4,128]{2,1,0:T(4,128)S(1)} fusion(f32[2,4,128,256]{3,2,1,0:T(8,128)S(1)} %get-tuple-element.12, f32[2,4,128]{2,1,0:T(4,128)S(1)} %get-tuple-element.11), kind=kLoop, calls=%fused_computation.14 | loop fusion | flops 523264 | bytes 1056768 | tf_op jit(solution)/shard_map/reduce_sum | solution.py:126
  27.0 0.4 %fusion.4 = bf16[2,128,4,64]{1,3,2,0:T(8,128)(2,1)S(1)} fusion(bf16[2,256,4,64]{1,3,2,0:T(8,128)(2,1)S(1)} %bitcast.81, f32[2,4,128,256]{3,2,1,0:T(8,128)S(1)} %get-tuple-element.12, f32[2,4,128]{2,1,0:T(4,128)S(1)} %get-tuple-element.11, f32[2,128,4]{1,2,0:T(4,128)S(1)} %bitcast.82), kind=kOutput, calls=%fused_computation.11 | convolution fusion | flops 34209792 | bytes 1449984 | tf_op jit(solution)/shard_map/bhqk,bkhd->bqhd/dot_general | solution.py:127
  27.4 0.2 copy.39
  27.6 0.9 %reshape.109 = bf16[2,16,8,256]{3,2,1,0:T(8,128)(2,1)} reshape(bf16[2,128,4,64]{3,2,1,0:T(4,128)(2,1)S(1)} %copy.39) | data formatting | bytes 262144 | tf_op jit(solution)/shard_map/reshape | solution.py:131
  (22 shorter events, 0.4 us)
Async XLA Ops:
  0.0 1.0 %copy-start = (bf16[8,4,8,512]{3,2,1,0:T(8,128)(2,1)S(1)}, bf16[8,4,8,512]{3,2,1,0:T(8,128)(2,1)}, u32[]{:S(2)}) copy-start(bf16[8,4,8,512]{3,2,1,0:T(8,128)(2,1)} %param.6) | copy-start | bytes 786436
  0.0 11.9 %copy-start.2 = (bf16[2,16,8,512]{3,2,1,0:T(8,128)(2,1)S(1)}, bf16[2,16,8,512]{3,2,1,0:T(8,128)(2,1)}, u32[]{:S(2)}) copy-start(bf16[2,16,8,512]{3,2,1,0:T(8,128)(2,1)} %param.7) | copy-start | bytes 786436
  0.0 21.8 %collective-permute-start.2 = (bf16[3,3,512,256]{3,2,1,0:T(8,128)(2,1)}, bf16[3,3,512,256]{3,2,1,0:T(8,128)(2,1)S(1)}, u32[]{:S(2)}, u32[]{:S(2)}) collective-permute-start(bf16[3,3,512,256]{3,2,1,0:T(8,128)(2,1)} %param.9), channel_id=1, source_target_pairs={{0,1},{1,0},{2,3},{3,2},{4,5},{5,4},{6,7},{7,6},{8,9},{9,8},{10,11... | collective-permute-start | bytes 7077896 | tf_op jit(solution)/shard_map/ppermute | solution.py:21
  0.5 11.5 %collective-permute-start = (bf16[256,256]{1,0:T(8,128)(2,1)}, bf16[256,256]{1,0:T(8,128)(2,1)S(1)}, u32[]{:S(2)}, u32[]{:S(2)}) collective-permute-start(bf16[256,256]{1,0:T(8,128)(2,1)} %param.10), channel_id=1, source_target_pairs={{0,1},{1,0},{2,3},{3,2},{4,5},{5,4},{6,7},{7,6},{8,9},{9,8},{10,11... | collective-permute-start | bytes 393224 | tf_op jit(solution)/shard_map/ppermute | solution.py:21
  1.7 17.1 %all-to-all-start = ((bf16[8,1,4,8,512]{4,3,2,1,0:T(8,128)(2,1)}), bf16[8,1,4,8,512]{4,3,2,1,0:T(8,128)(2,1)S(1)}, u32[]{:S(2)}, u32[]{:S(2)}) async-start(bf16[8,1,4,8,512]{4,3,2,1,0:T(8,128)(2,1)} %bitcast.2), calls=%async_computation | async-start | bytes 524288 | tf_op jit(solution)/shard_map/all_to_all | solution.py:75
  12.1 6.7 %collective-permute-start.1 = (bf16[1,16,8,512]{3,2,1,0:T(8,128)(2,1)S(1)}, bf16[1,16,8,512]{3,2,1,0:T(8,128)(2,1)S(1)}, u32[]{:S(2)}, u32[]{:S(2)}) collective-permute-start(bf16[1,16,8,512]{3,2,1,0:T(8,128)(2,1)S(1)} %constant_dynamic-slice_fusion.2), channel_id=1, source_target_pairs={{0,2},{2,0},{1,3},{3,1},{4,6},{6,4},{5,7},{7,5},{8,10},{10,8},{9,1... | collective-permute-start | bytes 393224 | tf_op jit(solution)/shard_map/ppermute | solution.py:21
  19.0 1.7 %copy-start.3 = (bf16[3,3,512,256]{3,2,1,0:T(8,128)(2,1)S(1)}, bf16[3,3,512,256]{3,2,1,0:T(8,128)(2,1)}, u32[]{:S(2)}) copy-start(bf16[3,3,512,256]{3,2,1,0:T(8,128)(2,1)} %param.9) | copy-start | bytes 7077892
  19.0 1.7 %copy-start.4 = (pred[8,3]{0,1:T(4,128)(4,1)S(1)}, pred[8,3]{0,1:T(4,128)(4,1)}, u32[]{:S(2)}) copy-start(pred[8,3]{0,1:T(4,128)(4,1)} %constant.69) | copy-start | bytes 76
  23.4 1.8 %copy-start.1 = (bf16[3,512,256]{2,1,0:T(8,128)(2,1)S(1)}, bf16[3,512,256]{2,1,0:T(8,128)(2,1)}, u32[]{:S(2)}) copy-start(bf16[3,512,256]{2,1,0:T(8,128)(2,1)} %param.11) | copy-start | bytes 2359300
  23.4 1.6 %collective-permute-start.3 = (bf16[1,16,16,512]{3,2,1,0:T(8,128)(2,1)S(1)}, bf16[1,16,16,512]{3,2,1,0:T(8,128)(2,1)S(1)}, u32[]{:S(2)}, u32[]{:S(2)}) collective-permute-start(bf16[1,16,16,512]{3,2,1,0:T(8,128)(2,1)S(1)} %bitcast.77), channel_id=1, source_target_pairs={{0,1},{1,0},{2,3},{3,2},{4,5},{5,4},{6,7},{7,6},{8,9},{9,8},{10,11... | collective-permute-start | bytes 786440 | tf_op jit(solution)/shard_map/ppermute | solution.py:21

commit v14 on v11

--- a/solution.py
+++ b/solution.py
@@ -101,20 +101,27 @@
         jnp.concatenate([feat_own, feat_other, feat_own], axis=3), l_idx * half, 2 * half, 3
     )
     nat_part = swap(nat_own, "low")
-    features = lax.dynamic_slice_in_dim(
-        jnp.concatenate([nat_own, nat_part, nat_own], axis=0), l_idx * per_core, per_tile, 0
-    )
-    rows_total, cols_total = features.shape[1], features.shape[2]
+    rows_total, cols_total = nat_own.shape[1], nat_own.shape[2]
     tokens = rows_total * cols_total
 
     def project(part, which):
         return jnp.dot(part, attend_weight[which], preferred_element_type=jnp.float32).astype(jnp.bfloat16)
 
-    own_cols = lax.dynamic_slice_in_dim(features, c_idx * col_local, col_local, 2)
-    flat = features.reshape(per_tile, tokens, width)
-    queries = project(own_cols.reshape(per_tile, -1, width), 0)
-    keys = project(flat, 1)
-    values = project(flat, 2)
+    def project_sample(sample_features):
+        own_cols = lax.dynamic_slice_in_dim(sample_features, c_idx * col_local, col_local, 2)
+        flat = sample_features.reshape(per_core, tokens, width)
+        return (
+            project(own_cols.reshape(per_core, -1, width), 0),
+            project(flat, 1),
+            project(flat, 2),
+        )
+
+    mine, theirs = project_sample(nat_own), project_sample(nat_part)
+
+    def in_order(pair):
+        return lax.dynamic_slice_in_dim(jnp.concatenate([pair[0], pair[1], pair[0]], axis=0), l_idx * per_core, per_tile, 0)
+
+    queries, keys, values = (in_order(pair) for pair in zip(mine, theirs))
     query_count = queries.shape[1]
     if tokens * query_count * 4 * per_tile * heads_local <= (8 << 20):
         split = lambda x: x.reshape(per_tile, x.shape[1], heads_local, HEAD)

time: 28.1 us -> 28.3 us (level)
  waiting for transfers between devices: 5.39 us -> 3.89 us
  local copies, waits for them, and re-layouts: 5.66 us -> 6.42 us
  matrix products: 5.18 us -> 5.77 us
  other arithmetic: 0.77 us -> 1.11 us
    ppermute x4, waiting for transfers between devices: 1.65 us -> 0.19 us  [swap(): return lax.ppermute(tree, axis, [(0, 1), (1, 0)])]
    unnamed x11, local copies, waits for them, and re-layouts: 1.74 us -> 2.44 us
    dot_general x3 -> x6, matrix products: 0.94 us -> 1.53 us  [project(): jnp.dot(part, attend_weight[which], preferred_element_type=jnp.float32)]
    concatenate x1 -> x2, other arithmetic: 0.09 us -> 0.37 us  [in_order(): jnp.concatenate([pair[0], pair[1], pair[0]], axis=0)]
  transfers between devices with their start and end apart: 5 -> 5, of which waited for: 3 -> 2; matrix products, arithmetic and copies ran while one was open for 18% -> 21% of each run, Pallas kernels for 0% -> 0%
where the time goes in v14:
time: 28.3 us; the launch traced here: 28 us
  starting transfers between devices  9.92 us (35%)
  local copies, waits for them, and re-layouts  6.42 us (23%)
  matrix products  5.77 us (20%)
  waiting for transfers between devices  3.89 us (14%)
  other arithmetic  1.11 us (4%)
  between operations  0.89 us (3%)
    all_to_all x1, starting transfers between devices, per_device(): lax.all_to_all(outgoing.reshape((tiles * chans,) + blocks.shape[1:]), ('t...  7.25 us
    all_to_all x1, waiting for transfers between devices, per_device(): lax.all_to_all(outgoing.reshape((tiles * chans,) + blocks.shape[1:]), ('t...  3.69 us
    ppermute x4, starting transfers between devices, swap(): return lax.ppermute(tree, axis, [(0, 1), (1, 0)])  2.67 us
    unnamed x11, local copies, waits for them, and re-layouts  2.44 us
    conv_general_dilated x2, matrix products, convolve(): lax.conv_general_dilated(joined, weight, window_strides=(1, 1), padding=(...  2.25 us
    dot_general x6, matrix products, project(): jnp.dot(part, attend_weight[which], preferred_element_type=jnp.float32)  1.53 us
    dynamic_slice x1, local copies, waits for them, and re-layouts, per_device(): lax.dynamic_slice_in_dim(timestep, t_idx * per_tile + start, per_core, 0)  1.24 us
    dot_general x1, matrix products, per_device(): jnp.dot(embedded, time_weight.astype(jnp.float32), precision=lax.Precisio...  1.04 us
  transfers between devices with their start and end apart: 5, of which 2 were waited for; matrix products, arithmetic and copies ran while one was open for 21% of the time, Pallas kernels for 0%

profile of v14, /device:TPU:0, one launch (start us, length us, event | category | flops | bytes accessed | tf_op | source)
XLA Modules:
  0.0 28.0 jit_solution(512999306332968361)
XLA Ops:
  0.0 0.5 %collective-permute-start.2 = (bf16[3,3,512,256]{3,2,1,0:T(8,128)(2,1)}, bf16[3,3,512,256]{3,2,1,0:T(8,128)(2,1)S(1)}, u32[]{:S(2)}, u32[]{:S(2)}) collective-permute-start(bf16[3,3,512,256]{3,2,1,0:T(8,128)(2,1)} %param.9), channel_id=1, source_target_pairs={{0,1},{1,0},{2,3},{3,2},{4,5},{5,4},{6,7},{7,6},{8,9},{9,8},{10,11... | collective-permute-start | bytes 7077896 | tf_op jit(solution)/shard_map/ppermute | solution.py:21
  0.5 0.4 %copy-done = bf16[8,4,8,512]{3,2,1,0:T(8,128)(2,1)S(1)} copy-done((bf16[8,4,8,512]{3,2,1,0:T(8,128)(2,1)S(1)}, bf16[8,4,8,512]{3,2,1,0:T(8,128)(2,1)}, u32[]{:S(2)}) %copy-start) | copy-done | bytes 262168
  1.0 0.7 %broadcast_in_dim.7 = bf16[4,2,4,8,512]{4,3,2,1,0:T(8,128)(2,1)} broadcast(bf16[4,4,8,512]{3,2,1,0:T(8,128)(2,1)S(1)} %dynamic-slice_bitcast_fusion), dimensions={0,2,3,4} | broadcast | bytes 393216 | tf_op jit(solution)/shard_map/broadcast_in_dim | solution.py:74
  1.7 7.3 %all-to-all-start = ((bf16[8,1,4,8,512]{4,3,2,1,0:T(8,128)(2,1)}), bf16[8,1,4,8,512]{4,3,2,1,0:T(8,128)(2,1)S(1)}, u32[]{:S(2)}, u32[]{:S(2)}) async-start(bf16[8,1,4,8,512]{4,3,2,1,0:T(8,128)(2,1)} %bitcast.2), calls=%async_computation | async-start | bytes 524288 | tf_op jit(solution)/shard_map/all_to_all | solution.py:75
  8.9 1.2 %dynamic_slice.33 = s32[1]{0:T(128)} dynamic-slice(s32[8]{0:T(128)} %param.8, s32[]{:T(128)S(6)} %select_n.27), dynamic_slice_sizes={1} | dynamic-slice | bytes 12 | tf_op jit(solution)/shard_map/dynamic_slice | solution.py:62
  10.9 1.0 %fusion.54 = f32[1,256]{1,0:T(1,128)S(1)} fusion(bf16[256,256]{1,0:T(8,128)(2,1)} %param.10, f32[1,128]{1,0:T(1,128)S(1)} %fusion.45, f32[1,128]{1,0:T(1,128)S(1)} %fusion.46), kind=kOutput, calls=%fused_computation.88 | convolution fusion | flops 786688 | bytes 133120 | tf_op jit(solution)/shard_map/dot_general | solution.py:64
  12.1 0.1 fusion.53
  12.2 2.1 %collective-permute-start.1 = (bf16[1,16,8,512]{3,2,1,0:T(8,128)(2,1)S(1)}, bf16[1,16,8,512]{3,2,1,0:T(8,128)(2,1)S(1)}, u32[]{:S(2)}, u32[]{:S(2)}) collective-permute-start(bf16[1,16,8,512]{3,2,1,0:T(8,128)(2,1)S(1)} %constant_dynamic-slice_fusion.2), channel_id=1, source_target_pairs={{0,2},{2,0},{1,3},{3,1},{4,6},{6,4},{5,7},{7,5},{8,10},{10,8},{9,1... | collective-permute-start | bytes 393224 | tf_op jit(solution)/shard_map/ppermute | solution.py:21
  14.3 3.7 %all-to-all-done = bf16[8,1,4,8,512]{4,3,2,1,0:T(8,128)(2,1)S(1)} async-done(((bf16[8,1,4,8,512]{4,3,2,1,0:T(8,128)(2,1)}), bf16[8,1,4,8,512]{4,3,2,1,0:T(8,128)(2,1)S(1)}, u32[]{:S(2)}, u32[]{:S(2)}) %all-to-all-start) | async-done | bytes 262176 | tf_op jit(solution)/shard_map/all_to_all | solution.py:75
  18.1 0.2 collective-permute-done.1
  18.3 0.1 fusion.31
  18.4 0.2 copy.44
  18.6 0.2 copy.37
  18.9 1.2 %copy-done.3 = bf16[3,3,512,256]{3,2,1,0:T(8,128)(2,1)S(1)} copy-done((bf16[3,3,512,256]{3,2,1,0:T(8,128)(2,1)S(1)}, bf16[3,3,512,256]{3,2,1,0:T(8,128)(2,1)}, u32[]{:S(2)}) %copy-start.3) | copy-done | bytes 2359320
  20.1 1.1 %multiply_convert_fusion.1 = bf16[16,8,3,256]{3,1,2,0:T(8,128)(2,1)S(1)} fusion(bf16[3,3,512,256]{3,2,1,0:T(8,128)(2,1)S(1)} %copy-done.3, bf16[16,1,7,2,512]{4,2,3,0,1:T(8,128)(2,1)S(1)} %slice.18, bf16[16,1,8,3,512]{4,2,3,0,1:T(8,128)(2,1)S(1)} %copy.37, f32[256]{0:T(256)S(1)} %bitcast.104, pred[8,3]{0,1:T(4,128)(4,1)S(1)} %copy-done.4), kind=kOutput, calls=%fused_computation.41 | convolution fusion | flops 870875136 | bytes 3179544 | tf_op jit(solution)/shard_map/conv_general_dilated | solution.py:25
  21.2 1.1 %multiply_convert_fusion = bf16[16,8,3,256]{3,1,2,0:T(8,128)(2,1)S(1)} fusion(bf16[3,3,512,256]{3,2,1,0:T(8,128)(2,1)S(1)} %collective-permute-done.2, bf16[16,1,7,2,512]{4,2,3,0,1:T(8,128)(2,1)S(1)} %slice.18, bf16[16,1,8,3,512]{4,2,3,0,1:T(8,128)(2,1)S(1)} %copy.37, f32[256]{0:T(256)S(1)} %bitcast.103, pred[8,3]{0,1:T(4,128)(4,1)S(1)} %copy-done.4), kind=kOutput, calls=%fused_computation.40 | convolution fusion | flops 870875136 | bytes 3179544 | tf_op jit(solution)/shard_map/conv_general_dilated | solution.py:25
  22.6 0.2 copy.51
  22.8 0.1 constant_dynamic-slice_fusion
  22.9 0.7 %copy-done.1 = bf16[3,512,256]{2,1,0:T(8,128)(2,1)S(1)} copy-done((bf16[3,512,256]{2,1,0:T(8,128)(2,1)S(1)}, bf16[3,512,256]{2,1,0:T(8,128)(2,1)}, u32[]{:S(2)}) %copy-start.1) | copy-done | bytes 786456
  23.6 0.3 fusion.5
  23.9 0.2 fusion.9
  24.1 0.3 fusion.7
  24.4 0.3 fusion.6
  24.7 0.3 %fusion.8 = bf16[1,256,256]{1,2,0:T(8,128)(2,1)S(1)} fusion(bf16[256,512]{1,0:T(8,128)(2,1)S(1)} %bitcast.96, bf16[3,512,256]{2,1,0:T(8,128)(2,1)S(1)} %copy-done.1), kind=kOutput, calls=%fused_computation.17 | convolution fusion | flops 67174400 | bytes 655360 | tf_op jit(solution)/shard_map/dot_general | solution.py:108
  25.0 0.2 fusion.10
  25.3 0.1 copy.42
  25.4 0.3 %fusion.20 = (bf16[2,256,256]{1,2,0:T(8,128)(2,1)S(1)}, bf16[2,256,256]{1,2,0:T(8,128)(2,1)S(1)}) fusion(s32[]{:T(128)S(6)} %select_n.30, bf16[1,256,256]{1,2,0:T(8,128)(2,1)S(1)} %fusion.7, bf16[1,256,256]{1,2,0:T(8,128)(2,1)S(1)} %fusion.8, bf16[1,256,256]{1,2,0:T(8,128)(2,1)S(1)} %fusion.5, bf16[1,256,256]{1,2,0:T(8,128)(2,1)S(1)} %fusion.6), kind=kLoop, calls=%fused_computation.43 | loop fusion | flops 524288 | bytes 1048580 | tf_op jit(solution)/shard_map/concatenate | solution.py:122
  25.7 0.4 %fusion.55 = (f32[2,4,128]{2,1,0:T(4,128)S(1)}, f32[2,4,128,256]{3,2,1,0:T(8,128)S(1)}) fusion(bf16[2,128,4,64]{1,3,2,0:T(8,128)(2,1)S(1)} %bitcast.100, bf16[2,256,4,64]{1,3,2,0:T(8,128)(2,1)S(1)} %bitcast.99), kind=kOutput, calls=%fused_computation.90 | convolution fusion | flops 34077696 | bytes 1445888 | tf_op jit(solution)/shard_map/bqhd,bkhd->bhqk/dot_general | solution.py:129
  26.1 0.4 %fusion.11 = f32[2,4,128]{2,1,0:T(4,128)S(1)} fusion(f32[2,4,128,256]{3,2,1,0:T(8,128)S(1)} %get-tuple-element.14, f32[2,4,128]{2,1,0:T(4,128)S(1)} %get-tuple-element.13), kind=kLoop, calls=%fused_computation.23 | loop fusion | flops 523264 | bytes 1056768 | tf_op jit(solution)/shard_map/reduce_sum | solution.py:133
  26.5 0.4 %fusion.4 = bf16[2,128,4,64]{1,3,2,0:T(8,128)(2,1)S(1)} fusion(bf16[2,256,4,64]{1,3,2,0:T(8,128)(2,1)S(1)} %bitcast.101, f32[2,4,128,256]{3,2,1,0:T(8,128)S(1)} %get-tuple-element.14, f32[2,4,128]{2,1,0:T(4,128)S(1)} %get-tuple-element.13, f32[2,128,4]{1,2,0:T(4,128)S(1)} %bitcast.102), kind=kOutput, calls=%fused_computation.9 | convolution fusion | flops 34209792 | bytes 1449984 | tf_op jit(solution)/shard_map/bhqk,bkhd->bqhd/dot_general | solution.py:134
  26.9 0.2 copy.43
  27.1 0.9 %reshape.141 = bf16[2,16,8,256]{3,2,1,0:T(8,128)(2,1)} reshape(bf16[2,128,4,64]{3,2,1,0:T(4,128)(2,1)S(1)} %copy.43) | data formatting | bytes 262144 | tf_op jit(solution)/shard_map/reshape | solution.py:138
  (27 shorter events, 0.8 us)
Async XLA Ops:
  0.0 1.0 %copy-start = (bf16[8,4,8,512]{3,2,1,0:T(8,128)(2,1)S(1)}, bf16[8,4,8,512]{3,2,1,0:T(8,128)(2,1)}, u32[]{:S(2)}) copy-start(bf16[8,4,8,512]{3,2,1,0:T(8,128)(2,1)} %param.6) | copy-start | bytes 786436
  0.0 12.0 %copy-start.2 = (bf16[2,16,8,512]{3,2,1,0:T(8,128)(2,1)S(1)}, bf16[2,16,8,512]{3,2,1,0:T(8,128)(2,1)}, u32[]{:S(2)}) copy-start(bf16[2,16,8,512]{3,2,1,0:T(8,128)(2,1)} %param.7) | copy-start | bytes 786436
  0.0 21.2 %collective-permute-start.2 = (bf16[3,3,512,256]{3,2,1,0:T(8,128)(2,1)}, bf16[3,3,512,256]{3,2,1,0:T(8,128)(2,1)S(1)}, u32[]{:S(2)}, u32[]{:S(2)}) collective-permute-start(bf16[3,3,512,256]{3,2,1,0:T(8,128)(2,1)} %param.9), channel_id=1, source_target_pairs={{0,1},{1,0},{2,3},{3,2},{4,5},{5,4},{6,7},{7,6},{8,9},{9,8},{10,11... | collective-permute-start | bytes 7077896 | tf_op jit(solution)/shard_map/ppermute | solution.py:21
  0.5 11.6 %collective-permute-start = (bf16[256,256]{1,0:T(8,128)(2,1)}, bf16[256,256]{1,0:T(8,128)(2,1)S(1)}, u32[]{:S(2)}, u32[]{:S(2)}) collective-permute-start(bf16[256,256]{1,0:T(8,128)(2,1)} %param.10), channel_id=1, source_target_pairs={{0,1},{1,0},{2,3},{3,2},{4,5},{5,4},{6,7},{7,6},{8,9},{9,8},{10,11... | collective-permute-start | bytes 393224 | tf_op jit(solution)/shard_map/ppermute | solution.py:21
  1.7 16.3 %all-to-all-start = ((bf16[8,1,4,8,512]{4,3,2,1,0:T(8,128)(2,1)}), bf16[8,1,4,8,512]{4,3,2,1,0:T(8,128)(2,1)S(1)}, u32[]{:S(2)}, u32[]{:S(2)}) async-start(bf16[8,1,4,8,512]{4,3,2,1,0:T(8,128)(2,1)} %bitcast.2), calls=%async_computation | async-start | bytes 524288 | tf_op jit(solution)/shard_map/all_to_all | solution.py:75
  12.2 6.1 %collective-permute-start.1 = (bf16[1,16,8,512]{3,2,1,0:T(8,128)(2,1)S(1)}, bf16[1,16,8,512]{3,2,1,0:T(8,128)(2,1)S(1)}, u32[]{:S(2)}, u32[]{:S(2)}) collective-permute-start(bf16[1,16,8,512]{3,2,1,0:T(8,128)(2,1)S(1)} %constant_dynamic-slice_fusion.2), channel_id=1, source_target_pairs={{0,2},{2,0},{1,3},{3,1},{4,6},{6,4},{5,7},{7,5},{8,10},{10,8},{9,1... | collective-permute-start | bytes 393224 | tf_op jit(solution)/shard_map/ppermute | solution.py:21
  18.4 1.7 %copy-start.3 = (bf16[3,3,512,256]{3,2,1,0:T(8,128)(2,1)S(1)}, bf16[3,3,512,256]{3,2,1,0:T(8,128)(2,1)}, u32[]{:S(2)}) copy-start(bf16[3,3,512,256]{3,2,1,0:T(8,128)(2,1)} %param.9) | copy-start | bytes 7077892
  18.4 1.7 %copy-start.4 = (pred[8,3]{0,1:T(4,128)(4,1)S(1)}, pred[8,3]{0,1:T(4,128)(4,1)}, u32[]{:S(2)}) copy-start(pred[8,3]{0,1:T(4,128)(4,1)} %constant.68) | copy-start | bytes 76
  22.5 1.1 %copy-start.1 = (bf16[3,512,256]{2,1,0:T(8,128)(2,1)S(1)}, bf16[3,512,256]{2,1,0:T(8,128)(2,1)}, u32[]{:S(2)}) copy-start(bf16[3,512,256]{2,1,0:T(8,128)(2,1)} %param.11) | copy-start | bytes 2359300
  22.7 1.7 %collective-permute-start.3 = (bf16[1,16,16,512]{3,2,1,0:T(8,128)(2,1)S(1)}, bf16[1,16,16,512]{3,2,1,0:T(8,128)(2,1)S(1)}, u32[]{:S(2)}, u32[]{:S(2)}) collective-permute-start(bf16[1,16,16,512]{3,2,1,0:T(8,128)(2,1)S(1)} %bitcast.90), channel_id=1, source_target_pairs={{0,1},{1,0},{2,3},{3,2},{4,5},{5,4},{6,7},{7,6},{8,9},{9,8},{10,11... | collective-permute-start | bytes 786440 | tf_op jit(solution)/shard_map/ppermute | solution.py:21

commit v15 on v11

--- a/solution.py
+++ b/solution.py
@@ -113,8 +113,9 @@
     own_cols = lax.dynamic_slice_in_dim(features, c_idx * col_local, col_local, 2)
     flat = features.reshape(per_tile, tokens, width)
     queries = project(own_cols.reshape(per_tile, -1, width), 0)
-    keys = project(flat, 1)
-    values = project(flat, 2)
+    pair_weight = jnp.concatenate([attend_weight[1], attend_weight[2]], axis=1)
+    both = jnp.dot(flat, pair_weight, preferred_element_type=jnp.float32).astype(jnp.bfloat16)
+    keys, values = both[..., :half], both[..., half:]
     query_count = queries.shape[1]
     if tokens * query_count * 4 * per_tile * heads_local <= (8 << 20):
         split = lambda x: x.reshape(per_tile, x.shape[1], heads_local, HEAD)

time: 28.1 us -> 28.2 us (level)
  local copies, waits for them, and re-layouts: 5.66 us -> 6.69 us
  waiting for transfers between devices: 5.39 us -> 4.66 us
    ppermute x4, waiting for transfers between devices: 1.65 us -> 0.91 us  [swap(): return lax.ppermute(tree, axis, [(0, 1), (1, 0)])]
    dot_general x3 -> x1, matrix products: 0.94 us -> 0.24 us  [project(): jnp.dot(part, attend_weight[which], preferred_element_type=jnp.float32)]
    unnamed x11, local copies, waits for them, and re-layouts: 1.74 us -> 2.44 us
    dot_general x0 -> x1, matrix products: none -> 0.44 us  [per_device(): jnp.dot(flat, pair_weight, preferred_element_type=jnp.float32)]
    slice x0 -> x3, local copies, waits for them, and re-layouts: none -> 0.31 us  [per_device(): keys, values = (both[..., :half], both[..., half:])]
where the time goes in v15:
time: 28.2 us; the launch traced here: 27.9 us
  starting transfers between devices  9.92 us (35%)
  local copies, waits for them, and re-layouts  6.69 us (24%)
  matrix products  4.92 us (17%)
  waiting for transfers between devices  4.66 us (17%)
  between operations  0.9 us (3%)
  other arithmetic  0.77 us (3%)
    all_to_all x1, starting transfers between devices, per_device(): lax.all_to_all(outgoing.reshape((tiles * chans,) + blocks.shape[1:]), ('t...  7.25 us
    all_to_all x1, waiting for transfers between devices, per_device(): lax.all_to_all(outgoing.reshape((tiles * chans,) + blocks.shape[1:]), ('t...  3.75 us
    ppermute x4, starting transfers between devices, swap(): return lax.ppermute(tree, axis, [(0, 1), (1, 0)])  2.67 us
    unnamed x11, local copies, waits for them, and re-layouts  2.44 us
    conv_general_dilated x2, matrix products, convolve(): lax.conv_general_dilated(joined, weight, window_strides=(1, 1), padding=(...  2.25 us
    dynamic_slice x1, local copies, waits for them, and re-layouts, per_device(): lax.dynamic_slice_in_dim(timestep, t_idx * per_tile + start, per_core, 0)  1.24 us
    dot_general x1, matrix products, per_device(): jnp.dot(embedded, time_weight.astype(jnp.float32), precision=lax.Precisio...  1.04 us
    ppermute x4, waiting for transfers between devices, swap(): return lax.ppermute(tree, axis, [(0, 1), (1, 0)])  0.91 us
  transfers between devices with their start and end apart: 5, of which 3 were waited for; matrix products, arithmetic and copies ran while one was open for 18% of the time, Pallas kernels for 0%

profile of v15, /device:TPU:0, one launch (start us, length us, event | category | flops | bytes accessed | tf_op | source)
XLA Modules:
  0.0 27.9 jit_solution(13790063770644062605)
XLA Ops:
  0.0 0.5 %collective-permute-start.2 = (bf16[3,3,512,256]{3,2,1,0:T(8,128)(2,1)}, bf16[3,3,512,256]{3,2,1,0:T(8,128)(2,1)S(1)}, u32[]{:S(2)}, u32[]{:S(2)}) collective-permute-start(bf16[3,3,512,256]{3,2,1,0:T(8,128)(2,1)} %param.9), channel_id=1, source_target_pairs={{0,1},{1,0},{2,3},{3,2},{4,5},{5,4},{6,7},{7,6},{8,9},{9,8},{10,11... | collective-permute-start | bytes 7077896 | tf_op jit(solution)/shard_map/ppermute | solution.py:21
  0.5 0.1 collective-permute-start
  0.5 0.4 %copy-done = bf16[8,4,8,512]{3,2,1,0:T(8,128)(2,1)S(1)} copy-done((bf16[8,4,8,512]{3,2,1,0:T(8,128)(2,1)S(1)}, bf16[8,4,8,512]{3,2,1,0:T(8,128)(2,1)}, u32[]{:S(2)}) %copy-start) | copy-done | bytes 262168
  1.0 0.7 %broadcast_in_dim.7 = bf16[4,2,4,8,512]{4,3,2,1,0:T(8,128)(2,1)} broadcast(bf16[4,4,8,512]{3,2,1,0:T(8,128)(2,1)S(1)} %dynamic-slice_bitcast_fusion), dimensions={0,2,3,4} | broadcast | bytes 393216 | tf_op jit(solution)/shard_map/broadcast_in_dim | solution.py:74
  1.7 7.3 %all-to-all-start = ((bf16[8,1,4,8,512]{4,3,2,1,0:T(8,128)(2,1)}), bf16[8,1,4,8,512]{4,3,2,1,0:T(8,128)(2,1)S(1)}, u32[]{:S(2)}, u32[]{:S(2)}) async-start(bf16[8,1,4,8,512]{4,3,2,1,0:T(8,128)(2,1)} %bitcast.2), calls=%async_computation | async-start | bytes 524288 | tf_op jit(solution)/shard_map/all_to_all | solution.py:75
  8.9 1.2 %dynamic_slice.24 = s32[1]{0:T(128)} dynamic-slice(s32[8]{0:T(128)} %param.8, s32[]{:T(128)S(6)} %select_n.24), dynamic_slice_sizes={1} | dynamic-slice | bytes 12 | tf_op jit(solution)/shard_map/dynamic_slice | solution.py:62
  10.9 1.0 %fusion.33 = f32[1,256]{1,0:T(1,128)S(1)} fusion(bf16[256,256]{1,0:T(8,128)(2,1)} %param.10, f32[1,128]{1,0:T(1,128)S(1)} %get-tuple-element.17, f32[1,128]{1,0:T(1,128)S(1)} %get-tuple-element.18), kind=kOutput, calls=%fused_computation.59 | convolution fusion | flops 786688 | bytes 133120 | tf_op jit(solution)/shard_map/dot_general | solution.py:64
  12.0 0.1 fusion.32
  12.1 2.1 %collective-permute-start.1 = (bf16[1,16,8,512]{3,2,1,0:T(8,128)(2,1)S(1)}, bf16[1,16,8,512]{3,2,1,0:T(8,128)(2,1)S(1)}, u32[]{:S(2)}, u32[]{:S(2)}) collective-permute-start(bf16[1,16,8,512]{3,2,1,0:T(8,128)(2,1)S(1)} %constant_dynamic-slice_fusion.2), channel_id=1, source_target_pairs={{0,2},{2,0},{1,3},{3,1},{4,6},{6,4},{5,7},{7,5},{8,10},{10,8},{9,1... | collective-permute-start | bytes 393224 | tf_op jit(solution)/shard_map/ppermute | solution.py:21
  14.2 3.7 %all-to-all-done = bf16[8,1,4,8,512]{4,3,2,1,0:T(8,128)(2,1)S(1)} async-done(((bf16[8,1,4,8,512]{4,3,2,1,0:T(8,128)(2,1)}), bf16[8,1,4,8,512]{4,3,2,1,0:T(8,128)(2,1)S(1)}, u32[]{:S(2)}, u32[]{:S(2)}) %all-to-all-start) | async-done | bytes 262176 | tf_op jit(solution)/shard_map/all_to_all | solution.py:75
  18.1 0.1 collective-permute-done.1
  18.2 0.1 fusion.21
  18.4 0.2 copy.40
  18.6 0.2 copy.33
  18.9 1.2 %copy-done.3 = bf16[3,3,512,256]{3,2,1,0:T(8,128)(2,1)S(1)} copy-done((bf16[3,3,512,256]{3,2,1,0:T(8,128)(2,1)S(1)}, bf16[3,3,512,256]{3,2,1,0:T(8,128)(2,1)}, u32[]{:S(2)}) %copy-start.3) | copy-done | bytes 2359320
  20.0 1.1 %multiply_convert_fusion.1 = bf16[16,8,3,256]{3,1,2,0:T(8,128)(2,1)S(1)} fusion(bf16[3,3,512,256]{3,2,1,0:T(8,128)(2,1)S(1)} %copy-done.3, bf16[16,1,7,2,512]{4,2,3,0,1:T(8,128)(2,1)S(1)} %slice.23, bf16[16,1,8,3,512]{4,2,3,0,1:T(8,128)(2,1)S(1)} %copy.33, f32[256]{0:T(256)S(1)} %bitcast.79, pred[8,3]{0,1:T(4,128)(4,1)S(1)} %copy-done.4), kind=kOutput, calls=%fused_computation.29 | convolution fusion | flops 870875136 | bytes 3179544 | tf_op jit(solution)/shard_map/conv_general_dilated | solution.py:25
  21.1 1.1 %multiply_convert_fusion = bf16[16,8,3,256]{3,1,2,0:T(8,128)(2,1)S(1)} fusion(bf16[3,3,512,256]{3,2,1,0:T(8,128)(2,1)S(1)} %collective-permute-done.2, bf16[16,1,7,2,512]{4,2,3,0,1:T(8,128)(2,1)S(1)} %slice.23, bf16[16,1,8,3,512]{4,2,3,0,1:T(8,128)(2,1)S(1)} %copy.33, f32[256]{0:T(256)S(1)} %bitcast.78, pred[8,3]{0,1:T(4,128)(4,1)S(1)} %copy-done.4), kind=kOutput, calls=%fused_computation.28 | convolution fusion | flops 870875136 | bytes 3179544 | tf_op jit(solution)/shard_map/conv_general_dilated | solution.py:25
  22.3 0.1 copy.34
  22.5 0.2 copy.42
  22.8 0.7 %copy-done.1 = bf16[3,512,256]{2,1,0:T(8,128)(2,1)S(1)} copy-done((bf16[3,512,256]{2,1,0:T(8,128)(2,1)S(1)}, bf16[3,512,256]{2,1,0:T(8,128)(2,1)}, u32[]{:S(2)}) %copy-start.1) | copy-done | bytes 786456
  23.5 0.8 %collective-permute-done.3 = bf16[1,16,16,512]{3,2,1,0:T(8,128)(2,1)S(1)} collective-permute-done((bf16[1,16,16,512]{3,2,1,0:T(8,128)(2,1)S(1)}, bf16[1,16,16,512]{3,2,1,0:T(8,128)(2,1)S(1)}, u32[]{:S(2)}, u32[]{:S(2)}) %collective-permute-start.3) | collective-permute-done | bytes 262176 | tf_op jit(solution)/shard_map/ppermute | solution.py:21
  24.3 0.1 pad_maximum_fusion
  24.4 0.4 %convolution_convert_fusion = bf16[2,256,512]{2,1,0:T(8,128)(2,1)S(1)} fusion(bf16[2,256,512]{2,1,0:T(8,128)(2,1)S(1)} %bitcast.74, bf16[512,256]{1,0:T(8,128)(2,1)S(1)} %get-tuple-element.12, bf16[512,256]{1,0:T(8,128)(2,1)S(1)} %get-tuple-element.11), kind=kOutput, calls=%fused_computation.3 | convolution fusion | flops 269746176 | bytes 1572864 | tf_op jit(solution)/shard_map/dot_general | solution.py:117
  24.9 0.1 copy.38
  25.1 0.2 convolution_convert_fusion.1
  25.3 0.1 copy.37
  25.4 0.1 copy.36
  25.6 0.4 %fusion.35 = (f32[2,4,128]{2,1,0:T(4,128)S(1)}, f32[2,4,128,256]{3,2,1,0:T(8,128)S(1)}) fusion(bf16[2,128,4,64]{1,3,2,0:T(8,128)(2,1)S(1)} %bitcast.75, bf16[2,256,4,64]{1,3,2,0:T(8,128)(2,1)S(1)} %bitcast.73), kind=kOutput, calls=%fused_computation.61 | convolution fusion | flops 34077696 | bytes 1445888 | tf_op jit(solution)/shard_map/bqhd,bkhd->bhqk/dot_general | solution.py:123
  26.0 0.4 %fusion.5 = f32[2,4,128]{2,1,0:T(4,128)S(1)} fusion(f32[2,4,128,256]{3,2,1,0:T(8,128)S(1)} %get-tuple-element.16, f32[2,4,128]{2,1,0:T(4,128)S(1)} %get-tuple-element.15), kind=kLoop, calls=%fused_computation.13 | loop fusion | flops 523264 | bytes 1056768 | tf_op jit(solution)/shard_map/reduce_sum | solution.py:127
  26.4 0.4 %fusion.4 = bf16[2,128,4,64]{1,3,2,0:T(8,128)(2,1)S(1)} fusion(bf16[2,256,4,64]{1,3,2,0:T(8,128)(2,1)S(1)} %bitcast.76, f32[2,4,128,256]{3,2,1,0:T(8,128)S(1)} %get-tuple-element.16, f32[2,4,128]{2,1,0:T(4,128)S(1)} %get-tuple-element.15, f32[2,128,4]{1,2,0:T(4,128)S(1)} %bitcast.77), kind=kOutput, calls=%fused_computation.10 | convolution fusion | flops 34209792 | bytes 1449984 | tf_op jit(solution)/shard_map/bhqk,bkhd->bqhd/dot_general | solution.py:128
  26.8 0.2 copy.39
  27.0 0.9 %reshape.109 = bf16[2,16,8,256]{3,2,1,0:T(8,128)(2,1)} reshape(bf16[2,128,4,64]{3,2,1,0:T(4,128)(2,1)S(1)} %copy.39) | data formatting | bytes 262144 | tf_op jit(solution)/shard_map/reshape | solution.py:132
  (25 shorter events, 0.6 us)
Async XLA Ops:
  0.0 1.0 %copy-start = (bf16[8,4,8,512]{3,2,1,0:T(8,128)(2,1)S(1)}, bf16[8,4,8,512]{3,2,1,0:T(8,128)(2,1)}, u32[]{:S(2)}) copy-start(bf16[8,4,8,512]{3,2,1,0:T(8,128)(2,1)} %param.6) | copy-start | bytes 786436
  0.0 11.9 %copy-start.2 = (bf16[2,16,8,512]{3,2,1,0:T(8,128)(2,1)S(1)}, bf16[2,16,8,512]{3,2,1,0:T(8,128)(2,1)}, u32[]{:S(2)}) copy-start(bf16[2,16,8,512]{3,2,1,0:T(8,128)(2,1)} %param.7) | copy-start | bytes 786436
  0.0 21.1 %collective-permute-start.2 = (bf16[3,3,512,256]{3,2,1,0:T(8,128)(2,1)}, bf16[3,3,512,256]{3,2,1,0:T(8,128)(2,1)S(1)}, u32[]{:S(2)}, u32[]{:S(2)}) collective-permute-start(bf16[3,3,512,256]{3,2,1,0:T(8,128)(2,1)} %param.9), channel_id=1, source_target_pairs={{0,1},{1,0},{2,3},{3,2},{4,5},{5,4},{6,7},{7,6},{8,9},{9,8},{10,11... | collective-permute-start | bytes 7077896 | tf_op jit(solution)/shard_map/ppermute | solution.py:21
  0.5 11.5 %collective-permute-start = (bf16[256,256]{1,0:T(8,128)(2,1)}, bf16[256,256]{1,0:T(8,128)(2,1)S(1)}, u32[]{:S(2)}, u32[]{:S(2)}) collective-permute-start(bf16[256,256]{1,0:T(8,128)(2,1)} %param.10), channel_id=1, source_target_pairs={{0,1},{1,0},{2,3},{3,2},{4,5},{5,4},{6,7},{7,6},{8,9},{9,8},{10,11... | collective-permute-start | bytes 393224 | tf_op jit(solution)/shard_map/ppermute | solution.py:21
  1.7 16.3 %all-to-all-start = ((bf16[8,1,4,8,512]{4,3,2,1,0:T(8,128)(2,1)}), bf16[8,1,4,8,512]{4,3,2,1,0:T(8,128)(2,1)S(1)}, u32[]{:S(2)}, u32[]{:S(2)}) async-start(bf16[8,1,4,8,512]{4,3,2,1,0:T(8,128)(2,1)} %bitcast.2), calls=%async_computation | async-start | bytes 524288 | tf_op jit(solution)/shard_map/all_to_all | solution.py:75
  12.1 6.1 %collective-permute-start.1 = (bf16[1,16,8,512]{3,2,1,0:T(8,128)(2,1)S(1)}, bf16[1,16,8,512]{3,2,1,0:T(8,128)(2,1)S(1)}, u32[]{:S(2)}, u32[]{:S(2)}) collective-permute-start(bf16[1,16,8,512]{3,2,1,0:T(8,128)(2,1)S(1)} %constant_dynamic-slice_fusion.2), channel_id=1, source_target_pairs={{0,2},{2,0},{1,3},{3,1},{4,6},{6,4},{5,7},{7,5},{8,10},{10,8},{9,1... | collective-permute-start | bytes 393224 | tf_op jit(solution)/shard_map/ppermute | solution.py:21
  18.3 1.7 %copy-start.3 = (bf16[3,3,512,256]{3,2,1,0:T(8,128)(2,1)S(1)}, bf16[3,3,512,256]{3,2,1,0:T(8,128)(2,1)}, u32[]{:S(2)}) copy-start(bf16[3,3,512,256]{3,2,1,0:T(8,128)(2,1)} %param.9) | copy-start | bytes 7077892
  18.4 1.7 %copy-start.4 = (pred[8,3]{0,1:T(4,128)(4,1)S(1)}, pred[8,3]{0,1:T(4,128)(4,1)}, u32[]{:S(2)}) copy-start(pred[8,3]{0,1:T(4,128)(4,1)} %constant.69) | copy-start | bytes 76
  22.3 1.1 %copy-start.1 = (bf16[3,512,256]{2,1,0:T(8,128)(2,1)S(1)}, bf16[3,512,256]{2,1,0:T(8,128)(2,1)}, u32[]{:S(2)}) copy-start(bf16[3,512,256]{2,1,0:T(8,128)(2,1)} %param.11) | copy-start | bytes 2359300
  22.7 1.6 %collective-permute-start.3 = (bf16[1,16,16,512]{3,2,1,0:T(8,128)(2,1)S(1)}, bf16[1,16,16,512]{3,2,1,0:T(8,128)(2,1)S(1)}, u32[]{:S(2)}, u32[]{:S(2)}) collective-permute-start(bf16[1,16,16,512]{3,2,1,0:T(8,128)(2,1)S(1)} %bitcast.71), channel_id=1, source_target_pairs={{0,1},{1,0},{2,3},{3,2},{4,5},{5,4},{6,7},{7,6},{8,9},{9,8},{10,11... | collective-permute-start | bytes 786440 | tf_op jit(solution)/shard_map/ppermute | solution.py:21
